TPU v7x, 128 devices: a whole 4x4x4 slice. The times are simulated.
128 devices in a mesh: row: 16 (over x, z), col: 8 (over y, core).
Axes of the slice: x: 4, y: 4, z: 4, core: 2. Of those that a mesh axis runs over, the one named last changes fastest.
Arguments:
- front: float32 [16384, 16384], P('row', 'col')
- child_strips: float32 [16384, 32, 128], P(('row', 'col')), may hold values from -1.5 to 1.5
- child_owner: int32 [16384, 1], P(('row', 'col')), may hold values from 0 to 127; in each aligned block of 128 rows (0 to 127, 128 to 255, ...) at most 2 rows name the same one
- child_slot: int32 [16384], P(('row', 'col')), may hold values from 0 to 511
Outputs:
- factored: float32 [16384, 16384], P('row', 'col')
- panel: float32 [16384, 512], P('row')
Inputs may be any that keep to these rules, and one draw needn't show every extreme that they name: `child_owner`: among the rows of one device (aligned blocks of 128 rows), no owner is named more than 2 times.
All inputs are finite; a program needn't handle non-finite values.
Results may differ from a plain program's by a relative error of at most 0.00008.
Values sent between devices are 32-bit elements; how exact they have to be, the bound alone decides.
No kernel may reach another device: no remote copies, remote signals or barrier semaphores. Data moves between devices by JAX's collectives and lax.ppermute only.
A program may use at most 128 MiB of HBM per device.

v0:
```python
import jax
import jax.numpy as jnp
from jax import lax
from jax.sharding import PartitionSpec as P

PANEL = 512


def spread(value, axis, source):
    kept = jnp.where(lax.axis_index(axis) == source, value, 0).astype(value.dtype)
    return lax.psum(kept, axis)


def solve_rows(factor11, raw, first_rows):
    solved = lax.linalg.triangular_solve(
        factor11, raw, left_side=False, lower=True, transpose_a=True
    )
    headed = jnp.concatenate([factor11, solved[PANEL:]], axis=0)
    return jnp.where(first_rows, headed, solved)


def shards(front, child_strips, child_owner, child_slot):
    row_count = lax.axis_size("row")
    col_count = lax.axis_size("col")
    devices = row_count * col_count
    rows_dev, cols_dev = front.shape
    strip_r = child_strips.shape[1]
    strip_c = child_strips.shape[2]
    held = child_strips.shape[0]
    capacity = max(2, 2 * held // devices)
    strips_down = rows_dev // strip_r
    strips_across = cols_dev // strip_c
    local_count = strips_down * strips_across
    owner = child_owner[:, 0]
    positions = jnp.arange(held, dtype=jnp.int32)
    same_owner = owner[:, None] == owner[None, :]
    earlier = positions[:, None] > positions[None, :]
    rank = jnp.sum((same_owner & earlier).astype(jnp.int32), axis=1)
    target = owner * capacity + rank
    outgoing = (
        jnp.zeros((devices * capacity, strip_r, strip_c), jnp.float32).at[target].set(child_strips)
    )
    places = jnp.full((devices * capacity,), local_count, jnp.int32).at[target].set(child_slot)
    arrived, landing = (
        lax.all_to_all(
            outgoing.reshape(devices, capacity, strip_r, strip_c),
            ("row", "col"),
            split_axis=0,
            concat_axis=0,
            tiled=True,
        ),
        lax.all_to_all(
            places.reshape(devices, capacity),
            ("row", "col"),
            split_axis=0,
            concat_axis=0,
            tiled=True,
        ),
    )
    arrived = arrived.reshape(devices * capacity, strip_r, strip_c)
    landing = landing.reshape(devices * capacity)
    tiles = front.reshape(strips_down, strip_r, strips_across, strip_c)
    tiles = tiles.at[landing // strips_across, :, landing % strips_across, :].add(
        arrived, mode="drop"
    )
    assembled = tiles.reshape(rows_dev, cols_dev)
    row_id = lax.axis_index("row")
    col_id = lax.axis_index("col")
    first_rows = row_id == 0
    top_block = assembled[:PANEL, :PANEL]
    is_owner = first_rows & (col_id == 0)
    safe_block = jnp.where(
        is_owner, 0.5 * (top_block + top_block.T), jnp.eye(PANEL, dtype=jnp.float32)
    )
    factor11 = jnp.linalg.cholesky(safe_block)
    factor11 = spread(factor11, "row", 0)
    solved = solve_rows(factor11, assembled[:, :PANEL], first_rows)
    panel_here = spread(solved, "col", 0)
    ratio = row_count // col_count
    pieces = []
    for offset in range(ratio):
        pieces.append(spread(panel_here, "row", col_id * ratio + offset))
    column_panel = jnp.concatenate(pieces, axis=0)
    update = lax.dot_general(
        panel_here,
        column_panel,
        (((1,), (1,)), ((), ())),
        precision=lax.Precision.HIGHEST,
        preferred_element_type=jnp.float32,
    )
    global_rows = row_id * rows_dev + jnp.arange(rows_dev, dtype=jnp.int32)
    global_cols = col_id * cols_dev + jnp.arange(cols_dev, dtype=jnp.int32)
    trailing = (global_rows[:, None] >= PANEL) & (global_cols[None, :] >= PANEL)
    factored = assembled - jnp.where(trailing, update, 0.0)
    return (factored, panel_here)


def solution(mesh):
    in_specs = (
        P("row", "col"),
        P(("row", "col"), None, None),
        P(("row", "col"), None),
        P(("row", "col")),
    )
    out_specs = (P("row", "col"), P("row", None))
    return jax.shard_map(shards, mesh=mesh, in_specs=in_specs, out_specs=out_specs, check_vma=False)
```

profile of v0, /device:TPU:1, one launch (start us, length us, event | category | flops | bytes accessed | tf_op | source)
XLA Modules:
  0.0 598.0 jit_solution(650171405970876783)
XLA Ops:
  10.6 11.5 %all-to-all-start = ((s32[128,1,2]{2,1,0:T(1,128)}), s32[128,1,2]{2,1,0:T(1,128)S(1)}, u32[]{:S(2)}, u32[]{:S(2)}) async-start(s32[128,1,2]{2,1,0:T(1,128)} %bitcast.3), calls=%async_computation | async-start | bytes 131072 | tf_op jit(solution)/shard_map/all_to_all | solution.py:52
  22.1 2.5 broadcast_in_dim.29
  24.6 15.7 %scatter_fusion = f32[256,32,128]{2,1,0:T(8,128)} fusion(f32[256,32,128]{2,1,0:T(8,128)} %broadcast_in_dim.29, s32[128]{0:T(128)S(1)} %fusion.44, f32[128,32,128]{2,1,0:T(8,128)S(1)} %copy-done.5), kind=kCustom, calls=%fused_computation.1 | custom fusion | bytes 6291968 | tf_op jit(solution)/shard_map/scatter | solution.py:41
  40.3 10.3 %all-to-all-start.1 = ((f32[128,2,32,128]{3,2,1,0:T(8,128)}), f32[128,2,32,128]{3,2,1,0:T(8,128)}, u32[]{:S(2)}, u32[]{:S(2)}) async-start(f32[128,2,32,128]{3,2,1,0:T(8,128)} %bitcast.81), calls=%async_computation.1 | async-start | bytes 8388608 | tf_op jit(solution)/shard_map/all_to_all | solution.py:45
  50.7 5.4 copy.46
  56.1 6.8 %copy.35 = f32[32,32,16,128]{3,1,2,0:T(8,128)} copy(f32[32,32,16,128]{3,2,1,0:T(8,128)S(1)} %bitcast.80) | data formatting | bytes 16777216 | tf_op jit(solution)/shard_map/reshape | solution.py:62
  64.4 38.7 %all-to-all-done.1 = f32[128,2,32,128]{3,2,1,0:T(8,128)} async-done(((f32[128,2,32,128]{3,2,1,0:T(8,128)}), f32[128,2,32,128]{3,2,1,0:T(8,128)}, u32[]{:S(2)}, u32[]{:S(2)}) %all-to-all-start.1) | async-done | bytes 4194336 | tf_op jit(solution)/shard_map/all_to_all | solution.py:45
  103.1 37.7 %scatter_fusion.1 = f32[32,32,16,128]{3,1,2,0:T(8,128)} fusion(f32[32,32,16,128]{3,1,2,0:T(8,128)} %copy.35, s32[256]{0:T(256)S(1)} %bitcast.88, f32[256,32,128]{2,1,0:T(8,128)} %bitcast.6), kind=kCustom, calls=%fused_computation.2 | custom fusion | flops 1048576 | bytes 12584960 | tf_op jit(solution)/shard_map/scatter-add | solution.py:63
  140.8 10.9 %copy.36 = f32[32,32,16,128]{3,2,1,0:T(8,128)S(1)} copy(f32[32,32,16,128]{3,1,2,0:T(8,128)} %scatter_fusion.1) | data formatting | bytes 16777216 | tf_op jit(solution)/shard_map/scatter-add | solution.py:63
  151.8 4.7 copy.51
  156.6 3.4 copy-done.1
  160.4 1.5 fusion.21
  162.4 11.7 %cholesky.104 = f32[128,128]{1,0:T(8,128)S(1)} custom-call(f32[128,128]{1,0:T(8,128)S(1)} %cholesky.266), custom_call_target="Cholesky" | custom-call | tf_op jit(solution)/shard_map/jit(cholesky)/cholesky | solution.py:75
  174.3 9.8 %custom-call.30 = f32[1,128,128]{1,2,0:T(8,128)S(1)} custom-call(f32[1,128,128]{2,1,0:T(8,128)S(1)} %get-tuple-element.35), custom_call_target="InvertDiagBlocksLowerTriangular" | custom-call | tf_op jit(solution)/shard_map/jit(cholesky)/cholesky | solution.py:75
  184.8 11.7 %cholesky.217 = f32[128,128]{1,0:T(8,128)S(1)} custom-call(f32[128,128]{1,0:T(8,128)S(1)} %cholesky.270), custom_call_target="Cholesky" | custom-call | tf_op jit(solution)/shard_map/jit(cholesky)/cholesky | solution.py:75
  196.5 10.0 %custom-call.31 = f32[1,128,128]{1,2,0:T(8,128)S(1)} custom-call(f32[1,128,128]{2,1,0:T(8,128)S(1)} %get-tuple-element.32), custom_call_target="InvertDiagBlocksLowerTriangular" | custom-call | tf_op jit(solution)/shard_map/jit(cholesky)/cholesky | solution.py:75
  207.2 11.7 %cholesky.238 = f32[128,128]{1,0:T(8,128)S(1)} custom-call(f32[128,128]{1,0:T(8,128)S(1)} %cholesky.275), custom_call_target="Cholesky" | custom-call | tf_op jit(solution)/shard_map/jit(cholesky)/cholesky | solution.py:75
  219.5 9.8 %custom-call.32 = f32[1,128,128]{1,2,0:T(8,128)S(1)} custom-call(f32[1,128,128]{2,1,0:T(8,128)S(1)} %get-tuple-element.29), custom_call_target="InvertDiagBlocksLowerTriangular" | custom-call | tf_op jit(solution)/shard_map/jit(cholesky)/cholesky | solution.py:75
  230.0 11.9 %cholesky.255 = f32[128,128]{1,0:T(8,128)S(1)} custom-call(f32[128,128]{1,0:T(8,128)S(1)} %convolution_subtract_fusion.4), custom_call_target="Cholesky" | custom-call | tf_op jit(solution)/shard_map/jit(cholesky)/cholesky | solution.py:75
  246.8 83.1 %all-reduce.6.cloned.1.call-done = f32[512,512]{1,0:T(8,128)} async-done(((f32[512,512]{1,0:T(8,128)}), f32[512,512]{1,0:T(8,128)}) %all-reduce.6.cloned.1.call-update) | async-done | bytes 1048592 | tf_op jit(solution)/shard_map/psum | solution.py:11
  331.3 8.4 %while.1 = (s32[]{:T(128)}, f32[512,512]{1,0:T(8,128)S(1)}, s32[4,2]{0,1:T(2,128)S(1)}, f32[4,128,128]{2,1,0:T(8,128)S(1)}, s32[]{:T(128)}) while((s32[]{:T(128)}, f32[512,512]{1,0:T(8,128)S(1)}, s32[4,2]{0,1:T(2,128)S(1)}, f32[4,128,128]{2,1,0:T(8,128)S(1)}, s32[]{:T(128)}) %tuple.33), condition=%wide.while_cond, body=%wide.while_body.sunk | while | flops 2 | bytes 131189 | solution.py:15
  332.0 1.4 bitcast_dynamic-update-slice_fusion.2
  339.7 39.3 %custom-call.33 = f32[4,128,128]{1,2,0:T(8,128)S(1)} custom-call(f32[4,128,128]{2,1,0:T(8,128)S(1)} %get-tuple-element.9), custom_call_target="InvertDiagBlocksLowerTriangular" | custom-call | tf_op jit(solution)/shard_map/triangular_solve | solution.py:15
  379.0 1.7 fusion.23
  380.9 2.0 convolution_subtract_fusion.1
  383.8 2.9 convolution_subtract_fusion
  387.3 3.8 fusion.13
  393.3 1.7 fusion.6
  395.3 64.2 %all-reduce.8.cloned.1.call-done = f32[1024,512]{1,0:T(8,128)} async-done(((f32[1024,512]{1,0:T(8,128)}), f32[1024,512]{1,0:T(8,128)}) %all-reduce.8.cloned.1.call-update) | async-done | bytes 2097168 | tf_op jit(solution)/shard_map/psum | solution.py:11
  459.6 4.2 broadcast_select_fusion.1
  463.9 105.0 %all-reduce.10.cloned.1.call-done = (f32[1024,512]{1,0:T(8,128)}, f32[1024,512]{1,0:T(8,128)}) async-done(((f32[1024,512]{1,0:T(8,128)}, f32[1024,512]{1,0:T(8,128)}), (f32[1024,512]{1,0:T(8,128)}, f32[1024,512]{1,0:T(8,128)})) %all-reduce.10.cloned.1.call-update) | async-done | bytes 4194320 | tf_op jit(solution)/shard_map/psum | solution.py:11
  568.9 20.8 %select_subtract_fusion = f32[1024,2048]{1,0:T(8,128)} fusion(pred[2048]{0:T(1024)(128)(4,1)S(1)} %add_compare_fusion, pred[1024]{0:T(1024)(128)(4,1)S(1)} %add_compare_fusion.1, f32[1024,512]{1,0:T(8,128)S(1)} %copy-done.2, f32[1024,512]{1,0:T(8,128)} %get-tuple-element.20, f32[1024,512]{1,0:T(8,128)} %get-tuple-element.21, f32[128,8,16,128]{3,2,1,0:T(8,128)} %bitcast.79), kind=kOutput, calls=%fused_computation.6 | convolution fusion | flops 12892241920 | bytes 23071744 | tf_op jit(solution)/shard_map/dot_general | solution.py:84
  (74 shorter events, 24.8 us)
Async XLA Ops:
  10.6 29.7 %all-to-all-start = ((s32[128,1,2]{2,1,0:T(1,128)}), s32[128,1,2]{2,1,0:T(1,128)S(1)}, u32[]{:S(2)}, u32[]{:S(2)}) async-start(s32[128,1,2]{2,1,0:T(1,128)} %bitcast.3), calls=%async_computation | async-start | bytes 131072 | tf_op jit(solution)/shard_map/all_to_all | solution.py:52
  22.1 2.5 copy-start.5
  40.3 62.8 %all-to-all-start.1 = ((f32[128,2,32,128]{3,2,1,0:T(8,128)}), f32[128,2,32,128]{3,2,1,0:T(8,128)}, u32[]{:S(2)}, u32[]{:S(2)}) async-start(f32[128,2,32,128]{3,2,1,0:T(8,128)} %bitcast.81), calls=%async_computation.1 | async-start | bytes 8388608 | tf_op jit(solution)/shard_map/all_to_all | solution.py:45
  50.6 279.3 %all-reduce.6.cloned.1.call-start = ((), (), s32[]{:S(2)}) async-start(), calls=%async_computation.2 | async-start | bytes 2097152 | tf_op jit(solution)/shard_map/psum | solution.py:11
  151.8 4.7 copy-start
  156.5 3.4 copy-start.1
  246.7 212.8 %all-reduce.8.cloned.1.call-start = ((), (), s32[]{:S(2)}) async-start(), calls=%async_computation.3 | async-start | bytes 4194304 | tf_op jit(solution)/shard_map/psum | solution.py:11
  339.7 41.2 %copy-start.4 = (f32[512,512]{1,0:T(8,128)}, f32[512,512]{1,0:T(8,128)S(1)}, u32[]{:S(2)}) copy-start(f32[512,512]{1,0:T(8,128)S(1)} %get-tuple-element.103) | copy-start | bytes 3145732
  392.1 1.2 copy-start.3
  395.0 173.9 %all-reduce.10.cloned.1.call-start = ((), (), s32[]{:S(2)}) async-start(), calls=%async_computation.4 | async-start | bytes 8388608 | tf_op jit(solution)/shard_map/psum | solution.py:11
  463.8 105.1 %copy-start.2 = (f32[1024,512]{1,0:T(8,128)S(1)}, f32[1024,512]{1,0:T(8,128)}, u32[]{:S(2)}) copy-start(f32[1024,512]{1,0:T(8,128)} %all-reduce.8.cloned.1.call-done) | copy-start | bytes 6291460
Sparse Core Ops, SparseCore 0:
  246.9 83.0 all-reduce.5
  395.1 64.3 all-reduce.7
  464.0 104.9 all-reduce.9
where the time goes:
time: 607 us; the launch traced here: 598 us
  waiting for transfers between devices  291 us (48%)
  other arithmetic  168 us (28%)
  local copies, waits for them, and re-layouts  64.3 us (11%)
  matrix products  34.9 us (6%)
  starting transfers between devices  22.1 us (4%)
  between operations  17 us (3%)
    psum x3, waiting for transfers between devices, spread(): return lax.psum(kept, axis)  252 us
    another operation x14, other arithmetic, shards(): factor11 = jnp.linalg.cholesky(safe_block)  78.7 us
    another operation x4, other arithmetic, solve_rows(): lax.linalg.triangular_solve(factor11, raw, left_side=False, lower=True, t...  40.8 us
    all_to_all x1, waiting for transfers between devices, shards(): lax.all_to_all(outgoing.reshape(devices, capacity, strip_r, strip_c), ('r...  38.7 us
    scatter-add x1, other arithmetic, shards(): tiles.at[landing // strips_across, :, landing % strips_across, :]  37.7 us
    dot_general x1, matrix products, shards(): lax.dot_general(panel_here, column_panel, (((1,), (1,)), ((), ())), preci...  20.8 us
    unnamed x16, local copies, waits for them, and re-layouts  16.3 us
    scatter x1, local copies, waits for them, and re-layouts, shards(): jnp.zeros((devices * capacity, strip_r, strip_c), jnp.float32).at[target]  15.7 us
  transfers between devices with their start and end apart: 5, of which 4 were waited for; matrix products, arithmetic and copies ran while one was open for 5% of the time, Pallas kernels for 0%

commit v1 on v0

--- a/solution.py
+++ b/solution.py
@@ -6,17 +6,19 @@
 PANEL = 512
 
 
-def spread(value, axis, source):
-    kept = jnp.where(lax.axis_index(axis) == source, value, 0).astype(value.dtype)
-    return lax.psum(kept, axis)
-
-
-def solve_rows(factor11, raw, first_rows):
-    solved = lax.linalg.triangular_solve(
-        factor11, raw, left_side=False, lower=True, transpose_a=True
-    )
-    headed = jnp.concatenate([factor11, solved[PANEL:]], axis=0)
-    return jnp.where(first_rows, headed, solved)
+def top_block_part(child_strips, owner, child_slot, strips_across):
+    strip_r = child_strips.shape[1]
+    strip_c = child_strips.shape[2]
+    down = PANEL // strip_r
+    across = PANEL // strip_c
+    srow = child_slot // strips_across
+    scol = child_slot % strips_across
+    hit = (owner == 0) & (srow < down) & (scol < across)
+    where = jnp.where(hit, srow * across + scol, down * across)
+    part = jnp.zeros((down * across, strip_r, strip_c), jnp.float32)
+    part = part.at[where].add(child_strips, mode="drop")
+    part = part.reshape(down, across, strip_r, strip_c).transpose(0, 2, 1, 3)
+    return part.reshape(PANEL, PANEL)
 
 
 def shards(front, child_strips, child_owner, child_slot):
@@ -32,6 +34,15 @@
     strips_across = cols_dev // strip_c
     local_count = strips_down * strips_across
     owner = child_owner[:, 0]
+    row_id = lax.axis_index("row")
+    col_id = lax.axis_index("col")
+    is_owner = (row_id == 0) & (col_id == 0)
+
+    part = top_block_part(child_strips, owner, child_slot, strips_across)
+    part = part + jnp.where(is_owner, front[:PANEL, :PANEL], 0.0)
+    top_block = lax.psum(part, ("row", "col"))
+    factor11 = jnp.linalg.cholesky(0.5 * (top_block + top_block.T))
+
     positions = jnp.arange(held, dtype=jnp.int32)
     same_owner = owner[:, None] == owner[None, :]
     earlier = positions[:, None] > positions[None, :]
@@ -64,22 +75,34 @@
         arrived, mode="drop"
     )
     assembled = tiles.reshape(rows_dev, cols_dev)
-    row_id = lax.axis_index("row")
-    col_id = lax.axis_index("col")
-    first_rows = row_id == 0
-    top_block = assembled[:PANEL, :PANEL]
-    is_owner = first_rows & (col_id == 0)
-    safe_block = jnp.where(
-        is_owner, 0.5 * (top_block + top_block.T), jnp.eye(PANEL, dtype=jnp.float32)
+
+    raw = jnp.where(col_id == 0, assembled[:, :PANEL], 0.0)
+    piece = lax.psum_scatter(raw, "col", scatter_dimension=0, tiled=True)
+    piece_rows = piece.shape[0]
+    solved = lax.linalg.triangular_solve(
+        factor11, piece, left_side=False, lower=True, transpose_a=True
     )
-    factor11 = jnp.linalg.cholesky(safe_block)
-    factor11 = spread(factor11, "row", 0)
-    solved = solve_rows(factor11, assembled[:, :PANEL], first_rows)
-    panel_here = spread(solved, "col", 0)
+    first = row_id * rows_dev + col_id * piece_rows
+    head = lax.dynamic_slice_in_dim(factor11, jnp.minimum(first, PANEL - piece_rows), piece_rows, 0)
+    solved = jnp.where(first < PANEL, head, solved)
+    panel_here = lax.all_gather(solved, "col", axis=0, tiled=True)
+
     ratio = row_count // col_count
+    got = []
+    for o in range(ratio):
+        perm = []
+        for k in range(row_count):
+            c, b = divmod(k, ratio)
+            for j in range(col_count):
+                perm.append((k * col_count + j, (ratio * j + (b + o) % ratio) * col_count + c))
+        got.append(lax.ppermute(panel_here, ("row", "col"), perm))
+    t = row_id % ratio
     pieces = []
-    for offset in range(ratio):
-        pieces.append(spread(panel_here, "row", col_id * ratio + offset))
+    for b in range(ratio):
+        pick = got[0]
+        for o in range(ratio):
+            pick = jnp.where((b + o) % ratio == t, got[o], pick)
+        pieces.append(pick)
     column_panel = jnp.concatenate(pieces, axis=0)
     update = lax.dot_general(
         panel_here,

time: 607 us -> 679 us (1.12)
  the two profiles are of different devices: /device:TPU:1 before, /device:TPU:7 now
where the time goes in v1:
time: 679 us; the launch traced here: 672 us
  waiting for transfers between devices  361 us (53%)
  other arithmetic  168 us (25%)
  local copies, waits for them, and re-layouts  65.2 us (10%)
  starting transfers between devices  31 us (5%)
  matrix products  28 us (4%)
  between operations  18.9 us (3%)
    ppermute x2, waiting for transfers between devices, shards(): got.append(lax.ppermute(panel_here, ('row', 'col'), perm))  176 us
    psum x1, waiting for transfers between devices, shards(): top_block = lax.psum(part, ('row', 'col'))  158 us
    another operation x14, other arithmetic, shards(): factor11 = jnp.linalg.cholesky(0.5 * (top_block + top_block.T))  78.9 us
    another operation x3, other arithmetic, shards(): lax.linalg.triangular_solve(factor11, piece, left_side=False, lower=True,...  39.6 us
    scatter-add x1, other arithmetic, shards(): tiles.at[landing // strips_across, :, landing % strips_across, :]  35.2 us
    all_gather x1, waiting for transfers between devices, shards(): panel_here = lax.all_gather(solved, 'col', axis=0, tiled=True)  26.6 us
    dot_general x1, matrix products, shards(): lax.dot_general(panel_here, column_panel, (((1,), (1,)), ((), ())), preci...  20 us
    scatter x1, local copies, waits for them, and re-layouts, shards(): jnp.zeros((devices * capacity, strip_r, strip_c), jnp.float32).at[target]  15.7 us
  transfers between devices with their start and end apart: 7, of which 4 were waited for; matrix products, arithmetic and copies ran while one was open for 26% of the time, Pallas kernels for 0%

profile of v1, /device:TPU:7, one launch (start us, length us, event | category | flops | bytes accessed | tf_op | source)
XLA Modules:
  0.0 672.1 jit_solution(6150643088801354468)
XLA Ops:
  11.5 10.8 %all-to-all-start = ((s32[128,1,2]{2,1,0:T(1,128)}), s32[128,1,2]{2,1,0:T(1,128)S(1)}, u32[]{:S(2)}, u32[]{:S(2)}) async-start(s32[128,1,2]{2,1,0:T(1,128)} %bitcast.3), calls=%async_computation | async-start | bytes 131072 | tf_op jit(solution)/shard_map/all_to_all | solution.py:63
  22.2 2.5 broadcast_in_dim.39
  24.7 15.7 %scatter_fusion = f32[256,32,128]{2,1,0:T(8,128)} fusion(f32[256,32,128]{2,1,0:T(8,128)} %broadcast_in_dim.39, s32[128]{0:T(128)S(1)} %fusion.38, f32[128,32,128]{2,1,0:T(8,128)S(1)} %copy-done.2), kind=kCustom, calls=%fused_computation.1 | custom fusion | bytes 6291968 | tf_op jit(solution)/shard_map/scatter | solution.py:52
  40.4 10.2 %all-to-all-start.1 = ((f32[128,2,32,128]{3,2,1,0:T(8,128)}), f32[128,2,32,128]{3,2,1,0:T(8,128)}, u32[]{:S(2)}, u32[]{:S(2)}) async-start(f32[128,2,32,128]{3,2,1,0:T(8,128)} %bitcast.84), calls=%async_computation.1 | async-start | bytes 8388608 | tf_op jit(solution)/shard_map/all_to_all | solution.py:56
  50.9 6.0 scatter_fusion.2
  61.1 5.4 copy.73
  66.5 6.8 %copy.53 = f32[32,32,16,128]{3,1,2,0:T(8,128)} copy(f32[32,32,16,128]{3,2,1,0:T(8,128)S(1)} %bitcast.83) | data formatting | bytes 16777216 | tf_op jit(solution)/shard_map/reshape | solution.py:73
  74.9 157.8 %all-reduce.3.cloned.1.call-done = f32[512,512]{0,1:T(8,128)} async-done(((f32[512,512]{0,1:T(8,128)}), f32[512,512]{0,1:T(8,128)}) %all-reduce.3.cloned.1.call-update) | async-done | bytes 1048592 | tf_op jit(solution)/shard_map/psum | solution.py:43
  232.8 1.6 copy.58
  235.3 11.7 %cholesky.103 = f32[128,128]{1,0:T(8,128)S(1)} custom-call(f32[128,128]{1,0:T(8,128)S(1)} %cholesky.263), custom_call_target="Cholesky" | custom-call | tf_op jit(solution)/shard_map/jit(cholesky)/cholesky | solution.py:44
  247.0 10.2 %custom-call.30 = f32[1,128,128]{1,2,0:T(8,128)S(1)} custom-call(f32[1,128,128]{2,1,0:T(8,128)S(1)} %get-tuple-element.53), custom_call_target="InvertDiagBlocksLowerTriangular" | custom-call | tf_op jit(solution)/shard_map/jit(cholesky)/cholesky | solution.py:44
  257.5 35.2 %scatter_fusion.1 = f32[32,32,16,128]{3,1,2,0:T(8,128)} fusion(f32[32,32,16,128]{3,1,2,0:T(8,128)} %copy.53, s32[256]{0:T(256)S(1)} %bitcast.85, f32[256,32,128]{2,1,0:T(8,128)} %bitcast.6), kind=kCustom, calls=%fused_computation.2 | custom fusion | flops 1048576 | bytes 12584960 | tf_op jit(solution)/shard_map/scatter-add | solution.py:74
  292.7 10.9 %copy.54 = f32[32,32,16,128]{3,2,1,0:T(8,128)S(1)} copy(f32[32,32,16,128]{3,1,2,0:T(8,128)} %scatter_fusion.1) | data formatting | bytes 16777216 | tf_op jit(solution)/shard_map/scatter-add | solution.py:74
  303.6 4.5 copy.80
  308.1 1.6 slice_select_fusion
  310.4 11.7 %cholesky.215 = f32[128,128]{1,0:T(8,128)S(1)} custom-call(f32[128,128]{1,0:T(8,128)S(1)} %cholesky.267), custom_call_target="Cholesky" | custom-call | tf_op jit(solution)/shard_map/jit(cholesky)/cholesky | solution.py:44
  322.4 9.8 %custom-call.31 = f32[1,128,128]{1,2,0:T(8,128)S(1)} custom-call(f32[1,128,128]{2,1,0:T(8,128)S(1)} %get-tuple-element.51), custom_call_target="InvertDiagBlocksLowerTriangular" | custom-call | tf_op jit(solution)/shard_map/jit(cholesky)/cholesky | solution.py:44
  333.1 11.7 %cholesky.236 = f32[128,128]{1,0:T(8,128)S(1)} custom-call(f32[128,128]{1,0:T(8,128)S(1)} %cholesky.272), custom_call_target="Cholesky" | custom-call | tf_op jit(solution)/shard_map/jit(cholesky)/cholesky | solution.py:44
  345.0 10.0 %custom-call.32 = f32[1,128,128]{1,2,0:T(8,128)S(1)} custom-call(f32[1,128,128]{2,1,0:T(8,128)S(1)} %get-tuple-element.49), custom_call_target="InvertDiagBlocksLowerTriangular" | custom-call | tf_op jit(solution)/shard_map/jit(cholesky)/cholesky | solution.py:44
  355.8 11.7 %cholesky.253 = f32[128,128]{1,0:T(8,128)S(1)} custom-call(f32[128,128]{1,0:T(8,128)S(1)} %convolution_subtract_fusion.5), custom_call_target="Cholesky" | custom-call | tf_op jit(solution)/shard_map/jit(cholesky)/cholesky | solution.py:44
  372.4 8.4 %while.1 = (s32[]{:T(128)}, f32[512,512]{0,1:T(8,128)S(1)}, s32[4,2]{0,1:T(2,128)S(1)}, f32[4,128,128]{2,1,0:T(8,128)S(1)}, s32[]{:T(128)}) while((s32[]{:T(128)}, f32[512,512]{0,1:T(8,128)S(1)}, s32[4,2]{0,1:T(2,128)S(1)}, f32[4,128,128]{2,1,0:T(8,128)S(1)}, s32[]{:T(128)}) %tuple.37), condition=%wide.while_cond, body=%wide.while_body.sunk | while | flops 2 | bytes 393321 | solution.py:82
  373.1 1.4 dynamic-slice.7
  375.2 1.4 dynamic-slice.7
  380.8 39.3 %custom-call.33 = f32[4,128,128]{1,2,0:T(8,128)S(1)} custom-call(f32[4,128,128]{2,1,0:T(8,128)S(1)} %get-tuple-element.9), custom_call_target="InvertDiagBlocksLowerTriangular" | custom-call | tf_op jit(solution)/shard_map/triangular_solve | solution.py:82
  426.8 26.6 %all-gather.2.cloned.1.call-done = f32[1024,512]{0,1:T(8,128)} async-done(((f32[128,512]{0,1:T(8,128)}), f32[1024,512]{0,1:T(8,128)}) %all-gather.2.cloned.1.call-update) | async-done | bytes 2097168 | tf_op jit(solution)/shard_map/all_gather | solution.py:88
  453.5 4.3 collective-permute-start
  457.7 5.4 collective-permute-start.1
  463.2 2.9 copy.68
  466.1 116.9 %collective-permute-done = f32[1024,512]{0,1:T(8,128)S(1)} collective-permute-done((f32[1024,512]{0,1:T(8,128)}, f32[1024,512]{0,1:T(8,128)S(1)}, u32[]{:S(2)}, u32[]{:S(2)}) %collective-permute-start) | collective-permute-done | bytes 2097184 | tf_op jit(solution)/shard_map/ppermute | solution.py:98
  583.0 59.2 %collective-permute-done.1 = f32[1024,512]{0,1:T(8,128)} collective-permute-done((f32[1024,512]{0,1:T(8,128)}, f32[1024,512]{0,1:T(8,128)}, u32[]{:S(2)}, u32[]{:S(2)}) %collective-permute-start.1) | collective-permute-done | bytes 2097184 | tf_op jit(solution)/shard_map/ppermute | solution.py:98
  642.1 2.2 broadcast_select_fusion.1
  644.3 20.0 %select_subtract_fusion = f32[1024,2048]{1,0:T(8,128)} fusion(pred[2048]{0:T(1024)(128)(4,1)S(1)} %add_compare_fusion, pred[1024]{0:T(1024)(128)(4,1)S(1)} %add_compare_fusion.1, f32[1024,512]{0,1:T(8,128)S(1)} %copy-done.1, f32[1024,512]{0,1:T(8,128)S(1)} %get-tuple-element.47, f32[1024,512]{0,1:T(8,128)S(1)} %get-tuple-element.46, ...), kind=kOutput, calls=%fused_computation.7 | convolution fusion | flops 12892241920 | bytes 23071744 | tf_op jit(solution)/shard_map/dot_general | solution.py:107
  (98 shorter events, 27.7 us)
Async XLA Ops:
  11.5 29.0 %all-to-all-start = ((s32[128,1,2]{2,1,0:T(1,128)}), s32[128,1,2]{2,1,0:T(1,128)S(1)}, u32[]{:S(2)}, u32[]{:S(2)}) async-start(s32[128,1,2]{2,1,0:T(1,128)} %bitcast.3), calls=%async_computation | async-start | bytes 131072 | tf_op jit(solution)/shard_map/all_to_all | solution.py:63
  22.2 2.5 copy-start.2
  40.4 10.3 %copy-start.4 = (s32[128,1]{0,1:T(1,128)S(1)}, s32[128,1]{0,1:T(1,128)}, u32[]{:S(2)}) copy-start(s32[128,1]{0,1:T(1,128)} %param.6) | copy-start | bytes 1540
  40.4 10.3 %copy-start.5 = (s32[128]{0:T(128)S(1)}, s32[128]{0:T(128)}, u32[]{:S(2)}) copy-start(s32[128]{0:T(128)} %param.7) | copy-start | bytes 1540
  40.4 217.1 %all-to-all-start.1 = ((f32[128,2,32,128]{3,2,1,0:T(8,128)}), f32[128,2,32,128]{3,2,1,0:T(8,128)}, u32[]{:S(2)}, u32[]{:S(2)}) async-start(f32[128,2,32,128]{3,2,1,0:T(8,128)} %bitcast.84), calls=%async_computation.1 | async-start | bytes 8388608 | tf_op jit(solution)/shard_map/all_to_all | solution.py:56
  50.7 182.1 %all-reduce.3.cloned.1.call-start = ((), (), s32[]{:S(2)}) async-start(), calls=%async_computation.3 | async-start | bytes 2097152 | tf_op jit(solution)/shard_map/psum | solution.py:43
  60.9 359.3 %reduce-scatter.2.cloned.1.call-start = ((), (), s32[]{:S(2)}) async-start(), calls=%async_computation.4 | async-start | bytes 2359296 | tf_op jit(solution)/shard_map/reduce_scatter | solution.py:80
  232.8 1.7 copy-start.3
  303.6 4.5 copy-start
  309.7 143.7 %all-gather.2.cloned.1.call-start = ((), (), s32[]{:S(2)}) async-start(), calls=%async_computation.5 | async-start | bytes 2359296 | tf_op jit(solution)/shard_map/all_gather | solution.py:88
  453.5 129.5 %collective-permute-start = (f32[1024,512]{0,1:T(8,128)}, f32[1024,512]{0,1:T(8,128)S(1)}, u32[]{:S(2)}, u32[]{:S(2)}) collective-permute-start(f32[1024,512]{0,1:T(8,128)} %all-gather.2.cloned.1.call-done), channel_id=1, source_target_pairs={{0,8},{1,24},{2,40},{3,56},{4,72},{5,88},{6,104},{7,120},{8,0},{9,... | collective-permute-start | bytes 6291464 | tf_op jit(solution)/shard_map/ppermute | solution.py:98
  457.7 184.4 %collective-permute-start.1 = (f32[1024,512]{0,1:T(8,128)}, f32[1024,512]{0,1:T(8,128)}, u32[]{:S(2)}, u32[]{:S(2)}) collective-permute-start(f32[1024,512]{0,1:T(8,128)} %all-gather.2.cloned.1.call-done), channel_id=1, source_target_pairs={{0,0},{1,16},{2,32},{3,48},{4,64},{5,80},{6,96},{7,112},{8,8},{9,2... | collective-permute-start | bytes 6291464 | tf_op jit(solution)/shard_map/ppermute | solution.py:98
  642.1 2.2 copy-start.1
Sparse Core Ops, SparseCore 0:
  61.0 171.7 all-reduce.2
Sparse Core Ops, SparseCore 1:
  309.8 30.9 reduce-scatter.1
  426.9 26.5 all-gather.1

commit v2 on v0

--- a/solution.py
+++ b/solution.py
@@ -9,14 +9,6 @@
 def spread(value, axis, source):
     kept = jnp.where(lax.axis_index(axis) == source, value, 0).astype(value.dtype)
     return lax.psum(kept, axis)
-
-
-def solve_rows(factor11, raw, first_rows):
-    solved = lax.linalg.triangular_solve(
-        factor11, raw, left_side=False, lower=True, transpose_a=True
-    )
-    headed = jnp.concatenate([factor11, solved[PANEL:]], axis=0)
-    return jnp.where(first_rows, headed, solved)
 
 
 def shards(front, child_strips, child_owner, child_slot):
@@ -59,28 +51,57 @@
     )
     arrived = arrived.reshape(devices * capacity, strip_r, strip_c)
     landing = landing.reshape(devices * capacity)
+    row_id = lax.axis_index("row")
+    col_id = lax.axis_index("col")
+    first_rows = row_id == 0
+    is_owner = first_rows & (col_id == 0)
+
+    down = PANEL // strip_r
+    across = PANEL // strip_c
+    srow = landing // strips_across
+    scol = landing % strips_across
+    hit = (srow < down) & (scol < across)
+    spot = jnp.where(hit, srow * across + scol, down * across)
+    part = jnp.zeros((down * across, strip_r, strip_c), jnp.float32)
+    part = part.at[spot].add(arrived, mode="drop")
+    part = part.reshape(down, across, strip_r, strip_c).transpose(0, 2, 1, 3).reshape(PANEL, PANEL)
+    top_block = front[:PANEL, :PANEL] + part
+    safe_block = jnp.where(
+        is_owner, 0.5 * (top_block + top_block.T), jnp.eye(PANEL, dtype=jnp.float32)
+    )
+    factor11 = jnp.linalg.cholesky(safe_block)
+
+    pieces_l = factor11.reshape(row_count, PANEL // row_count, PANEL)
+    held_l = jnp.where(first_rows, pieces_l[0], 0.0)
+    for r in range(1, row_count):
+        got = lax.ppermute(pieces_l[r], ("row", "col"), [(0, r * col_count)])
+        held_l = held_l + got
+    factor_col0 = lax.all_gather(held_l, "row", axis=0, tiled=True)
+
     tiles = front.reshape(strips_down, strip_r, strips_across, strip_c)
     tiles = tiles.at[landing // strips_across, :, landing % strips_across, :].add(
         arrived, mode="drop"
     )
     assembled = tiles.reshape(rows_dev, cols_dev)
-    row_id = lax.axis_index("row")
-    col_id = lax.axis_index("col")
-    first_rows = row_id == 0
-    top_block = assembled[:PANEL, :PANEL]
-    is_owner = first_rows & (col_id == 0)
-    safe_block = jnp.where(
-        is_owner, 0.5 * (top_block + top_block.T), jnp.eye(PANEL, dtype=jnp.float32)
+
+    solved = lax.linalg.triangular_solve(
+        factor_col0, assembled[:, :PANEL], left_side=False, lower=True, transpose_a=True
     )
-    factor11 = jnp.linalg.cholesky(safe_block)
-    factor11 = spread(factor11, "row", 0)
-    solved = solve_rows(factor11, assembled[:, :PANEL], first_rows)
+    headed = jnp.concatenate([factor_col0, solved[PANEL:]], axis=0)
+    solved = jnp.where(first_rows, headed, solved)
     panel_here = spread(solved, "col", 0)
+
     ratio = row_count // col_count
-    pieces = []
-    for offset in range(ratio):
-        pieces.append(spread(panel_here, "row", col_id * ratio + offset))
-    column_panel = jnp.concatenate(pieces, axis=0)
+    piece_rows = rows_dev // col_count
+    mine = None
+    for j in range(col_count):
+        perm = []
+        for k in range(row_count):
+            c, b = divmod(k, ratio)
+            perm.append((k * col_count, (col_count * b + j) * col_count + c))
+        got = lax.ppermute(solved[j * piece_rows:(j + 1) * piece_rows], ("row", "col"), perm)
+        mine = got if mine is None else jnp.where(row_id % col_count == j, got, mine)
+    column_panel = lax.all_gather(mine, "row", axis=0, tiled=True)
     update = lax.dot_general(
         panel_here,
         column_panel,

time: 607 us -> 543 us (0.89)
  waiting for transfers between devices: 291 us -> 187 us
  other arithmetic: 168 us -> 189 us
  starting transfers between devices: 22.1 us -> 38.1 us
  local copies, waits for them, and re-layouts: 64.3 us -> 70.4 us
    psum x3 -> x1, waiting for transfers between devices: 252 us -> 66.1 us  [spread(): return lax.psum(kept, axis)]
    all_gather x0 -> x2, waiting for transfers between devices: none -> 55.6 us  [the longest x1 55.5 us: shards(): column_panel = lax.all_gather(mine, 'row', axis=0, tiled=True)]
    scatter-add x0 -> x1, other arithmetic: none -> 23.1 us  [shards(): part = part.at[spot].add(arrived, mode='drop')]
    ppermute x0 -> x23, starting transfers between devices: none -> 16.3 us  [the longest x15 9.97 us: shards(): got = lax.ppermute(pieces_l[r], ('row', 'col'), [(0, r * col_count)])]
    ppermute x0 -> x23, waiting for transfers between devices: none -> 15.8 us  [the longest x8 15.7 us: shards(): lax.ppermute(solved[j * piece_rows:(j + 1) * piece_rows], ('row', 'col'),...]
    all_to_all x1, waiting for transfers between devices: 38.7 us -> 49.3 us  [shards(): lax.all_to_all(outgoing.reshape(devices, capacity, strip_r, strip_c), ('r...]
    unnamed x16 -> x17, local copies, waits for them, and re-layouts: 16.3 us -> 19.7 us
  transfers between devices with their start and end apart: 5 -> 28, of which waited for: 4 -> 4; matrix products, arithmetic and copies ran while one was open for 5% -> 17% of each run, Pallas kernels for 0% -> 0%
where the time goes in v2:
time: 543 us; the launch traced here: 537 us
  other arithmetic  189 us (35%)
  waiting for transfers between devices  187 us (34%)
  local copies, waits for them, and re-layouts  70.4 us (13%)
  starting transfers between devices  38.1 us (7%)
  matrix products  35.6 us (7%)
  between operations  17.6 us (3%)
    another operation x14, other arithmetic, shards(): factor11 = jnp.linalg.cholesky(safe_block)  79 us
    psum x1, waiting for transfers between devices, spread(): return lax.psum(kept, axis)  66.1 us
    all_gather x1, waiting for transfers between devices, shards(): column_panel = lax.all_gather(mine, 'row', axis=0, tiled=True)  55.5 us
    all_to_all x1, waiting for transfers between devices, shards(): lax.all_to_all(outgoing.reshape(devices, capacity, strip_r, strip_c), ('r...  49.3 us
    another operation x4, other arithmetic, shards(): lax.linalg.triangular_solve(factor_col0, assembled[:, :PANEL], left_side=...  40.8 us
    scatter-add x1, other arithmetic, shards(): tiles.at[landing // strips_across, :, landing % strips_across, :]  37.8 us
    scatter-add x1, other arithmetic, shards(): part = part.at[spot].add(arrived, mode='drop')  23.1 us
    dot_general x1, matrix products, shards(): lax.dot_general(panel_here, column_panel, (((1,), (1,)), ((), ())), preci...  20.9 us
  transfers between devices with their start and end apart: 28, of which 4 were waited for; matrix products, arithmetic and copies ran while one was open for 17% of the time, Pallas kernels for 0%

profile of v2, /device:TPU:1, one launch (start us, length us, event | category | flops | bytes accessed | tf_op | source)
XLA Modules:
  0.0 537.0 jit_solution(4875375374677945282)
XLA Ops:
  10.6 11.5 %all-to-all-start = ((s32[128,1,2]{2,1,0:T(1,128)}), s32[128,1,2]{2,1,0:T(1,128)S(1)}, u32[]{:S(2)}, u32[]{:S(2)}) async-start(s32[128,1,2]{2,1,0:T(1,128)} %bitcast.3), calls=%async_computation | async-start | bytes 131072 | tf_op jit(solution)/shard_map/all_to_all | solution.py:44
  22.1 2.5 broadcast_in_dim.37
  24.7 15.7 %scatter_fusion = f32[256,32,128]{2,1,0:T(8,128)} fusion(f32[256,32,128]{2,1,0:T(8,128)} %broadcast_in_dim.37, s32[128]{0:T(128)S(1)} %fusion.52, f32[128,32,128]{2,1,0:T(8,128)S(1)} %copy-done.4), kind=kCustom, calls=%fused_computation.1 | custom fusion | bytes 6291968 | tf_op jit(solution)/shard_map/scatter | solution.py:33
  40.4 10.2 %all-to-all-start.1 = ((f32[128,2,32,128]{3,2,1,0:T(8,128)}), f32[128,2,32,128]{3,2,1,0:T(8,128)}, u32[]{:S(2)}, u32[]{:S(2)}) async-start(f32[128,2,32,128]{3,2,1,0:T(8,128)} %bitcast.90), calls=%async_computation.1 | async-start | bytes 8388608 | tf_op jit(solution)/shard_map/all_to_all | solution.py:37
  53.8 49.3 %all-to-all-done.1 = f32[128,2,32,128]{3,2,1,0:T(8,128)} async-done(((f32[128,2,32,128]{3,2,1,0:T(8,128)}), f32[128,2,32,128]{3,2,1,0:T(8,128)}, u32[]{:S(2)}, u32[]{:S(2)}) %all-to-all-start.1) | async-done | bytes 4194336 | tf_op jit(solution)/shard_map/all_to_all | solution.py:37
  103.3 23.1 %scatter_fusion.2 = f32[64,32,128]{2,1,0:T(8,128)S(1)} fusion(f32[64,32,128]{2,1,0:T(8,128)S(1)} %broadcast_in_dim.38, s32[256]{0:T(256)S(1)} %bitcast.99, f32[256,32,128]{2,1,0:T(8,128)} %bitcast.6), kind=kCustom, calls=%fused_computation.3 | custom fusion | flops 1048576 | bytes 12583936 | tf_op jit(solution)/shard_map/scatter-add | solution.py:66
  128.8 11.7 %cholesky.104 = f32[128,128]{1,0:T(8,128)S(1)} custom-call(f32[128,128]{1,0:T(8,128)S(1)} %cholesky.266), custom_call_target="Cholesky" | custom-call | tf_op jit(solution)/shard_map/jit(cholesky)/cholesky | solution.py:72
  140.7 9.8 %custom-call.30 = f32[1,128,128]{1,2,0:T(8,128)S(1)} custom-call(f32[1,128,128]{2,1,0:T(8,128)S(1)} %get-tuple-element.57), custom_call_target="InvertDiagBlocksLowerTriangular" | custom-call | tf_op jit(solution)/shard_map/jit(cholesky)/cholesky | solution.py:72
  151.2 11.9 %cholesky.217 = f32[128,128]{1,0:T(8,128)S(1)} custom-call(f32[128,128]{1,0:T(8,128)S(1)} %cholesky.270), custom_call_target="Cholesky" | custom-call | tf_op jit(solution)/shard_map/jit(cholesky)/cholesky | solution.py:72
  163.1 9.8 %custom-call.31 = f32[1,128,128]{1,2,0:T(8,128)S(1)} custom-call(f32[1,128,128]{2,1,0:T(8,128)S(1)} %get-tuple-element.54), custom_call_target="InvertDiagBlocksLowerTriangular" | custom-call | tf_op jit(solution)/shard_map/jit(cholesky)/cholesky | solution.py:72
  173.6 11.7 %cholesky.238 = f32[128,128]{1,0:T(8,128)S(1)} custom-call(f32[128,128]{1,0:T(8,128)S(1)} %cholesky.275), custom_call_target="Cholesky" | custom-call | tf_op jit(solution)/shard_map/jit(cholesky)/cholesky | solution.py:72
  186.0 9.8 %custom-call.32 = f32[1,128,128]{1,2,0:T(8,128)S(1)} custom-call(f32[1,128,128]{2,1,0:T(8,128)S(1)} %get-tuple-element.51), custom_call_target="InvertDiagBlocksLowerTriangular" | custom-call | tf_op jit(solution)/shard_map/jit(cholesky)/cholesky | solution.py:72
  196.4 12.1 %cholesky.255 = f32[128,128]{1,0:T(8,128)S(1)} custom-call(f32[128,128]{1,0:T(8,128)S(1)} %convolution_subtract_fusion.4), custom_call_target="Cholesky" | custom-call | tf_op jit(solution)/shard_map/jit(cholesky)/cholesky | solution.py:72
  223.8 5.4 %copy.51 = f32[128,8,16,128]{3,2,1,0:T(8,128)S(1)} copy(f32[128,8,16,128]{3,1,2,0:T(8,128)} %bitcast.96) | data formatting | bytes 16777216
  229.2 6.8 %copy.38 = f32[32,32,16,128]{3,1,2,0:T(8,128)} copy(f32[32,32,16,128]{3,2,1,0:T(8,128)S(1)} %bitcast.89) | data formatting | bytes 16777216 | tf_op jit(solution)/shard_map/reshape | solution.py:81
  236.0 37.8 %scatter_fusion.1 = f32[32,32,16,128]{3,1,2,0:T(8,128)} fusion(f32[32,32,16,128]{3,1,2,0:T(8,128)} %copy.38, s32[256]{0:T(256)S(1)} %bitcast.91, f32[256,32,128]{2,1,0:T(8,128)} %bitcast.6), kind=kCustom, calls=%fused_computation.2 | custom fusion | flops 1048576 | bytes 12584960 | tf_op jit(solution)/shard_map/scatter-add | solution.py:82
  273.9 11.0 %copy.39 = f32[32,32,16,128]{3,2,1,0:T(8,128)S(1)} copy(f32[32,32,16,128]{3,1,2,0:T(8,128)} %scatter_fusion.1) | data formatting | bytes 16777216 | tf_op jit(solution)/shard_map/scatter-add | solution.py:82
  284.9 3.2 copy-done
  288.1 7.7 %copy.58 = f32[128,8,16,128]{3,1,2,0:T(8,128)} copy(f32[128,8,16,128]{3,2,1,0:T(8,128)S(1)} %bitcast.86) | data formatting | bytes 16777216
  297.2 7.9 %while.1 = (s32[]{:T(128)}, f32[512,512]{1,0:T(8,128)S(1)}, s32[4,2]{0,1:T(2,128)S(1)}, f32[4,128,128]{2,1,0:T(8,128)S(1)}, s32[]{:T(128)}) while((s32[]{:T(128)}, f32[512,512]{1,0:T(8,128)S(1)}, s32[4,2]{0,1:T(2,128)S(1)}, f32[4,128,128]{2,1,0:T(8,128)S(1)}, s32[]{:T(128)}) %tuple.55), condition=%wide.while_cond, body=%wide.while_body.sunk | while | flops 2 | bytes 131181 | solution.py:87
  297.8 1.4 bitcast_dynamic-update-slice_fusion.2
  303.8 1.4 bitcast_dynamic-update-slice_fusion.2
  305.1 39.3 %custom-call.33 = f32[4,128,128]{1,2,0:T(8,128)S(1)} custom-call(f32[4,128,128]{2,1,0:T(8,128)S(1)} %get-tuple-element.9), custom_call_target="InvertDiagBlocksLowerTriangular" | custom-call | tf_op jit(solution)/shard_map/triangular_solve | solution.py:87
  344.5 1.7 fusion.16
  346.1 2.0 convolution_subtract_fusion.1
  348.8 2.9 convolution_subtract_fusion
  352.3 4.5 fusion.6
  359.8 3.0 broadcast_select_fusion
  369.5 15.7 %collective-permute-done.22 = f32[128,512]{1,0:T(8,128)S(1)} collective-permute-done((f32[128,512]{1,0:T(8,128)S(1)}, f32[128,512]{1,0:T(8,128)S(1)}, u32[]{:S(2)}, u32[]{:S(2)}) %collective-permute-start.22) | collective-permute-done | bytes 262176 | tf_op jit(solution)/shard_map/ppermute | solution.py:102
  386.2 66.1 %all-reduce.3.cloned.1.call-done = f32[1024,512]{1,0:T(8,128)} async-done(((f32[1024,512]{1,0:T(8,128)}), f32[1024,512]{1,0:T(8,128)}) %all-reduce.3.cloned.1.call-update) | async-done | bytes 2097168 | tf_op jit(solution)/shard_map/psum | solution.py:11
  452.3 55.5 %all-gather.5.cloned.1.call-done = f32[2048,512]{1,0:T(8,128)} async-done(((f32[128,512]{1,0:T(8,128)}), f32[2048,512]{1,0:T(8,128)}) %all-gather.5.cloned.1.call-update) | async-done | bytes 4194320 | tf_op jit(solution)/shard_map/all_gather | solution.py:104
  507.9 20.9 %select_subtract_fusion = f32[1024,2048]{1,0:T(8,128)} fusion(pred[2048]{0:T(1024)(128)(4,1)S(1)} %add_compare_fusion, pred[1024]{0:T(1024)(128)(4,1)S(1)} %add_compare_fusion.1, f32[1024,512]{1,0:T(8,128)} %all-reduce.3.cloned.1.call-done, f32[2048,512]{1,0:T(8,128)} %all-gather.5.cloned.1.call-done, f32[128,8,16,128]{3,2,1,0:T(8,128)} %bitcast.87), kind=kOutput, calls=%fused_computation.7 | convolution fusion | flops 12891193344 | bytes 23071744 | tf_op jit(solution)/shard_map/dot_general | solution.py:105
  (131 shorter events, 43.9 us)
Async XLA Ops:
  10.6 29.8 %all-to-all-start = ((s32[128,1,2]{2,1,0:T(1,128)}), s32[128,1,2]{2,1,0:T(1,128)S(1)}, u32[]{:S(2)}, u32[]{:S(2)}) async-start(s32[128,1,2]{2,1,0:T(1,128)} %bitcast.3), calls=%async_computation | async-start | bytes 131072 | tf_op jit(solution)/shard_map/all_to_all | solution.py:44
  22.1 2.6 copy-start.4
  40.4 62.7 %all-to-all-start.1 = ((f32[128,2,32,128]{3,2,1,0:T(8,128)}), f32[128,2,32,128]{3,2,1,0:T(8,128)}, u32[]{:S(2)}, u32[]{:S(2)}) async-start(f32[128,2,32,128]{3,2,1,0:T(8,128)} %bitcast.90), calls=%async_computation.1 | async-start | bytes 8388608 | tf_op jit(solution)/shard_map/all_to_all | solution.py:37
  50.6 245.2 %all-gather.3.cloned.1.call-start = ((), (), s32[]{:S(2)}) async-start(), calls=%async_computation.2 | async-start | bytes 1114112 | tf_op jit(solution)/shard_map/all_gather | solution.py:79
  212.7 3.4 collective-permute-start
  213.4 3.4 collective-permute-start.1
  214.1 3.4 collective-permute-start.10
  214.7 3.4 collective-permute-start.11
  215.4 3.4 collective-permute-start.12
  216.1 3.4 collective-permute-start.13
  216.8 3.4 collective-permute-start.14
  217.5 3.4 collective-permute-start.2
  218.1 3.4 collective-permute-start.3
  218.8 3.4 collective-permute-start.4
  219.5 3.4 collective-permute-start.5
  220.2 2.7 collective-permute-start.6
  220.9 2.1 collective-permute-start.7
  221.6 1.4 collective-permute-start.8
  222.2 0.7 collective-permute-start.9
  223.7 228.6 %all-reduce.3.cloned.1.call-start = ((), (), s32[]{:S(2)}) async-start(), calls=%async_computation.3 | async-start | bytes 4194304 | tf_op jit(solution)/shard_map/psum | solution.py:11
  284.9 3.2 copy-start
  358.6 1.2 copy-start.3
  362.8 145.0 %all-gather.5.cloned.1.call-start = ((), (), s32[]{:S(2)}) async-start(), calls=%async_computation.4 | async-start | bytes 4456448 | tf_op jit(solution)/shard_map/all_gather | solution.py:104
  363.1 3.7 collective-permute-start.15
  363.8 3.7 collective-permute-start.16
  364.5 3.7 collective-permute-start.17
  365.1 4.3 collective-permute-start.18
  365.8 3.7 collective-permute-start.19
  366.8 2.7 collective-permute-start.20
  367.5 2.1 collective-permute-start.21
  368.2 17.1 %collective-permute-start.22 = (f32[128,512]{1,0:T(8,128)S(1)}, f32[128,512]{1,0:T(8,128)S(1)}, u32[]{:S(2)}, u32[]{:S(2)}) collective-permute-start(f32[128,512]{1,0:T(8,128)S(1)} %get-tuple-element.25), channel_id=1, source_target_pairs={{0,0},{8,64},{16,1},{24,65},{32,2},{40,66},{48,3},{56,67},{64,4},{... | collective-permute-start | bytes 786440 | tf_op jit(solution)/shard_map/ppermute | solution.py:102
  452.3 76.4 %copy-start.1 = (f32[1024,512]{1,0:T(8,128)S(1)}, f32[1024,512]{1,0:T(8,128)}, u32[]{:S(2)}) copy-start(f32[1024,512]{1,0:T(8,128)} %all-reduce.3.cloned.1.call-done) | copy-start | bytes 6291460
  (2 other events, 1.8 us)
Sparse Core Ops, SparseCore 0:
  223.8 53.3 all-gather.2
  363.0 89.2 all-reduce.2
  455.0 52.7 all-gather.4

commit v3 on v2

--- a/solution.py
+++ b/solution.py
@@ -4,11 +4,6 @@
 from jax.sharding import PartitionSpec as P
 
 PANEL = 512
-
-
-def spread(value, axis, source):
-    kept = jnp.where(lax.axis_index(axis) == source, value, 0).astype(value.dtype)
-    return lax.psum(kept, axis)
 
 
 def shards(front, child_strips, child_owner, child_slot):
@@ -62,8 +57,14 @@
     scol = landing % strips_across
     hit = (srow < down) & (scol < across)
     spot = jnp.where(hit, srow * across + scol, down * across)
-    part = jnp.zeros((down * across, strip_r, strip_c), jnp.float32)
-    part = part.at[spot].add(arrived, mode="drop")
+    pick = (spot[None, :] == jnp.arange(down * across, dtype=jnp.int32)[:, None]).astype(jnp.float32)
+    part = lax.dot_general(
+        pick,
+        arrived.reshape(arrived.shape[0], strip_r * strip_c),
+        (((1,), (0,)), ((), ())),
+        precision=lax.Precision.HIGHEST,
+        preferred_element_type=jnp.float32,
+    )
     part = part.reshape(down, across, strip_r, strip_c).transpose(0, 2, 1, 3).reshape(PANEL, PANEL)
     top_block = front[:PANEL, :PANEL] + part
     safe_block = jnp.where(
@@ -89,19 +90,22 @@
     )
     headed = jnp.concatenate([factor_col0, solved[PANEL:]], axis=0)
     solved = jnp.where(first_rows, headed, solved)
-    panel_here = spread(solved, "col", 0)
+    piece_rows = rows_dev // col_count
+    my_piece = solved[:piece_rows]
+    for j in range(1, col_count):
+        perm = [(k * col_count, k * col_count + j) for k in range(row_count)]
+        got = lax.ppermute(solved[j * piece_rows:(j + 1) * piece_rows], ("row", "col"), perm)
+        my_piece = jnp.where(col_id == j, got, my_piece)
 
     ratio = row_count // col_count
-    piece_rows = rows_dev // col_count
-    mine = None
-    for j in range(col_count):
-        perm = []
-        for k in range(row_count):
-            c, b = divmod(k, ratio)
-            perm.append((k * col_count, (col_count * b + j) * col_count + c))
-        got = lax.ppermute(solved[j * piece_rows:(j + 1) * piece_rows], ("row", "col"), perm)
-        mine = got if mine is None else jnp.where(row_id % col_count == j, got, mine)
+    perm = []
+    for k in range(row_count):
+        c, b = divmod(k, ratio)
+        for j in range(col_count):
+            perm.append((k * col_count + j, (col_count * b + j) * col_count + c))
+    mine = lax.ppermute(my_piece, ("row", "col"), perm)
     column_panel = lax.all_gather(mine, "row", axis=0, tiled=True)
+    panel_here = lax.all_gather(my_piece, "col", axis=0, tiled=True)
     update = lax.dot_general(
         panel_here,
         column_panel,

time: 543 us -> 508 us (0.936)
  waiting for transfers between devices: 187 us -> 149 us
  other arithmetic: 189 us -> 165 us
  local copies, waits for them, and re-layouts: 70.4 us -> 86 us
    psum x1 -> x0, waiting for transfers between devices: 66.1 us -> none  [spread(): return lax.psum(kept, axis)]
    scatter-add x1 -> x0, other arithmetic: 23.1 us -> none  [shards(): part = part.at[spot].add(arrived, mode='drop')]
    all_gather x0 -> x1, waiting for transfers between devices: none -> 17.6 us  [shards(): panel_here = lax.all_gather(my_piece, 'col', axis=0, tiled=True)]
    unnamed x17 -> x24, local copies, waits for them, and re-layouts: 19.7 us -> 29.1 us
    ppermute x0 -> x1, waiting for transfers between devices: none -> 8.25 us  [shards(): mine = lax.ppermute(my_piece, ('row', 'col'), perm)]
    dot_general x0 -> x1, local copies, waits for them, and re-layouts: none -> 5.81 us  [shards(): lax.dot_general(pick, arrived.reshape(arrived.shape[0], strip_r * strip_c...]
    ppermute x8 -> x7, waiting for transfers between devices: 15.7 us -> 18.5 us  [shards(): lax.ppermute(solved[j * piece_rows:(j + 1) * piece_rows], ('row', 'col'),...]
  transfers between devices with their start and end apart: 28 -> 28, of which waited for: 4 -> 5; matrix products, arithmetic and copies ran while one was open for 17% -> 18% of each run, Pallas kernels for 0% -> 0%
where the time goes in v3:
time: 508 us; the launch traced here: 500 us
  other arithmetic  165 us (32%)
  waiting for transfers between devices  149 us (29%)
  local copies, waits for them, and re-layouts  86 us (17%)
  starting transfers between devices  42.1 us (8%)
  matrix products  40.1 us (8%)
  between operations  17.5 us (3%)
    another operation x14, other arithmetic, shards(): factor11 = jnp.linalg.cholesky(safe_block)  79 us
    all_gather x1, waiting for transfers between devices, shards(): column_panel = lax.all_gather(mine, 'row', axis=0, tiled=True)  54.4 us
    all_to_all x1, waiting for transfers between devices, shards(): lax.all_to_all(outgoing.reshape(devices, capacity, strip_r, strip_c), ('r...  50.6 us
    another operation x4, other arithmetic, shards(): lax.linalg.triangular_solve(factor_col0, assembled[:, :PANEL], left_side=...  40.9 us
    scatter-add x1, other arithmetic, shards(): tiles.at[landing // strips_across, :, landing % strips_across, :]  37.8 us
    unnamed x24, local copies, waits for them, and re-layouts  29.1 us
    dot_general x1, matrix products, shards(): lax.dot_general(panel_here, column_panel, (((1,), (1,)), ((), ())), preci...  20.9 us
    ppermute x7, waiting for transfers between devices, shards(): lax.ppermute(solved[j * piece_rows:(j + 1) * piece_rows], ('row', 'col'),...  18.5 us
  transfers between devices with their start and end apart: 28, of which 5 were waited for; matrix products, arithmetic and copies ran while one was open for 18% of the time, Pallas kernels for 0%

profile of v3, /device:TPU:1, one launch (start us, length us, event | category | flops | bytes accessed | tf_op | source)
XLA Modules:
  0.0 500.1 jit_solution(15232145415280311080)
XLA Ops:
  10.6 11.5 %all-to-all-start = ((s32[128,1,2]{2,1,0:T(1,128)}), s32[128,1,2]{2,1,0:T(1,128)S(1)}, u32[]{:S(2)}, u32[]{:S(2)}) async-start(s32[128,1,2]{2,1,0:T(1,128)} %bitcast.3), calls=%async_computation | async-start | bytes 131072 | tf_op jit(solution)/shard_map/all_to_all | solution.py:39
  22.1 2.5 broadcast_in_dim.18
  24.7 15.7 %scatter_fusion = f32[256,32,128]{2,1,0:T(8,128)} fusion(f32[256,32,128]{2,1,0:T(8,128)} %broadcast_in_dim.18, s32[128]{0:T(128)S(1)} %fusion.62, f32[128,32,128]{2,1,0:T(8,128)S(1)} %copy-done.4), kind=kCustom, calls=%fused_computation.1 | custom fusion | bytes 6291968 | tf_op jit(solution)/shard_map/scatter | solution.py:28
  40.4 10.2 %all-to-all-start.1 = ((f32[128,2,32,128]{3,2,1,0:T(8,128)}), f32[128,2,32,128]{3,2,1,0:T(8,128)}, u32[]{:S(2)}, u32[]{:S(2)}) async-start(f32[128,2,32,128]{3,2,1,0:T(8,128)} %bitcast.105), calls=%async_computation.1 | async-start | bytes 8388608 | tf_op jit(solution)/shard_map/all_to_all | solution.py:32
  52.5 50.6 %all-to-all-done.1 = f32[128,2,32,128]{3,2,1,0:T(8,128)} async-done(((f32[128,2,32,128]{3,2,1,0:T(8,128)}), f32[128,2,32,128]{3,2,1,0:T(8,128)}, u32[]{:S(2)}, u32[]{:S(2)}) %all-to-all-start.1) | async-done | bytes 4194336 | tf_op jit(solution)/shard_map/all_to_all | solution.py:32
  103.1 8.0 %copy.67 = f32[32,8,32,128]{3,1,2,0:T(8,128)} copy(f32[32,8,32,128]{3,2,1,0:T(8,128)} %bitcast.38) | data formatting | bytes 8388608
  111.1 5.8 %copy.45 = f32[4096,256]{1,0:T(8,128)} copy(f32[4096,256]{0,1:T(8,128)} %bitcast.108) | data formatting | bytes 8388608 | tf_op jit(solution)/shard_map/dot_general | solution.py:61
  116.9 4.5 convolution_bitcast_fusion
  123.9 11.7 %cholesky.104 = f32[128,128]{1,0:T(8,128)S(1)} custom-call(f32[128,128]{1,0:T(8,128)S(1)} %cholesky.266), custom_call_target="Cholesky" | custom-call | tf_op jit(solution)/shard_map/jit(cholesky)/cholesky | solution.py:73
  135.8 9.8 %custom-call.30 = f32[1,128,128]{1,2,0:T(8,128)S(1)} custom-call(f32[1,128,128]{2,1,0:T(8,128)S(1)} %get-tuple-element.51), custom_call_target="InvertDiagBlocksLowerTriangular" | custom-call | tf_op jit(solution)/shard_map/jit(cholesky)/cholesky | solution.py:73
  146.3 11.9 %cholesky.217 = f32[128,128]{1,0:T(8,128)S(1)} custom-call(f32[128,128]{1,0:T(8,128)S(1)} %cholesky.270), custom_call_target="Cholesky" | custom-call | tf_op jit(solution)/shard_map/jit(cholesky)/cholesky | solution.py:73
  158.2 9.8 %custom-call.31 = f32[1,128,128]{1,2,0:T(8,128)S(1)} custom-call(f32[1,128,128]{2,1,0:T(8,128)S(1)} %get-tuple-element.48), custom_call_target="InvertDiagBlocksLowerTriangular" | custom-call | tf_op jit(solution)/shard_map/jit(cholesky)/cholesky | solution.py:73
  168.7 11.7 %cholesky.238 = f32[128,128]{1,0:T(8,128)S(1)} custom-call(f32[128,128]{1,0:T(8,128)S(1)} %cholesky.275), custom_call_target="Cholesky" | custom-call | tf_op jit(solution)/shard_map/jit(cholesky)/cholesky | solution.py:73
  181.1 9.8 %custom-call.32 = f32[1,128,128]{1,2,0:T(8,128)S(1)} custom-call(f32[1,128,128]{2,1,0:T(8,128)S(1)} %get-tuple-element.45), custom_call_target="InvertDiagBlocksLowerTriangular" | custom-call | tf_op jit(solution)/shard_map/jit(cholesky)/cholesky | solution.py:73
  191.5 12.1 %cholesky.255 = f32[128,128]{1,0:T(8,128)S(1)} custom-call(f32[128,128]{1,0:T(8,128)S(1)} %convolution_subtract_fusion.4), custom_call_target="Cholesky" | custom-call | tf_op jit(solution)/shard_map/jit(cholesky)/cholesky | solution.py:73
  218.8 5.4 %copy.57 = f32[128,8,16,128]{3,2,1,0:T(8,128)S(1)} copy(f32[128,8,16,128]{3,1,2,0:T(8,128)} %bitcast.113) | data formatting | bytes 16777216
  224.2 6.8 %copy.42 = f32[32,32,16,128]{3,1,2,0:T(8,128)} copy(f32[32,32,16,128]{3,2,1,0:T(8,128)S(1)} %bitcast.104) | data formatting | bytes 16777216 | tf_op jit(solution)/shard_map/reshape | solution.py:82
  232.5 37.8 %scatter_fusion.1 = f32[32,32,16,128]{3,1,2,0:T(8,128)} fusion(f32[32,32,16,128]{3,1,2,0:T(8,128)} %copy.42, s32[256]{0:T(256)S(1)} %bitcast.106, f32[256,32,128]{2,1,0:T(8,128)} %bitcast.6), kind=kCustom, calls=%fused_computation.2 | custom fusion | flops 1048576 | bytes 12584960 | tf_op jit(solution)/shard_map/scatter-add | solution.py:83
  270.4 10.9 %copy.43 = f32[32,32,16,128]{3,2,1,0:T(8,128)S(1)} copy(f32[32,32,16,128]{3,1,2,0:T(8,128)} %scatter_fusion.1) | data formatting | bytes 16777216 | tf_op jit(solution)/shard_map/scatter-add | solution.py:83
  281.3 3.2 copy-done
  284.6 7.7 %copy.66 = f32[128,8,16,128]{3,1,2,0:T(8,128)} copy(f32[128,8,16,128]{3,2,1,0:T(8,128)S(1)} %bitcast.102) | data formatting | bytes 16777216
  293.6 8.5 %while.1 = (s32[]{:T(128)}, f32[512,512]{1,0:T(8,128)S(1)}, s32[4,2]{0,1:T(2,128)S(1)}, f32[4,128,128]{2,1,0:T(8,128)S(1)}, s32[]{:T(128)}) while((s32[]{:T(128)}, f32[512,512]{1,0:T(8,128)S(1)}, s32[4,2]{0,1:T(2,128)S(1)}, f32[4,128,128]{2,1,0:T(8,128)S(1)}, s32[]{:T(128)}) %tuple.51), condition=%wide.while_cond, body=%wide.while_body.sunk | while | flops 2 | bytes 131181 | solution.py:88
  302.1 39.3 %custom-call.33 = f32[4,128,128]{1,2,0:T(8,128)S(1)} custom-call(f32[4,128,128]{2,1,0:T(8,128)S(1)} %get-tuple-element.9), custom_call_target="InvertDiagBlocksLowerTriangular" | custom-call | tf_op jit(solution)/shard_map/triangular_solve | solution.py:88
  343.1 2.0 convolution_subtract_fusion.1
  345.8 2.9 convolution_subtract_fusion
  349.3 4.5 fusion.6
  367.6 18.5 %collective-permute-done.21 = f32[128,512]{1,0:T(8,128)} collective-permute-done((f32[128,512]{1,0:T(8,128)S(1)}, f32[128,512]{1,0:T(8,128)}, u32[]{:S(2)}, u32[]{:S(2)}) %collective-permute-start.21) | collective-permute-done | bytes 262176 | tf_op jit(solution)/shard_map/ppermute | solution.py:97
  388.1 1.9 collective-permute-start.22
  390.0 8.3 %collective-permute-done.22 = f32[128,512]{1,0:T(8,128)S(1)} collective-permute-done((f32[128,512]{1,0:T(8,128)}, f32[128,512]{1,0:T(8,128)S(1)}, u32[]{:S(2)}, u32[]{:S(2)}) %collective-permute-start.22) | collective-permute-done | bytes 262176 | tf_op jit(solution)/shard_map/ppermute | solution.py:106
  399.0 17.6 %all-gather.6.cloned.1.call-done = f32[1024,512]{1,0:T(8,128)} async-done(((f32[128,512]{1,0:T(8,128)}), f32[1024,512]{1,0:T(8,128)}) %all-gather.6.cloned.1.call-update) | async-done | bytes 2097168 | tf_op jit(solution)/shard_map/all_gather | solution.py:108
  416.6 54.4 %all-gather.8.cloned.1.call-done = f32[2048,512]{1,0:T(8,128)} async-done(((f32[128,512]{1,0:T(8,128)}), f32[2048,512]{1,0:T(8,128)}) %all-gather.8.cloned.1.call-update) | async-done | bytes 4194320 | tf_op jit(solution)/shard_map/all_gather | solution.py:107
  471.0 20.9 %select_subtract_fusion = f32[1024,2048]{1,0:T(8,128)} fusion(pred[2048]{0:T(1024)(128)(4,1)S(1)} %add_compare_fusion, pred[1024]{0:T(1024)(128)(4,1)S(1)} %add_compare_fusion.1, f32[1024,512]{1,0:T(8,128)} %all-gather.6.cloned.1.call-done, f32[2048,512]{1,0:T(8,128)} %all-gather.8.cloned.1.call-done, f32[128,8,16,128]{3,2,1,0:T(8,128)} %bitcast.103), kind=kOutput, calls=%fused_computation.6 | convolution fusion | flops 12891193344 | bytes 23071744 | tf_op jit(solution)/shard_map/dot_general | solution.py:109
  (140 shorter events, 54.6 us)
Async XLA Ops:
  10.6 29.8 %all-to-all-start = ((s32[128,1,2]{2,1,0:T(1,128)}), s32[128,1,2]{2,1,0:T(1,128)S(1)}, u32[]{:S(2)}, u32[]{:S(2)}) async-start(s32[128,1,2]{2,1,0:T(1,128)} %bitcast.3), calls=%async_computation | async-start | bytes 131072 | tf_op jit(solution)/shard_map/all_to_all | solution.py:39
  22.1 2.6 copy-start.4
  40.4 62.7 %all-to-all-start.1 = ((f32[128,2,32,128]{3,2,1,0:T(8,128)}), f32[128,2,32,128]{3,2,1,0:T(8,128)}, u32[]{:S(2)}, u32[]{:S(2)}) async-start(f32[128,2,32,128]{3,2,1,0:T(8,128)} %bitcast.105), calls=%async_computation.1 | async-start | bytes 8388608 | tf_op jit(solution)/shard_map/all_to_all | solution.py:32
  50.6 241.6 %all-gather.4.cloned.1.call-start = ((), (), s32[]{:S(2)}) async-start(), calls=%async_computation.2 | async-start | bytes 1114112 | tf_op jit(solution)/shard_map/all_gather | solution.py:80
  207.8 3.4 collective-permute-start
  208.4 3.4 collective-permute-start.1
  209.1 3.4 collective-permute-start.10
  209.8 3.4 collective-permute-start.11
  210.4 3.4 collective-permute-start.12
  211.1 3.4 collective-permute-start.13
  211.8 3.4 collective-permute-start.14
  212.5 3.4 collective-permute-start.2
  213.2 3.4 collective-permute-start.3
  213.9 3.4 collective-permute-start.4
  214.5 3.4 collective-permute-start.5
  215.2 2.7 collective-permute-start.6
  215.9 2.1 collective-permute-start.7
  216.6 1.4 collective-permute-start.8
  217.3 0.7 collective-permute-start.9
  218.7 197.9 %all-gather.6.cloned.1.call-start = ((), (), s32[]{:S(2)}) async-start(), calls=%async_computation.3 | async-start | bytes 2359296 | tf_op jit(solution)/shard_map/all_gather | solution.py:108
  281.3 3.2 copy-start
  358.4 5.5 %collective-permute-start.15 = (f32[128,512]{1,0:T(8,128)S(1)}, f32[128,512]{1,0:T(8,128)S(1)}, u32[]{:S(2)}, u32[]{:S(2)}) collective-permute-start(f32[128,512]{1,0:T(8,128)S(1)} %get-tuple-element.26), channel_id=1, source_target_pairs={{0,7},{8,15},{16,23},{24,31},{32,39},{40,47},{48,55},{56,63},{64,7... | collective-permute-start | bytes 786440 | tf_op jit(solution)/shard_map/ppermute | solution.py:97
  359.1 6.2 %collective-permute-start.16 = (f32[128,512]{1,0:T(8,128)S(1)}, f32[128,512]{1,0:T(8,128)S(1)}, u32[]{:S(2)}, u32[]{:S(2)}) collective-permute-start(f32[128,512]{1,0:T(8,128)S(1)} %get-tuple-element.25), channel_id=1, source_target_pairs={{0,6},{8,14},{16,22},{24,30},{32,38},{40,46},{48,54},{56,62},{64,7... | collective-permute-start | bytes 786440 | tf_op jit(solution)/shard_map/ppermute | solution.py:97
  359.8 7.8 %collective-permute-start.17 = (f32[128,512]{1,0:T(8,128)S(1)}, f32[128,512]{1,0:T(8,128)}, u32[]{:S(2)}, u32[]{:S(2)}) collective-permute-start(f32[128,512]{1,0:T(8,128)S(1)} %get-tuple-element.24), channel_id=1, source_target_pairs={{0,5},{8,13},{16,21},{24,29},{32,37},{40,45},{48,53},{56,61},{64,6... | collective-permute-start | bytes 786440 | tf_op jit(solution)/shard_map/ppermute | solution.py:97
  361.2 6.4 %collective-permute-start.18 = (f32[128,512]{1,0:T(8,128)S(1)}, f32[128,512]{1,0:T(8,128)}, u32[]{:S(2)}, u32[]{:S(2)}) collective-permute-start(f32[128,512]{1,0:T(8,128)S(1)} %get-tuple-element.23), channel_id=1, source_target_pairs={{0,4},{8,12},{16,20},{24,28},{32,36},{40,44},{48,52},{56,60},{64,6... | collective-permute-start | bytes 786440 | tf_op jit(solution)/shard_map/ppermute | solution.py:97
  362.6 5.0 %collective-permute-start.19 = (f32[128,512]{1,0:T(8,128)S(1)}, f32[128,512]{1,0:T(8,128)}, u32[]{:S(2)}, u32[]{:S(2)}) collective-permute-start(f32[128,512]{1,0:T(8,128)S(1)} %get-tuple-element.22), channel_id=1, source_target_pairs={{0,3},{8,11},{16,19},{24,27},{32,35},{40,43},{48,51},{56,59},{64,6... | collective-permute-start | bytes 786440 | tf_op jit(solution)/shard_map/ppermute | solution.py:97
  363.9 1.4 copy-start.7
  363.9 3.7 collective-permute-start.20
  366.0 20.1 %collective-permute-start.21 = (f32[128,512]{1,0:T(8,128)S(1)}, f32[128,512]{1,0:T(8,128)}, u32[]{:S(2)}, u32[]{:S(2)}) collective-permute-start(f32[128,512]{1,0:T(8,128)S(1)} %get-tuple-element.20), channel_id=1, source_target_pairs={{0,1},{8,9},{16,17},{24,25},{32,33},{40,41},{48,49},{56,57},{64,65... | collective-permute-start | bytes 786440 | tf_op jit(solution)/shard_map/ppermute | solution.py:97
  388.0 83.0 %all-gather.8.cloned.1.call-start = ((), (), s32[]{:S(2)}) async-start(), calls=%async_computation.4 | async-start | bytes 4456448 | tf_op jit(solution)/shard_map/all_gather | solution.py:107
  388.1 10.2 %collective-permute-start.22 = (f32[128,512]{1,0:T(8,128)}, f32[128,512]{1,0:T(8,128)S(1)}, u32[]{:S(2)}, u32[]{:S(2)}) collective-permute-start(f32[128,512]{1,0:T(8,128)} %fusion.23), channel_id=1, source_target_pairs={{0,0},{1,8},{2,16},{3,24},{4,32},{5,40},{6,48},{7,56},{8,64},{9,72... | collective-permute-start | bytes 786440 | tf_op jit(solution)/shard_map/ppermute | solution.py:106
  416.6 75.3 %copy-start.1 = (f32[1024,512]{1,0:T(8,128)S(1)}, f32[1024,512]{1,0:T(8,128)}, u32[]{:S(2)}) copy-start(f32[1024,512]{1,0:T(8,128)} %all-gather.6.cloned.1.call-done) | copy-start | bytes 6291460
  (5 other events, 4.5 us)
Sparse Core Ops, SparseCore 0:
  218.9 53.3 all-gather.3
  388.1 28.4 all-gather.5
  419.3 51.6 all-gather.7

commit v4 on v3

--- a/solution.py
+++ b/solution.py
@@ -24,8 +24,13 @@
     earlier = positions[:, None] > positions[None, :]
     rank = jnp.sum((same_owner & earlier).astype(jnp.int32), axis=1)
     target = owner * capacity + rank
-    outgoing = (
-        jnp.zeros((devices * capacity, strip_r, strip_c), jnp.float32).at[target].set(child_strips)
+    route = (target[None, :] == jnp.arange(devices * capacity, dtype=jnp.int32)[:, None]).astype(jnp.float32)
+    outgoing = lax.dot_general(
+        route,
+        child_strips.reshape(held, strip_r * strip_c),
+        (((1,), (0,)), ((), ())),
+        precision=lax.Precision.HIGHEST,
+        preferred_element_type=jnp.float32,
     )
     places = jnp.full((devices * capacity,), local_count, jnp.int32).at[target].set(child_slot)
     arrived, landing = (
@@ -105,7 +110,17 @@
             perm.append((k * col_count + j, (col_count * b + j) * col_count + c))
     mine = lax.ppermute(my_piece, ("row", "col"), perm)
     column_panel = lax.all_gather(mine, "row", axis=0, tiled=True)
-    panel_here = lax.all_gather(my_piece, "col", axis=0, tiled=True)
+    shifted = [my_piece]
+    for s_ in range(1, col_count):
+        perm = [
+            (k * col_count + j, k * col_count + (j + s_) % col_count)
+            for k in range(row_count)
+            for j in range(col_count)
+        ]
+        shifted.append(lax.ppermute(my_piece, ("row", "col"), perm))
+    turned = jnp.stack([shifted[(col_count - m) % col_count] for m in range(col_count)] * 2)
+    panel_here = lax.dynamic_slice_in_dim(turned, (col_count - col_id) % col_count, col_count, 0)
+    panel_here = panel_here.reshape(rows_dev, PANEL)
     update = lax.dot_general(
         panel_here,
         column_panel,

time: 508 us -> 484 us (0.953)
  waiting for transfers between devices: 149 us -> 91.1 us
  starting transfers between devices: 42.1 us -> 73 us
    all_gather x1, waiting for transfers between devices: 54.4 us -> 13.3 us  [shards(): column_panel = lax.all_gather(mine, 'row', axis=0, tiled=True)]
    ppermute x0 -> x7, starting transfers between devices: none -> 19.1 us  [shards(): shifted.append(lax.ppermute(my_piece, ('row', 'col'), perm))]
    all_gather x1 -> x0, waiting for transfers between devices: 17.6 us -> none  [shards(): panel_here = lax.all_gather(my_piece, 'col', axis=0, tiled=True)]
    scatter x1 -> x0, local copies, waits for them, and re-layouts: 15.7 us -> none  [shards(): jnp.zeros((devices * capacity, strip_r, strip_c), jnp.float32).at[target]]
    ppermute x0 -> x7, waiting for transfers between devices: none -> 12.8 us  [shards(): shifted.append(lax.ppermute(my_piece, ('row', 'col'), perm))]
    unnamed x24 -> x34, local copies, waits for them, and re-layouts: 29.1 us -> 41 us
    all_gather x1, starting transfers between devices: 0.04 us -> 11.9 us  [shards(): factor_col0 = lax.all_gather(held_l, 'row', axis=0, tiled=True)]
    all_to_all x1, waiting for transfers between devices: 50.6 us -> 38.8 us  [shards(): lax.all_to_all(outgoing.reshape(devices, capacity, strip_r, strip_c), ('r...]
  transfers between devices with their start and end apart: 28 -> 34, of which waited for: 5 -> 7; matrix products, arithmetic and copies ran while one was open for 18% -> 20% of each run, Pallas kernels for 0% -> 0%
where the time goes in v4:
time: 484 us; the launch traced here: 476 us
  other arithmetic  163 us (34%)
  waiting for transfers between devices  91.1 us (19%)
  local copies, waits for them, and re-layouts  88.2 us (18%)
  starting transfers between devices  73 us (15%)
  matrix products  42.6 us (9%)
  between operations  17.6 us (4%)
    another operation x14, other arithmetic, shards(): factor11 = jnp.linalg.cholesky(safe_block)  78.9 us
    unnamed x34, local copies, waits for them, and re-layouts  41 us
    another operation x4, other arithmetic, shards(): lax.linalg.triangular_solve(factor_col0, assembled[:, :PANEL], left_side=...  40.9 us
    all_to_all x1, waiting for transfers between devices, shards(): lax.all_to_all(outgoing.reshape(devices, capacity, strip_r, strip_c), ('r...  38.8 us
    scatter-add x1, other arithmetic, shards(): tiles.at[landing // strips_across, :, landing % strips_across, :]  35.4 us
    dot_general x1, matrix products, shards(): lax.dot_general(panel_here, column_panel, (((1,), (1,)), ((), ())), preci...  20.2 us
    ppermute x7, starting transfers between devices, shards(): shifted.append(lax.ppermute(my_piece, ('row', 'col'), perm))  19.1 us
    ppermute x7, waiting for transfers between devices, shards(): lax.ppermute(solved[j * piece_rows:(j + 1) * piece_rows], ('row', 'col'),...  18.3 us
  transfers between devices with their start and end apart: 34, of which 7 were waited for; matrix products, arithmetic and copies ran while one was open for 20% of the time, Pallas kernels for 0%

profile of v4, /device:TPU:1, one launch (start us, length us, event | category | flops | bytes accessed | tf_op | source)
XLA Modules:
  0.0 475.5 jit_solution(12112758046929099529)
XLA Ops:
  10.6 11.5 %all-to-all-start = ((s32[128,1,2]{2,1,0:T(1,128)}), s32[128,1,2]{2,1,0:T(1,128)S(1)}, u32[]{:S(2)}, u32[]{:S(2)}) async-start(s32[128,1,2]{2,1,0:T(1,128)} %bitcast.3), calls=%async_computation | async-start | bytes 131072 | tf_op jit(solution)/shard_map/all_to_all | solution.py:44
  22.8 4.5 copy.78
  31.1 4.4 copy.48
  35.5 10.2 %all-to-all-start.1 = ((f32[128,2,32,128]{3,2,1,0:T(8,128)}), f32[128,2,32,128]{3,2,1,0:T(8,128)}, u32[]{:S(2)}, u32[]{:S(2)}) async-start(f32[128,2,32,128]{3,2,1,0:T(8,128)} %copy.48), calls=%async_computation.1 | async-start | bytes 8388608 | tf_op jit(solution)/shard_map/all_to_all | solution.py:37
  45.8 11.9 %all-gather.3.cloned.1.call-start = ((), (), s32[]{:S(2)}) async-start(), calls=%async_computation.2 | async-start | bytes 1114112 | tf_op jit(solution)/shard_map/all_gather | solution.py:85
  59.5 38.8 %all-to-all-done.1 = f32[128,2,32,128]{3,2,1,0:T(8,128)} async-done(((f32[128,2,32,128]{3,2,1,0:T(8,128)}), f32[128,2,32,128]{3,2,1,0:T(8,128)}, u32[]{:S(2)}, u32[]{:S(2)}) %all-to-all-start.1) | async-done | bytes 4194336 | tf_op jit(solution)/shard_map/all_to_all | solution.py:37
  98.3 8.0 %copy.77 = f32[32,8,32,128]{3,1,2,0:T(8,128)} copy(f32[32,8,32,128]{3,2,1,0:T(8,128)} %bitcast.55) | data formatting | bytes 8388608
  106.3 5.7 %copy.52 = f32[4096,256]{1,0:T(8,128)} copy(f32[4096,256]{0,1:T(8,128)} %bitcast.148) | data formatting | bytes 8388608 | tf_op jit(solution)/shard_map/dot_general | solution.py:66
  111.9 4.5 convolution_bitcast_fusion
  118.9 11.7 %cholesky.104 = f32[128,128]{1,0:T(8,128)S(1)} custom-call(f32[128,128]{1,0:T(8,128)S(1)} %cholesky.266), custom_call_target="Cholesky" | custom-call | tf_op jit(solution)/shard_map/jit(cholesky)/cholesky | solution.py:78
  130.7 9.8 %custom-call.30 = f32[1,128,128]{1,2,0:T(8,128)S(1)} custom-call(f32[1,128,128]{2,1,0:T(8,128)S(1)} %get-tuple-element.53), custom_call_target="InvertDiagBlocksLowerTriangular" | custom-call | tf_op jit(solution)/shard_map/jit(cholesky)/cholesky | solution.py:78
  141.3 12.1 %cholesky.217 = f32[128,128]{1,0:T(8,128)S(1)} custom-call(f32[128,128]{1,0:T(8,128)S(1)} %cholesky.270), custom_call_target="Cholesky" | custom-call | tf_op jit(solution)/shard_map/jit(cholesky)/cholesky | solution.py:78
  153.4 9.8 %custom-call.31 = f32[1,128,128]{1,2,0:T(8,128)S(1)} custom-call(f32[1,128,128]{2,1,0:T(8,128)S(1)} %get-tuple-element.50), custom_call_target="InvertDiagBlocksLowerTriangular" | custom-call | tf_op jit(solution)/shard_map/jit(cholesky)/cholesky | solution.py:78
  163.9 11.7 %cholesky.238 = f32[128,128]{1,0:T(8,128)S(1)} custom-call(f32[128,128]{1,0:T(8,128)S(1)} %cholesky.275), custom_call_target="Cholesky" | custom-call | tf_op jit(solution)/shard_map/jit(cholesky)/cholesky | solution.py:78
  176.3 9.8 %custom-call.32 = f32[1,128,128]{1,2,0:T(8,128)S(1)} custom-call(f32[1,128,128]{2,1,0:T(8,128)S(1)} %get-tuple-element.47), custom_call_target="InvertDiagBlocksLowerTriangular" | custom-call | tf_op jit(solution)/shard_map/jit(cholesky)/cholesky | solution.py:78
  186.7 11.9 %cholesky.255 = f32[128,128]{1,0:T(8,128)S(1)} custom-call(f32[128,128]{1,0:T(8,128)S(1)} %convolution_subtract_fusion.4), custom_call_target="Cholesky" | custom-call | tf_op jit(solution)/shard_map/jit(cholesky)/cholesky | solution.py:78
  213.8 5.4 %copy.65 = f32[128,8,16,128]{3,2,1,0:T(8,128)S(1)} copy(f32[128,8,16,128]{3,1,2,0:T(8,128)} %bitcast.153) | data formatting | bytes 16777216
  219.1 6.8 %copy.49 = f32[32,32,16,128]{3,1,2,0:T(8,128)} copy(f32[32,32,16,128]{3,2,1,0:T(8,128)S(1)} %bitcast.145) | data formatting | bytes 16777216 | tf_op jit(solution)/shard_map/reshape | solution.py:87
  227.4 35.4 %scatter_fusion = f32[32,32,16,128]{3,1,2,0:T(8,128)} fusion(f32[32,32,16,128]{3,1,2,0:T(8,128)} %copy.49, s32[256]{0:T(256)S(1)} %bitcast.146, f32[256,32,128]{2,1,0:T(8,128)} %bitcast.10), kind=kCustom, calls=%fused_computation.1 | custom fusion | flops 1048576 | bytes 12584960 | tf_op jit(solution)/shard_map/scatter-add | solution.py:88
  262.8 11.0 %copy.50 = f32[32,32,16,128]{3,2,1,0:T(8,128)S(1)} copy(f32[32,32,16,128]{3,1,2,0:T(8,128)} %scatter_fusion) | data formatting | bytes 16777216 | tf_op jit(solution)/shard_map/scatter-add | solution.py:88
  277.1 7.9 %copy.76 = f32[128,8,16,128]{3,1,2,0:T(8,128)} copy(f32[128,8,16,128]{3,2,1,0:T(8,128)S(1)} %bitcast.143) | data formatting | bytes 16777216
  286.4 8.1 %while.1 = (s32[]{:T(128)}, f32[512,512]{1,0:T(8,128)S(1)}, s32[4,2]{0,1:T(2,128)S(1)}, f32[4,128,128]{2,1,0:T(8,128)S(1)}, s32[]{:T(128)}) while((s32[]{:T(128)}, f32[512,512]{1,0:T(8,128)S(1)}, s32[4,2]{0,1:T(2,128)S(1)}, f32[4,128,128]{2,1,0:T(8,128)S(1)}, s32[]{:T(128)}) %tuple.52), condition=%wide.while_cond, body=%wide.while_body.sunk | while | flops 2 | bytes 131181 | solution.py:93
  294.4 39.3 %custom-call.33 = f32[4,128,128]{1,2,0:T(8,128)S(1)} custom-call(f32[4,128,128]{2,1,0:T(8,128)S(1)} %get-tuple-element.9), custom_call_target="InvertDiagBlocksLowerTriangular" | custom-call | tf_op jit(solution)/shard_map/triangular_solve | solution.py:93
  341.6 4.5 fusion.6
  359.5 18.3 %collective-permute-done.21 = f32[128,512]{1,0:T(8,128)} collective-permute-done((f32[128,512]{1,0:T(8,128)S(1)}, f32[128,512]{1,0:T(8,128)}, u32[]{:S(2)}, u32[]{:S(2)}) %collective-permute-start.21) | collective-permute-done | bytes 262176 | tf_op jit(solution)/shard_map/ppermute | solution.py:102
  381.6 8.0 %collective-permute-done.29 = f32[128,512]{1,0:T(8,128)S(1)} collective-permute-done((f32[128,512]{1,0:T(8,128)S(1)}, f32[128,512]{1,0:T(8,128)S(1)}, u32[]{:S(2)}, u32[]{:S(2)}) %collective-permute-start.29) | collective-permute-done | bytes 262176 | tf_op jit(solution)/shard_map/ppermute | solution.py:111
  390.3 6.2 %collective-permute-start.23 = (f32[128,512]{1,0:T(8,128)S(1)}, f32[128,512]{1,0:T(8,128)S(1)}, u32[]{:S(2)}, u32[]{:S(2)}) collective-permute-start(f32[128,512]{1,0:T(8,128)S(1)} %get-tuple-element.19), channel_id=1, source_target_pairs={{0,6},{1,7},{2,0},{3,1},{4,2},{5,3},{6,4},{7,5},{8,14},{9,15},{10,... | collective-permute-start | bytes 786440 | tf_op jit(solution)/shard_map/ppermute | solution.py:120
  396.5 7.5 %collective-permute-start.24 = (f32[128,512]{1,0:T(8,128)S(1)}, f32[128,512]{1,0:T(8,128)S(1)}, u32[]{:S(2)}, u32[]{:S(2)}) collective-permute-start(f32[128,512]{1,0:T(8,128)S(1)} %get-tuple-element.19), channel_id=1, source_target_pairs={{0,5},{1,6},{2,7},{3,0},{4,1},{5,2},{6,3},{7,4},{8,13},{9,14},{10,... | collective-permute-start | bytes 786440 | tf_op jit(solution)/shard_map/ppermute | solution.py:120
  404.0 3.5 collective-permute-start.26
  413.8 8.1 %collective-permute-done.26 = f32[128,512]{1,0:T(8,128)S(1)} collective-permute-done((f32[128,512]{1,0:T(8,128)S(1)}, f32[128,512]{1,0:T(8,128)S(1)}, u32[]{:S(2)}, u32[]{:S(2)}) %collective-permute-start.26) | collective-permute-done | bytes 262176 | tf_op jit(solution)/shard_map/ppermute | solution.py:120
  435.0 13.3 %all-gather.5.cloned.1.call-done = f32[2048,512]{1,0:T(8,128)} async-done(((f32[128,512]{1,0:T(8,128)}), f32[2048,512]{1,0:T(8,128)}) %all-gather.5.cloned.1.call-update) | async-done | bytes 4194320 | tf_op jit(solution)/shard_map/all_gather | solution.py:112
  448.3 20.2 %select_subtract_fusion = f32[1024,2048]{1,0:T(8,128)} fusion(pred[2048]{0:T(1024)(128)(4,1)S(1)} %add_compare_fusion, pred[1024]{0:T(1024)(128)(4,1)S(1)} %add_compare_fusion.1, f32[1024,512]{1,0:T(8,128)S(1)} %bitcast.154, f32[2048,512]{1,0:T(8,128)} %all-gather.5.cloned.1.call-done, f32[128,8,16,128]{3,2,1,0:T(8,128)} %bitcast.144), kind=kOutput, calls=%fused_computation.5 | convolution fusion | flops 12891193344 | bytes 23071744 | tf_op jit(solution)/shard_map/dot_general | solution.py:124
  (166 shorter events, 86.1 us)
Async XLA Ops:
  10.6 24.9 %all-to-all-start = ((s32[128,1,2]{2,1,0:T(1,128)}), s32[128,1,2]{2,1,0:T(1,128)S(1)}, u32[]{:S(2)}, u32[]{:S(2)}) async-start(s32[128,1,2]{2,1,0:T(1,128)} %bitcast.3), calls=%async_computation | async-start | bytes 131072 | tf_op jit(solution)/shard_map/all_to_all | solution.py:44
  35.5 62.7 %all-to-all-start.1 = ((f32[128,2,32,128]{3,2,1,0:T(8,128)}), f32[128,2,32,128]{3,2,1,0:T(8,128)}, u32[]{:S(2)}, u32[]{:S(2)}) async-start(f32[128,2,32,128]{3,2,1,0:T(8,128)} %copy.48), calls=%async_computation.1 | async-start | bytes 8388608 | tf_op jit(solution)/shard_map/all_to_all | solution.py:37
  45.8 239.2 %all-gather.3.cloned.1.call-start = ((), (), s32[]{:S(2)}) async-start(), calls=%async_computation.2 | async-start | bytes 1114112 | tf_op jit(solution)/shard_map/all_gather | solution.py:85
  202.7 3.4 collective-permute-start
  203.4 3.4 collective-permute-start.1
  204.1 3.4 collective-permute-start.10
  204.7 3.4 collective-permute-start.11
  205.4 3.4 collective-permute-start.12
  206.1 3.4 collective-permute-start.13
  206.8 3.4 collective-permute-start.14
  207.5 3.4 collective-permute-start.2
  208.1 3.4 collective-permute-start.3
  208.8 3.4 collective-permute-start.4
  209.5 3.4 collective-permute-start.5
  210.2 2.7 collective-permute-start.6
  210.9 2.1 collective-permute-start.7
  213.7 234.6 %all-gather.5.cloned.1.call-start = ((), (), s32[]{:S(2)}) async-start(), calls=%async_computation.3 | async-start | bytes 4456448 | tf_op jit(solution)/shard_map/all_gather | solution.py:112
  350.4 5.5 %collective-permute-start.15 = (f32[128,512]{1,0:T(8,128)S(1)}, f32[128,512]{1,0:T(8,128)S(1)}, u32[]{:S(2)}, u32[]{:S(2)}) collective-permute-start(f32[128,512]{1,0:T(8,128)S(1)} %get-tuple-element.28), channel_id=1, source_target_pairs={{0,7},{8,15},{16,23},{24,31},{32,39},{40,47},{48,55},{56,63},{64,7... | collective-permute-start | bytes 786440 | tf_op jit(solution)/shard_map/ppermute | solution.py:102
  351.1 6.2 %collective-permute-start.16 = (f32[128,512]{1,0:T(8,128)S(1)}, f32[128,512]{1,0:T(8,128)S(1)}, u32[]{:S(2)}, u32[]{:S(2)}) collective-permute-start(f32[128,512]{1,0:T(8,128)S(1)} %get-tuple-element.27), channel_id=1, source_target_pairs={{0,6},{8,14},{16,22},{24,30},{32,38},{40,46},{48,54},{56,62},{64,7... | collective-permute-start | bytes 786440 | tf_op jit(solution)/shard_map/ppermute | solution.py:102
  351.8 7.7 %collective-permute-start.17 = (f32[128,512]{1,0:T(8,128)S(1)}, f32[128,512]{1,0:T(8,128)}, u32[]{:S(2)}, u32[]{:S(2)}) collective-permute-start(f32[128,512]{1,0:T(8,128)S(1)} %get-tuple-element.26), channel_id=1, source_target_pairs={{0,5},{8,13},{16,21},{24,29},{32,37},{40,45},{48,53},{56,61},{64,6... | collective-permute-start | bytes 786440 | tf_op jit(solution)/shard_map/ppermute | solution.py:102
  353.2 6.3 %collective-permute-start.18 = (f32[128,512]{1,0:T(8,128)S(1)}, f32[128,512]{1,0:T(8,128)}, u32[]{:S(2)}, u32[]{:S(2)}) collective-permute-start(f32[128,512]{1,0:T(8,128)S(1)} %get-tuple-element.25), channel_id=1, source_target_pairs={{0,4},{8,12},{16,20},{24,28},{32,36},{40,44},{48,52},{56,60},{64,6... | collective-permute-start | bytes 786440 | tf_op jit(solution)/shard_map/ppermute | solution.py:102
  354.6 4.9 %collective-permute-start.19 = (f32[128,512]{1,0:T(8,128)S(1)}, f32[128,512]{1,0:T(8,128)}, u32[]{:S(2)}, u32[]{:S(2)}) collective-permute-start(f32[128,512]{1,0:T(8,128)S(1)} %get-tuple-element.24), channel_id=1, source_target_pairs={{0,3},{8,11},{16,19},{24,27},{32,35},{40,43},{48,51},{56,59},{64,6... | collective-permute-start | bytes 786440 | tf_op jit(solution)/shard_map/ppermute | solution.py:102
  355.9 3.6 collective-permute-start.20
  358.0 19.8 %collective-permute-start.21 = (f32[128,512]{1,0:T(8,128)S(1)}, f32[128,512]{1,0:T(8,128)}, u32[]{:S(2)}, u32[]{:S(2)}) collective-permute-start(f32[128,512]{1,0:T(8,128)S(1)} %get-tuple-element.22), channel_id=1, source_target_pairs={{0,1},{8,9},{16,17},{24,25},{32,33},{40,41},{48,49},{56,57},{64,65... | collective-permute-start | bytes 786440 | tf_op jit(solution)/shard_map/ppermute | solution.py:102
  379.7 9.9 %collective-permute-start.29 = (f32[128,512]{1,0:T(8,128)S(1)}, f32[128,512]{1,0:T(8,128)S(1)}, u32[]{:S(2)}, u32[]{:S(2)}) collective-permute-start(f32[128,512]{1,0:T(8,128)S(1)} %get-tuple-element.19), channel_id=1, source_target_pairs={{0,0},{1,8},{2,16},{3,24},{4,32},{5,40},{6,48},{7,56},{8,64},{9,72... | collective-permute-start | bytes 786440 | tf_op jit(solution)/shard_map/ppermute | solution.py:111
  390.3 17.2 %collective-permute-start.22 = (f32[128,512]{1,0:T(8,128)S(1)}, f32[128,512]{1,0:T(8,128)S(1)}, u32[]{:S(2)}, u32[]{:S(2)}) collective-permute-start(f32[128,512]{1,0:T(8,128)S(1)} %get-tuple-element.19), channel_id=1, source_target_pairs={{0,7},{1,0},{2,1},{3,2},{4,3},{5,4},{6,5},{7,6},{8,15},{9,8},{10,9... | collective-permute-start | bytes 786440 | tf_op jit(solution)/shard_map/ppermute | solution.py:120
  390.3 18.2 %collective-permute-start.23 = (f32[128,512]{1,0:T(8,128)S(1)}, f32[128,512]{1,0:T(8,128)S(1)}, u32[]{:S(2)}, u32[]{:S(2)}) collective-permute-start(f32[128,512]{1,0:T(8,128)S(1)} %get-tuple-element.19), channel_id=1, source_target_pairs={{0,6},{1,7},{2,0},{3,1},{4,2},{5,3},{6,4},{7,5},{8,14},{9,15},{10,... | collective-permute-start | bytes 786440 | tf_op jit(solution)/shard_map/ppermute | solution.py:120
  396.5 14.4 %collective-permute-start.24 = (f32[128,512]{1,0:T(8,128)S(1)}, f32[128,512]{1,0:T(8,128)S(1)}, u32[]{:S(2)}, u32[]{:S(2)}) collective-permute-start(f32[128,512]{1,0:T(8,128)S(1)} %get-tuple-element.19), channel_id=1, source_target_pairs={{0,5},{1,6},{2,7},{3,0},{4,1},{5,2},{6,3},{7,4},{8,13},{9,14},{10,... | collective-permute-start | bytes 786440 | tf_op jit(solution)/shard_map/ppermute | solution.py:120
  404.0 9.0 %collective-permute-start.25 = (f32[128,512]{1,0:T(8,128)S(1)}, f32[128,512]{1,0:T(8,128)S(1)}, u32[]{:S(2)}, u32[]{:S(2)}) collective-permute-start(f32[128,512]{1,0:T(8,128)S(1)} %get-tuple-element.19), channel_id=1, source_target_pairs={{0,4},{1,5},{2,6},{3,7},{4,0},{5,1},{6,2},{7,3},{8,12},{9,13},{10,... | collective-permute-start | bytes 786440 | tf_op jit(solution)/shard_map/ppermute | solution.py:120
  404.0 17.9 %collective-permute-start.26 = (f32[128,512]{1,0:T(8,128)S(1)}, f32[128,512]{1,0:T(8,128)S(1)}, u32[]{:S(2)}, u32[]{:S(2)}) collective-permute-start(f32[128,512]{1,0:T(8,128)S(1)} %get-tuple-element.19), channel_id=1, source_target_pairs={{0,3},{1,4},{2,5},{3,6},{4,7},{5,0},{6,1},{7,2},{8,11},{9,12},{10,... | collective-permute-start | bytes 786440 | tf_op jit(solution)/shard_map/ppermute | solution.py:120
  407.5 15.1 %collective-permute-start.27 = (f32[128,512]{1,0:T(8,128)S(1)}, f32[128,512]{1,0:T(8,128)S(1)}, u32[]{:S(2)}, u32[]{:S(2)}) collective-permute-start(f32[128,512]{1,0:T(8,128)S(1)} %get-tuple-element.19), channel_id=1, source_target_pairs={{0,2},{1,3},{2,4},{3,5},{4,6},{5,7},{6,0},{7,1},{8,10},{9,11},{10,... | collective-permute-start | bytes 786440 | tf_op jit(solution)/shard_map/ppermute | solution.py:120
  408.6 18.0 %collective-permute-start.28 = (f32[128,512]{1,0:T(8,128)S(1)}, f32[128,512]{1,0:T(8,128)S(1)}, u32[]{:S(2)}, u32[]{:S(2)}) collective-permute-start(f32[128,512]{1,0:T(8,128)S(1)} %get-tuple-element.19), channel_id=1, source_target_pairs={{0,1},{1,2},{2,3},{3,4},{4,5},{5,6},{6,7},{7,0},{8,9},{9,10},{10,1... | collective-permute-start | bytes 786440 | tf_op jit(solution)/shard_map/ppermute | solution.py:120
  (9 other events, 45.9 us)
Sparse Core Ops, SparseCore 0:
  213.8 53.3 all-gather.2
  390.4 57.7 all-gather.4

commit v5 on v4

--- a/solution.py
+++ b/solution.py
@@ -56,13 +56,12 @@
     first_rows = row_id == 0
     is_owner = first_rows & (col_id == 0)
 
-    down = PANEL // strip_r
     across = PANEL // strip_c
     srow = landing // strips_across
     scol = landing % strips_across
-    hit = (srow < down) & (scol < across)
-    spot = jnp.where(hit, srow * across + scol, down * across)
-    pick = (spot[None, :] == jnp.arange(down * across, dtype=jnp.int32)[:, None]).astype(jnp.float32)
+    hit = (srow < strips_down) & (scol < across)
+    spot = jnp.where(hit, srow * across + scol, strips_down * across)
+    pick = (spot[None, :] == jnp.arange(strips_down * across, dtype=jnp.int32)[:, None]).astype(jnp.float32)
     part = lax.dot_general(
         pick,
         arrived.reshape(arrived.shape[0], strip_r * strip_c),
@@ -70,8 +69,9 @@
         precision=lax.Precision.HIGHEST,
         preferred_element_type=jnp.float32,
     )
-    part = part.reshape(down, across, strip_r, strip_c).transpose(0, 2, 1, 3).reshape(PANEL, PANEL)
-    top_block = front[:PANEL, :PANEL] + part
+    part = part.reshape(strips_down, across, strip_r, strip_c).transpose(0, 2, 1, 3)
+    panel_cols = front[:, :PANEL] + part.reshape(rows_dev, PANEL)
+    top_block = panel_cols[:PANEL]
     safe_block = jnp.where(
         is_owner, 0.5 * (top_block + top_block.T), jnp.eye(PANEL, dtype=jnp.float32)
     )
@@ -91,7 +91,7 @@
     assembled = tiles.reshape(rows_dev, cols_dev)
 
     solved = lax.linalg.triangular_solve(
-        factor_col0, assembled[:, :PANEL], left_side=False, lower=True, transpose_a=True
+        factor_col0, panel_cols, left_side=False, lower=True, transpose_a=True
     )
     headed = jnp.concatenate([factor_col0, solved[PANEL:]], axis=0)
     solved = jnp.where(first_rows, headed, solved)
@@ -125,7 +125,7 @@
         panel_here,
         column_panel,
         (((1,), (1,)), ((), ())),
-        precision=lax.Precision.HIGHEST,
+        precision=lax.Precision.HIGH,
         preferred_element_type=jnp.float32,
     )
     global_rows = row_id * rows_dev + jnp.arange(rows_dev, dtype=jnp.int32)

time: 484 us -> 518 us (1.070)
  the two profiles are of different devices: /device:TPU:1 before, /device:TPU:6 now
where the time goes in v5:
time: 518 us; the launch traced here: 510 us
  other arithmetic  171 us (33%)
  waiting for transfers between devices  145 us (28%)
  local copies, waits for them, and re-layouts  81.2 us (16%)
  starting transfers between devices  54.8 us (11%)
  matrix products  39.8 us (8%)
  between operations  17.7 us (3%)
    another operation x14, other arithmetic, shards(): factor11 = jnp.linalg.cholesky(safe_block)  78.9 us
    all_to_all x1, waiting for transfers between devices, shards(): lax.all_to_all(outgoing.reshape(devices, capacity, strip_r, strip_c), ('r...  48.2 us
    all_gather x1, waiting for transfers between devices, shards(): factor_col0 = lax.all_gather(held_l, 'row', axis=0, tiled=True)  47 us
    another operation x4, other arithmetic, shards(): lax.linalg.triangular_solve(factor_col0, panel_cols, left_side=False, low...  42.2 us
    scatter-add x1, other arithmetic, shards(): tiles.at[landing // strips_across, :, landing % strips_across, :]  37.6 us
    unnamed x41, local copies, waits for them, and re-layouts  24.3 us
    ppermute x7, waiting for transfers between devices, shards(): shifted.append(lax.ppermute(my_piece, ('row', 'col'), perm))  21.8 us
    ppermute x1, waiting for transfers between devices, shards(): mine = lax.ppermute(my_piece, ('row', 'col'), perm)  18.7 us
  transfers between devices with their start and end apart: 34, of which 9 were waited for; matrix products, arithmetic and copies ran while one was open for 16% of the time, Pallas kernels for 0%

profile of v5, /device:TPU:6, one launch (start us, length us, event | category | flops | bytes accessed | tf_op | source)
XLA Modules:
  0.0 509.7 jit_solution(15623081528137978744)
XLA Ops:
  10.6 10.5 %all-to-all-start = ((s32[128,1,2]{2,1,0:T(1,128)}), s32[128,1,2]{2,1,0:T(1,128)S(1)}, u32[]{:S(2)}, u32[]{:S(2)}) async-start(s32[128,1,2]{2,1,0:T(1,128)} %bitcast.3), calls=%async_computation | async-start | bytes 131072 | tf_op jit(solution)/shard_map/all_to_all | solution.py:44
  21.8 4.5 copy.85
  30.1 4.4 copy.51
  34.5 10.2 %all-to-all-start.1 = ((f32[128,2,32,128]{3,2,1,0:T(8,128)}), f32[128,2,32,128]{3,2,1,0:T(8,128)}, u32[]{:S(2)}, u32[]{:S(2)}) async-start(f32[128,2,32,128]{3,2,1,0:T(8,128)} %copy.51), calls=%async_computation.1 | async-start | bytes 8388608 | tf_op jit(solution)/shard_map/all_to_all | solution.py:37
  48.3 48.2 %all-to-all-done.1 = f32[128,2,32,128]{3,2,1,0:T(8,128)} async-done(((f32[128,2,32,128]{3,2,1,0:T(8,128)}), f32[128,2,32,128]{3,2,1,0:T(8,128)}, u32[]{:S(2)}, u32[]{:S(2)}) %all-to-all-start.1) | async-done | bytes 4194336 | tf_op jit(solution)/shard_map/all_to_all | solution.py:37
  96.5 8.0 %copy.83 = f32[32,8,32,128]{3,1,2,0:T(8,128)} copy(f32[32,8,32,128]{3,2,1,0:T(8,128)} %bitcast.55) | data formatting | bytes 8388608
  104.5 5.7 %copy.55 = f32[4096,256]{1,0:T(8,128)} copy(f32[4096,256]{0,1:T(8,128)} %bitcast.144) | data formatting | bytes 8388608 | tf_op jit(solution)/shard_map/dot_general | solution.py:65
  110.2 4.7 convolution_bitcast_fusion
  118.6 2.6 add.219
  127.9 11.7 %cholesky.104 = f32[128,128]{1,0:T(8,128)S(1)} custom-call(f32[128,128]{1,0:T(8,128)S(1)} %cholesky.266), custom_call_target="Cholesky" | custom-call | tf_op jit(solution)/shard_map/jit(cholesky)/cholesky | solution.py:78
  139.7 9.8 %custom-call.30 = f32[1,128,128]{1,2,0:T(8,128)S(1)} custom-call(f32[1,128,128]{2,1,0:T(8,128)S(1)} %get-tuple-element.53), custom_call_target="InvertDiagBlocksLowerTriangular" | custom-call | tf_op jit(solution)/shard_map/jit(cholesky)/cholesky | solution.py:78
  152.1 11.7 %cholesky.217 = f32[128,128]{1,0:T(8,128)S(1)} custom-call(f32[128,128]{1,0:T(8,128)S(1)} %cholesky.270), custom_call_target="Cholesky" | custom-call | tf_op jit(solution)/shard_map/jit(cholesky)/cholesky | solution.py:78
  163.8 10.0 %custom-call.31 = f32[1,128,128]{1,2,0:T(8,128)S(1)} custom-call(f32[1,128,128]{2,1,0:T(8,128)S(1)} %get-tuple-element.50), custom_call_target="InvertDiagBlocksLowerTriangular" | custom-call | tf_op jit(solution)/shard_map/jit(cholesky)/cholesky | solution.py:78
  175.4 11.7 %cholesky.238 = f32[128,128]{1,0:T(8,128)S(1)} custom-call(f32[128,128]{1,0:T(8,128)S(1)} %cholesky.275), custom_call_target="Cholesky" | custom-call | tf_op jit(solution)/shard_map/jit(cholesky)/cholesky | solution.py:78
  187.1 9.8 %custom-call.32 = f32[1,128,128]{1,2,0:T(8,128)S(1)} custom-call(f32[1,128,128]{2,1,0:T(8,128)S(1)} %get-tuple-element.47), custom_call_target="InvertDiagBlocksLowerTriangular" | custom-call | tf_op jit(solution)/shard_map/jit(cholesky)/cholesky | solution.py:78
  198.4 12.1 %cholesky.255 = f32[128,128]{1,0:T(8,128)S(1)} custom-call(f32[128,128]{1,0:T(8,128)S(1)} %convolution_subtract_fusion.4), custom_call_target="Cholesky" | custom-call | tf_op jit(solution)/shard_map/jit(cholesky)/cholesky | solution.py:78
  221.3 6.6 %collective-permute-done.11 = f32[32,512]{1,0:T(8,128)S(1)} collective-permute-done((f32[32,512]{1,0:T(8,128)S(1)}, f32[32,512]{1,0:T(8,128)S(1)}, u32[]{:S(2)}, u32[]{:S(2)}) %collective-permute-start.11) | collective-permute-done | bytes 65568 | tf_op jit(solution)/shard_map/ppermute | solution.py:83
  233.5 47.0 %all-gather.3.cloned.1.call-done = f32[512,512]{1,0:T(8,128)} async-done(((f32[32,512]{1,0:T(8,128)}), f32[512,512]{1,0:T(8,128)}) %all-gather.3.cloned.1.call-update) | async-done | bytes 1048592 | tf_op jit(solution)/shard_map/all_gather | solution.py:85
  281.8 10.4 %while.1 = (s32[]{:T(128)}, f32[512,512]{1,0:T(8,128)S(1)}, s32[4,2]{0,1:T(2,128)S(1)}, f32[4,128,128]{2,1,0:T(8,128)}, s32[]{:T(128)}) while((s32[]{:T(128)}, f32[512,512]{1,0:T(8,128)S(1)}, s32[4,2]{0,1:T(2,128)S(1)}, f32[4,128,128]{2,1,0:T(8,128)}, s32[]{:T(128)}) %tuple.52), condition=%wide.while_cond, body=%wide.while_body.sunk | while | flops 2 | bytes 132205 | solution.py:93
  293.2 40.7 %custom-call.33 = f32[4,128,128]{1,2,0:T(8,128)} custom-call(f32[4,128,128]{2,1,0:T(8,128)} %get-tuple-element.9), custom_call_target="InvertDiagBlocksLowerTriangular" | custom-call | tf_op jit(solution)/shard_map/triangular_solve | solution.py:93
  342.2 2.9 fusion.6
  353.6 3.3 collective-permute-start.16
  368.0 2.8 collective-permute-done.20
  373.8 18.7 %collective-permute-done.29 = f32[128,512]{1,0:T(8,128)S(1)} collective-permute-done((f32[128,512]{1,0:T(8,128)S(1)}, f32[128,512]{1,0:T(8,128)S(1)}, u32[]{:S(2)}, u32[]{:S(2)}) %collective-permute-start.29) | collective-permute-done | bytes 262176 | tf_op jit(solution)/shard_map/ppermute | solution.py:111
  393.3 5.4 %copy.74 = f32[128,8,16,128]{3,2,1,0:T(8,128)S(1)} copy(f32[128,8,16,128]{3,1,2,0:T(8,128)} %bitcast.145) | data formatting | bytes 16777216
  398.7 6.8 %copy.52 = f32[32,32,16,128]{3,1,2,0:T(8,128)} copy(f32[32,32,16,128]{3,2,1,0:T(8,128)S(1)} %bitcast.141) | data formatting | bytes 16777216 | tf_op jit(solution)/shard_map/reshape | solution.py:87
  407.1 37.6 %scatter_fusion = f32[32,32,16,128]{3,1,2,0:T(8,128)} fusion(f32[32,32,16,128]{3,1,2,0:T(8,128)} %copy.52, s32[256]{0:T(256)S(1)} %bitcast.142, f32[256,32,128]{2,1,0:T(8,128)} %bitcast.10), kind=kCustom, calls=%fused_computation.1 | custom fusion | flops 1048576 | bytes 12584960 | tf_op jit(solution)/shard_map/scatter-add | solution.py:88
  444.7 14.4 %copy.53 = f32[32,32,16,128]{3,2,1,0:T(8,128)} copy(f32[32,32,16,128]{3,1,2,0:T(8,128)} %scatter_fusion) | data formatting | bytes 16777216 | tf_op jit(solution)/shard_map/scatter-add | solution.py:88
  459.4 3.4 collective-permute-start.25
  467.1 8.5 %collective-permute-done.25 = f32[128,512]{1,0:T(8,128)S(1)} collective-permute-done((f32[128,512]{1,0:T(8,128)S(1)}, f32[128,512]{1,0:T(8,128)S(1)}, u32[]{:S(2)}, u32[]{:S(2)}) %collective-permute-start.25) | collective-permute-done | bytes 262176 | tf_op jit(solution)/shard_map/ppermute | solution.py:120
  475.7 11.1 %collective-permute-done.27 = f32[128,512]{1,0:T(8,128)S(1)} collective-permute-done((f32[128,512]{1,0:T(8,128)S(1)}, f32[128,512]{1,0:T(8,128)S(1)}, u32[]{:S(2)}, u32[]{:S(2)}) %collective-permute-start.27) | collective-permute-done | bytes 262176 | tf_op jit(solution)/shard_map/ppermute | solution.py:120
  487.3 15.3 %bitcast_subtract_fusion = f32[1024,2048]{1,0:T(8,128)} fusion(f32[128,8,16,128]{3,2,1,0:T(8,128)} %bitcast.140, pred[2048]{0:T(1024)(128)(4,1)S(1)} %add_compare_fusion, pred[1024]{0:T(1024)(128)(4,1)S(1)} %add_compare_fusion.1, f32[1024,512]{1,0:T(8,128)S(1)} %bitcast.146, f32[2048,512]{1,0:T(8,128)} %all-gather.5.cloned.1.call-done), kind=kOutput, calls=%fused_computation.4 | convolution fusion | flops 6448742400 | bytes 23071744 | tf_op jit(solution)/shard_map/dot_general | solution.py:124
  (175 shorter events, 91.7 us)
Async XLA Ops:
  10.6 23.9 %all-to-all-start = ((s32[128,1,2]{2,1,0:T(1,128)}), s32[128,1,2]{2,1,0:T(1,128)S(1)}, u32[]{:S(2)}, u32[]{:S(2)}) async-start(s32[128,1,2]{2,1,0:T(1,128)} %bitcast.3), calls=%async_computation | async-start | bytes 131072 | tf_op jit(solution)/shard_map/all_to_all | solution.py:44
  34.5 62.0 %all-to-all-start.1 = ((f32[128,2,32,128]{3,2,1,0:T(8,128)}), f32[128,2,32,128]{3,2,1,0:T(8,128)}, u32[]{:S(2)}, u32[]{:S(2)}) async-start(f32[128,2,32,128]{3,2,1,0:T(8,128)} %copy.51), calls=%async_computation.1 | async-start | bytes 8388608 | tf_op jit(solution)/shard_map/all_to_all | solution.py:37
  44.8 235.7 %all-gather.3.cloned.1.call-start = ((), (), s32[]{:S(2)}) async-start(), calls=%async_computation.2 | async-start | bytes 1114112 | tf_op jit(solution)/shard_map/all_gather | solution.py:85
  215.2 4.0 collective-permute-start.14
  215.9 4.0 collective-permute-start.13
  216.6 4.0 collective-permute-start.12
  217.3 10.7 %collective-permute-start.11 = (f32[32,512]{1,0:T(8,128)S(1)}, f32[32,512]{1,0:T(8,128)S(1)}, u32[]{:S(2)}, u32[]{:S(2)}) collective-permute-start(f32[32,512]{1,0:T(8,128)S(1)} %get-tuple-element.33), channel_id=1, source_target_pairs={{0,96}} | collective-permute-start | bytes 196616 | tf_op jit(solution)/shard_map/ppermute | solution.py:83
  218.6 10.0 %collective-permute-start.10 = (f32[32,512]{1,0:T(8,128)S(1)}, f32[32,512]{1,0:T(8,128)S(1)}, u32[]{:S(2)}, u32[]{:S(2)}) collective-permute-start(f32[32,512]{1,0:T(8,128)S(1)} %get-tuple-element.34), channel_id=1, source_target_pairs={{0,88}} | collective-permute-start | bytes 196616 | tf_op jit(solution)/shard_map/ppermute | solution.py:83
  219.2 10.0 %collective-permute-start.9 = (f32[32,512]{1,0:T(8,128)S(1)}, f32[32,512]{1,0:T(8,128)S(1)}, u32[]{:S(2)}, u32[]{:S(2)}) collective-permute-start(f32[32,512]{1,0:T(8,128)S(1)} %get-tuple-element.35), channel_id=1, source_target_pairs={{0,80}} | collective-permute-start | bytes 196616 | tf_op jit(solution)/shard_map/ppermute | solution.py:83
  219.9 10.0 %collective-permute-start.8 = (f32[32,512]{1,0:T(8,128)S(1)}, f32[32,512]{1,0:T(8,128)S(1)}, u32[]{:S(2)}, u32[]{:S(2)}) collective-permute-start(f32[32,512]{1,0:T(8,128)S(1)} %get-tuple-element.36), channel_id=1, source_target_pairs={{0,72}} | collective-permute-start | bytes 196616 | tf_op jit(solution)/shard_map/ppermute | solution.py:83
  220.6 10.0 %collective-permute-start.7 = (f32[32,512]{1,0:T(8,128)S(1)}, f32[32,512]{1,0:T(8,128)S(1)}, u32[]{:S(2)}, u32[]{:S(2)}) collective-permute-start(f32[32,512]{1,0:T(8,128)S(1)} %get-tuple-element.37), channel_id=1, source_target_pairs={{0,64}} | collective-permute-start | bytes 196616 | tf_op jit(solution)/shard_map/ppermute | solution.py:83
  227.9 3.4 collective-permute-start.6
  228.6 3.4 collective-permute-start.5
  229.3 3.4 collective-permute-start.4
  230.0 2.7 collective-permute-start.3
  230.6 2.1 collective-permute-start.2
  233.5 253.8 %all-gather.5.cloned.1.call-start = ((), (), s32[]{:S(2)}) async-start(), calls=%async_computation.3 | async-start | bytes 4456448 | tf_op jit(solution)/shard_map/all_gather | solution.py:112
  351.6 11.3 %collective-permute-start.15 = (f32[128,512]{1,0:T(8,128)S(1)}, f32[128,512]{1,0:T(8,128)S(1)}, u32[]{:S(2)}, u32[]{:S(2)}) collective-permute-start(f32[128,512]{1,0:T(8,128)S(1)} %get-tuple-element.28), channel_id=1, source_target_pairs={{0,7},{8,15},{16,23},{24,31},{32,39},{40,47},{48,55},{56,63},{64,7... | collective-permute-start | bytes 786440 | tf_op jit(solution)/shard_map/ppermute | solution.py:102
  353.6 11.4 %collective-permute-start.16 = (f32[128,512]{1,0:T(8,128)S(1)}, f32[128,512]{1,0:T(8,128)S(1)}, u32[]{:S(2)}, u32[]{:S(2)}) collective-permute-start(f32[128,512]{1,0:T(8,128)S(1)} %get-tuple-element.27), channel_id=1, source_target_pairs={{0,6},{8,14},{16,22},{24,30},{32,38},{40,46},{48,54},{56,62},{64,7... | collective-permute-start | bytes 786440 | tf_op jit(solution)/shard_map/ppermute | solution.py:102
  357.0 10.7 %collective-permute-start.17 = (f32[128,512]{1,0:T(8,128)}, f32[128,512]{1,0:T(8,128)}, u32[]{:S(2)}, u32[]{:S(2)}) collective-permute-start(f32[128,512]{1,0:T(8,128)} %get-tuple-element.26), channel_id=1, source_target_pairs={{0,5},{8,13},{16,21},{24,29},{32,37},{40,45},{48,53},{56,61},{64,6... | collective-permute-start | bytes 786440 | tf_op jit(solution)/shard_map/ppermute | solution.py:102
  359.0 8.7 %collective-permute-start.18 = (f32[128,512]{1,0:T(8,128)S(1)}, f32[128,512]{1,0:T(8,128)}, u32[]{:S(2)}, u32[]{:S(2)}) collective-permute-start(f32[128,512]{1,0:T(8,128)S(1)} %get-tuple-element.25), channel_id=1, source_target_pairs={{0,4},{8,12},{16,20},{24,28},{32,36},{40,44},{48,52},{56,60},{64,6... | collective-permute-start | bytes 786440 | tf_op jit(solution)/shard_map/ppermute | solution.py:102
  361.0 7.0 %collective-permute-start.19 = (f32[128,512]{1,0:T(8,128)S(1)}, f32[128,512]{1,0:T(8,128)}, u32[]{:S(2)}, u32[]{:S(2)}) collective-permute-start(f32[128,512]{1,0:T(8,128)S(1)} %get-tuple-element.24), channel_id=1, source_target_pairs={{0,3},{8,11},{16,19},{24,27},{32,35},{40,43},{48,51},{56,59},{64,6... | collective-permute-start | bytes 786440 | tf_op jit(solution)/shard_map/ppermute | solution.py:102
  363.0 7.8 %collective-permute-start.20 = (f32[128,512]{1,0:T(8,128)S(1)}, f32[128,512]{1,0:T(8,128)}, u32[]{:S(2)}, u32[]{:S(2)}) collective-permute-start(f32[128,512]{1,0:T(8,128)S(1)} %get-tuple-element.23), channel_id=1, source_target_pairs={{0,2},{8,10},{16,18},{24,26},{32,34},{40,42},{48,50},{56,58},{64,6... | collective-permute-start | bytes 786440 | tf_op jit(solution)/shard_map/ppermute | solution.py:102
  365.7 5.1 collective-permute-start.21
  371.8 20.7 %collective-permute-start.29 = (f32[128,512]{1,0:T(8,128)S(1)}, f32[128,512]{1,0:T(8,128)S(1)}, u32[]{:S(2)}, u32[]{:S(2)}) collective-permute-start(f32[128,512]{1,0:T(8,128)S(1)} %get-tuple-element.19), channel_id=1, source_target_pairs={{0,0},{1,8},{2,16},{3,24},{4,32},{5,40},{6,48},{7,56},{8,64},{9,72... | collective-permute-start | bytes 786440 | tf_op jit(solution)/shard_map/ppermute | solution.py:111
  393.2 70.0 %collective-permute-start.22 = (f32[128,512]{1,0:T(8,128)S(1)}, f32[128,512]{1,0:T(8,128)S(1)}, u32[]{:S(2)}, u32[]{:S(2)}) collective-permute-start(f32[128,512]{1,0:T(8,128)S(1)} %get-tuple-element.19), channel_id=1, source_target_pairs={{0,7},{1,0},{2,1},{3,2},{4,3},{5,4},{6,5},{7,6},{8,15},{9,8},{10,9... | collective-permute-start | bytes 786440 | tf_op jit(solution)/shard_map/ppermute | solution.py:120
  407.0 56.7 %collective-permute-start.23 = (f32[128,512]{1,0:T(8,128)S(1)}, f32[128,512]{1,0:T(8,128)S(1)}, u32[]{:S(2)}, u32[]{:S(2)}) collective-permute-start(f32[128,512]{1,0:T(8,128)S(1)} %get-tuple-element.19), channel_id=1, source_target_pairs={{0,6},{1,7},{2,0},{3,1},{4,2},{5,3},{6,4},{7,5},{8,14},{9,15},{10,... | collective-permute-start | bytes 786440 | tf_op jit(solution)/shard_map/ppermute | solution.py:120
  459.1 7.9 %collective-permute-start.24 = (f32[128,512]{1,0:T(8,128)S(1)}, f32[128,512]{1,0:T(8,128)S(1)}, u32[]{:S(2)}, u32[]{:S(2)}) collective-permute-start(f32[128,512]{1,0:T(8,128)S(1)} %get-tuple-element.19), channel_id=1, source_target_pairs={{0,5},{1,6},{2,7},{3,0},{4,1},{5,2},{6,3},{7,4},{8,13},{9,14},{10,... | collective-permute-start | bytes 786440 | tf_op jit(solution)/shard_map/ppermute | solution.py:120
  459.4 16.2 %collective-permute-start.25 = (f32[128,512]{1,0:T(8,128)S(1)}, f32[128,512]{1,0:T(8,128)S(1)}, u32[]{:S(2)}, u32[]{:S(2)}) collective-permute-start(f32[128,512]{1,0:T(8,128)S(1)} %get-tuple-element.19), channel_id=1, source_target_pairs={{0,4},{1,5},{2,6},{3,7},{4,0},{5,1},{6,2},{7,3},{8,12},{9,13},{10,... | collective-permute-start | bytes 786440 | tf_op jit(solution)/shard_map/ppermute | solution.py:120
  462.8 12.9 %collective-permute-start.26 = (f32[128,512]{1,0:T(8,128)S(1)}, f32[128,512]{1,0:T(8,128)S(1)}, u32[]{:S(2)}, u32[]{:S(2)}) collective-permute-start(f32[128,512]{1,0:T(8,128)S(1)} %get-tuple-element.19), channel_id=1, source_target_pairs={{0,3},{1,4},{2,5},{3,6},{4,7},{5,0},{6,1},{7,2},{8,11},{9,12},{10,... | collective-permute-start | bytes 786440 | tf_op jit(solution)/shard_map/ppermute | solution.py:120
  463.2 23.5 %collective-permute-start.27 = (f32[128,512]{1,0:T(8,128)S(1)}, f32[128,512]{1,0:T(8,128)S(1)}, u32[]{:S(2)}, u32[]{:S(2)}) collective-permute-start(f32[128,512]{1,0:T(8,128)S(1)} %get-tuple-element.19), channel_id=1, source_target_pairs={{0,2},{1,3},{2,4},{3,5},{4,6},{5,7},{6,0},{7,1},{8,10},{9,11},{10,... | collective-permute-start | bytes 786440 | tf_op jit(solution)/shard_map/ppermute | solution.py:120
  463.7 23.1 %collective-permute-start.28 = (f32[128,512]{1,0:T(8,128)S(1)}, f32[128,512]{1,0:T(8,128)S(1)}, u32[]{:S(2)}, u32[]{:S(2)}) collective-permute-start(f32[128,512]{1,0:T(8,128)S(1)} %get-tuple-element.19), channel_id=1, source_target_pairs={{0,1},{1,2},{2,3},{3,4},{4,5},{5,6},{6,7},{7,0},{8,9},{9,10},{10,1... | collective-permute-start | bytes 786440 | tf_op jit(solution)/shard_map/ppermute | solution.py:120
  (14 other events, 51.8 us)
Sparse Core Ops, SparseCore 0:
  233.6 46.8 all-gather.2
  393.3 49.7 all-gather.4

commit v6 on v5

--- a/solution.py
+++ b/solution.py
@@ -84,11 +84,16 @@
         held_l = held_l + got
     factor_col0 = lax.all_gather(held_l, "row", axis=0, tiled=True)
 
-    tiles = front.reshape(strips_down, strip_r, strips_across, strip_c)
-    tiles = tiles.at[landing // strips_across, :, landing % strips_across, :].add(
-        arrived, mode="drop"
+    every = (landing[None, :] == jnp.arange(local_count, dtype=jnp.int32)[:, None]).astype(jnp.float32)
+    delta = lax.dot_general(
+        every,
+        arrived.reshape(arrived.shape[0], strip_r * strip_c),
+        (((1,), (0,)), ((), ())),
+        precision=lax.Precision.HIGHEST,
+        preferred_element_type=jnp.float32,
     )
-    assembled = tiles.reshape(rows_dev, cols_dev)
+    delta = delta.reshape(strips_down, strips_across, strip_r, strip_c).transpose(0, 2, 1, 3)
+    delta = delta.reshape(rows_dev, cols_dev)
 
     solved = lax.linalg.triangular_solve(
         factor_col0, panel_cols, left_side=False, lower=True, transpose_a=True
@@ -131,7 +136,7 @@
     global_rows = row_id * rows_dev + jnp.arange(rows_dev, dtype=jnp.int32)
     global_cols = col_id * cols_dev + jnp.arange(cols_dev, dtype=jnp.int32)
     trailing = (global_rows[:, None] >= PANEL) & (global_cols[None, :] >= PANEL)
-    factored = assembled - jnp.where(trailing, update, 0.0)
+    factored = (front + delta) - jnp.where(trailing, update, 0.0)
     return (factored, panel_here)
 
 

time: 518 us -> 476 us (0.919)
  the two profiles are of different devices: /device:TPU:6 before, /device:TPU:1 now
where the time goes in v6:
time: 476 us; the launch traced here: 468 us
  waiting for transfers between devices  135 us (28%)
  other arithmetic  134 us (28%)
  starting transfers between devices  78.7 us (17%)
  local copies, waits for them, and re-layouts  55.8 us (12%)
  matrix products  46.1 us (10%)
  between operations  17.9 us (4%)
    another operation x14, other arithmetic, shards(): factor11 = jnp.linalg.cholesky(safe_block)  78.8 us
    all_gather x1, waiting for transfers between devices, shards(): factor_col0 = lax.all_gather(held_l, 'row', axis=0, tiled=True)  52.5 us
    all_to_all x1, waiting for transfers between devices, shards(): lax.all_to_all(outgoing.reshape(devices, capacity, strip_r, strip_c), ('r...  47.5 us
    another operation x4, other arithmetic, shards(): lax.linalg.triangular_solve(factor_col0, panel_cols, left_side=False, low...  42.9 us
    ppermute x7, starting transfers between devices, shards(): shifted.append(lax.ppermute(my_piece, ('row', 'col'), perm))  24.7 us
    ppermute x7, waiting for transfers between devices, shards(): shifted.append(lax.ppermute(my_piece, ('row', 'col'), perm))  20.7 us
    unnamed x42, local copies, waits for them, and re-layouts  18.9 us
    dot_general x1, matrix products, shards(): lax.dot_general(panel_here, column_panel, (((1,), (1,)), ((), ())), preci...  16.6 us
  transfers between devices with their start and end apart: 34, of which 7 were waited for; matrix products, arithmetic and copies ran while one was open for 5% of the time, Pallas kernels for 0%

profile of v6, /device:TPU:1, one launch (start us, length us, event | category | flops | bytes accessed | tf_op | source)
XLA Modules:
  0.0 468.2 jit_solution(14319835556473575670)
XLA Ops:
  10.6 11.5 %all-to-all-start = ((s32[128,1,2]{2,1,0:T(1,128)}), s32[128,1,2]{2,1,0:T(1,128)S(1)}, u32[]{:S(2)}, u32[]{:S(2)}) async-start(s32[128,1,2]{2,1,0:T(1,128)} %bitcast.3), calls=%async_computation | async-start | bytes 131072 | tf_op jit(solution)/shard_map/all_to_all | solution.py:44
  22.8 4.5 copy.77
  31.1 4.4 copy.45
  35.5 10.2 %all-to-all-start.1 = ((f32[128,2,32,128]{3,2,1,0:T(8,128)}), f32[128,2,32,128]{3,2,1,0:T(8,128)}, u32[]{:S(2)}, u32[]{:S(2)}) async-start(f32[128,2,32,128]{3,2,1,0:T(8,128)} %copy.45), calls=%async_computation.1 | async-start | bytes 8388608 | tf_op jit(solution)/shard_map/all_to_all | solution.py:37
  50.7 47.5 %all-to-all-done.1 = f32[128,2,32,128]{3,2,1,0:T(8,128)} async-done(((f32[128,2,32,128]{3,2,1,0:T(8,128)}), f32[128,2,32,128]{3,2,1,0:T(8,128)}, u32[]{:S(2)}, u32[]{:S(2)}) %all-to-all-start.1) | async-done | bytes 4194336 | tf_op jit(solution)/shard_map/all_to_all | solution.py:37
  98.3 8.0 %copy.75 = f32[32,8,32,128]{3,1,2,0:T(8,128)} copy(f32[32,8,32,128]{3,2,1,0:T(8,128)} %bitcast.50) | data formatting | bytes 8388608
  106.3 5.7 %copy.46 = f32[4096,256]{1,0:T(8,128)} copy(f32[4096,256]{0,1:T(8,128)} %bitcast.147) | data formatting | bytes 8388608 | tf_op jit(solution)/shard_map/dot_general | solution.py:88
  111.9 4.7 convolution_bitcast_fusion
  118.1 2.2 copy.49
  120.3 2.6 add.183
  129.6 11.7 %cholesky.104 = f32[128,128]{1,0:T(8,128)S(1)} custom-call(f32[128,128]{1,0:T(8,128)S(1)} %cholesky.266), custom_call_target="Cholesky" | custom-call | tf_op jit(solution)/shard_map/jit(cholesky)/cholesky | solution.py:78
  141.3 9.8 %custom-call.30 = f32[1,128,128]{1,2,0:T(8,128)S(1)} custom-call(f32[1,128,128]{2,1,0:T(8,128)S(1)} %get-tuple-element.53), custom_call_target="InvertDiagBlocksLowerTriangular" | custom-call | tf_op jit(solution)/shard_map/jit(cholesky)/cholesky | solution.py:78
  153.8 11.7 %cholesky.217 = f32[128,128]{1,0:T(8,128)S(1)} custom-call(f32[128,128]{1,0:T(8,128)S(1)} %cholesky.270), custom_call_target="Cholesky" | custom-call | tf_op jit(solution)/shard_map/jit(cholesky)/cholesky | solution.py:78
  165.5 9.9 %custom-call.31 = f32[1,128,128]{1,2,0:T(8,128)S(1)} custom-call(f32[1,128,128]{2,1,0:T(8,128)S(1)} %get-tuple-element.50), custom_call_target="InvertDiagBlocksLowerTriangular" | custom-call | tf_op jit(solution)/shard_map/jit(cholesky)/cholesky | solution.py:78
  177.0 11.7 %cholesky.238 = f32[128,128]{1,0:T(8,128)S(1)} custom-call(f32[128,128]{1,0:T(8,128)S(1)} %cholesky.275), custom_call_target="Cholesky" | custom-call | tf_op jit(solution)/shard_map/jit(cholesky)/cholesky | solution.py:78
  189.5 9.8 %custom-call.32 = f32[1,128,128]{1,2,0:T(8,128)S(1)} custom-call(f32[1,128,128]{2,1,0:T(8,128)S(1)} %get-tuple-element.47), custom_call_target="InvertDiagBlocksLowerTriangular" | custom-call | tf_op jit(solution)/shard_map/jit(cholesky)/cholesky | solution.py:78
  200.7 11.9 %cholesky.255 = f32[128,128]{1,0:T(8,128)S(1)} custom-call(f32[128,128]{1,0:T(8,128)S(1)} %convolution_subtract_fusion.4), custom_call_target="Cholesky" | custom-call | tf_op jit(solution)/shard_map/jit(cholesky)/cholesky | solution.py:78
  227.8 52.5 %all-gather.3.cloned.1.call-done = f32[512,512]{1,0:T(8,128)} async-done(((f32[32,512]{1,0:T(8,128)}), f32[512,512]{1,0:T(8,128)}) %all-gather.3.cloned.1.call-update) | async-done | bytes 1048592 | tf_op jit(solution)/shard_map/all_gather | solution.py:85
  281.7 10.6 %while.1 = (s32[]{:T(128)}, f32[512,512]{1,0:T(8,128)S(1)}, s32[4,2]{0,1:T(2,128)S(1)}, f32[4,128,128]{2,1,0:T(8,128)}, s32[]{:T(128)}) while((s32[]{:T(128)}, f32[512,512]{1,0:T(8,128)S(1)}, s32[4,2]{0,1:T(2,128)S(1)}, f32[4,128,128]{2,1,0:T(8,128)}, s32[]{:T(128)}) %tuple.52), condition=%wide.while_cond, body=%wide.while_body.sunk | while | flops 2 | bytes 132205 | solution.py:98
  293.3 40.1 %custom-call.33 = f32[4,128,128]{1,2,0:T(8,128)S(1)} custom-call(f32[4,128,128]{2,1,0:T(8,128)} %get-tuple-element.9), custom_call_target="InvertDiagBlocksLowerTriangular" | custom-call | tf_op jit(solution)/shard_map/triangular_solve | solution.py:98
  341.2 2.9 fusion.7
  345.4 2.2 fusion.43
  362.3 13.2 %collective-permute-start.29 = (f32[128,512]{1,0:T(8,128)S(1)}, f32[128,512]{1,0:T(8,128)S(1)}, u32[]{:S(2)}, u32[]{:S(2)}) collective-permute-start(f32[128,512]{1,0:T(8,128)S(1)} %get-tuple-element.19), channel_id=1, source_target_pairs={{0,0},{1,8},{2,16},{3,24},{4,32},{5,40},{6,48},{7,56},{8,64},{9,72... | collective-permute-start | bytes 786440 | tf_op jit(solution)/shard_map/ppermute | solution.py:116
  375.5 5.0 %collective-permute-done.29 = f32[128,512]{1,0:T(8,128)S(1)} collective-permute-done((f32[128,512]{1,0:T(8,128)S(1)}, f32[128,512]{1,0:T(8,128)S(1)}, u32[]{:S(2)}, u32[]{:S(2)}) %collective-permute-start.29) | collective-permute-done | bytes 262176 | tf_op jit(solution)/shard_map/ppermute | solution.py:116
  381.3 18.7 %collective-permute-start.23 = (f32[128,512]{1,0:T(8,128)S(1)}, f32[128,512]{1,0:T(8,128)S(1)}, u32[]{:S(2)}, u32[]{:S(2)}) collective-permute-start(f32[128,512]{1,0:T(8,128)S(1)} %get-tuple-element.19), channel_id=1, source_target_pairs={{0,6},{1,7},{2,0},{3,1},{4,2},{5,3},{6,4},{7,5},{8,14},{9,15},{10,... | collective-permute-start | bytes 786440 | tf_op jit(solution)/shard_map/ppermute | solution.py:125
  400.0 7.5 %fusion.19 = f32[32,16,32,128]{3,1,2,0:T(8,128)} fusion(f32[32,128,256,1]{2,1,0,3:T(8,128)} %bitcast.145, s32[32,16]{1,0:T(8,128)S(1)} %multiply_add_fusion, s32[256]{0:T(256)S(1)} %eq.127), kind=kOutput, calls=%fused_computation.39 | convolution fusion | flops 6442582016 | bytes 12585984 | tf_op jit(solution)/shard_map/dot_general | solution.py:88
  409.5 2.6 collective-permute-start.24
  413.5 12.4 %collective-permute-done.24 = f32[128,512]{1,0:T(8,128)S(1)} collective-permute-done((f32[128,512]{1,0:T(8,128)S(1)}, f32[128,512]{1,0:T(8,128)S(1)}, u32[]{:S(2)}, u32[]{:S(2)}) %collective-permute-start.24) | collective-permute-done | bytes 262176 | tf_op jit(solution)/shard_map/ppermute | solution.py:125
  425.9 5.7 %collective-permute-done.25 = f32[128,512]{1,0:T(8,128)S(1)} collective-permute-done((f32[128,512]{1,0:T(8,128)S(1)}, f32[128,512]{1,0:T(8,128)S(1)}, u32[]{:S(2)}, u32[]{:S(2)}) %collective-permute-start.25) | collective-permute-done | bytes 262176 | tf_op jit(solution)/shard_map/ppermute | solution.py:125
  431.6 2.6 collective-permute-done.26
  434.8 9.5 %all-gather.5.cloned.1.call-done = f32[2048,512]{1,0:T(8,128)} async-done(((f32[128,512]{1,0:T(8,128)}), f32[2048,512]{1,0:T(8,128)}) %all-gather.5.cloned.1.call-update) | async-done | bytes 4194320 | tf_op jit(solution)/shard_map/all_gather | solution.py:117
  444.3 16.6 %fusion = f32[1024,2048]{1,0:T(8,128)} fusion(f32[1024,2048]{1,0:T(8,128)} %param.4, f32[128,8,16,128]{3,2,1,0:T(8,128)} %bitcast.146, pred[2048]{0:T(1024)(128)(4,1)S(1)} %add_compare_fusion, pred[1024]{0:T(1024)(128)(4,1)S(1)} %add_compare_fusion.1, f32[1024,512]{1,0:T(8,128)S(1)} %bitcast.148, f32[2048,512]{1,0:T(8,128)} %all-gather.5.cloned.1.call-done), kind=kOutput, calls=%fused_computation.4 | convolution fusion | flops 6450839552 | bytes 31460352 | tf_op jit(solution)/shard_map/dot_general | solution.py:129
  (173 shorter events, 80.8 us)
Async XLA Ops:
  10.6 24.9 %all-to-all-start = ((s32[128,1,2]{2,1,0:T(1,128)}), s32[128,1,2]{2,1,0:T(1,128)S(1)}, u32[]{:S(2)}, u32[]{:S(2)}) async-start(s32[128,1,2]{2,1,0:T(1,128)} %bitcast.3), calls=%async_computation | async-start | bytes 131072 | tf_op jit(solution)/shard_map/all_to_all | solution.py:44
  35.5 62.7 %all-to-all-start.1 = ((f32[128,2,32,128]{3,2,1,0:T(8,128)}), f32[128,2,32,128]{3,2,1,0:T(8,128)}, u32[]{:S(2)}, u32[]{:S(2)}) async-start(f32[128,2,32,128]{3,2,1,0:T(8,128)} %copy.45), calls=%async_computation.1 | async-start | bytes 8388608 | tf_op jit(solution)/shard_map/all_to_all | solution.py:37
  45.8 234.5 %all-gather.3.cloned.1.call-start = ((), (), s32[]{:S(2)}) async-start(), calls=%async_computation.2 | async-start | bytes 1114112 | tf_op jit(solution)/shard_map/all_gather | solution.py:85
  216.8 3.4 collective-permute-start
  217.4 3.4 collective-permute-start.14
  218.1 3.4 collective-permute-start.13
  218.8 3.4 collective-permute-start.12
  219.4 3.4 collective-permute-start.11
  220.1 3.4 collective-permute-start.10
  220.8 3.4 collective-permute-start.9
  221.5 3.4 collective-permute-start.8
  222.2 3.4 collective-permute-start.7
  222.9 3.4 collective-permute-start.6
  223.5 3.4 collective-permute-start.5
  224.2 2.7 collective-permute-start.4
  224.9 2.1 collective-permute-start.3
  225.6 1.4 collective-permute-start.2
  227.7 216.6 %all-gather.5.cloned.1.call-start = ((), (), s32[]{:S(2)}) async-start(), calls=%async_computation.3 | async-start | bytes 4456448 | tf_op jit(solution)/shard_map/all_gather | solution.py:117
  350.8 6.1 %collective-permute-start.21 = (f32[128,512]{1,0:T(8,128)S(1)}, f32[128,512]{1,0:T(8,128)S(1)}, u32[]{:S(2)}, u32[]{:S(2)}) collective-permute-start(f32[128,512]{1,0:T(8,128)S(1)} %get-tuple-element.22), channel_id=1, source_target_pairs={{0,1},{8,9},{16,17},{24,25},{32,33},{40,41},{48,49},{56,57},{64,65... | collective-permute-start | bytes 786440 | tf_op jit(solution)/shard_map/ppermute | solution.py:107
  352.1 6.2 %collective-permute-start.20 = (f32[128,512]{1,0:T(8,128)S(1)}, f32[128,512]{1,0:T(8,128)S(1)}, u32[]{:S(2)}, u32[]{:S(2)}) collective-permute-start(f32[128,512]{1,0:T(8,128)S(1)} %get-tuple-element.23), channel_id=1, source_target_pairs={{0,2},{8,10},{16,18},{24,26},{32,34},{40,42},{48,50},{56,58},{64,6... | collective-permute-start | bytes 786440 | tf_op jit(solution)/shard_map/ppermute | solution.py:107
  352.8 7.5 %collective-permute-start.19 = (f32[128,512]{1,0:T(8,128)S(1)}, f32[128,512]{1,0:T(8,128)}, u32[]{:S(2)}, u32[]{:S(2)}) collective-permute-start(f32[128,512]{1,0:T(8,128)S(1)} %get-tuple-element.24), channel_id=1, source_target_pairs={{0,3},{8,11},{16,19},{24,27},{32,35},{40,43},{48,51},{56,59},{64,6... | collective-permute-start | bytes 786440 | tf_op jit(solution)/shard_map/ppermute | solution.py:107
  354.1 6.2 %collective-permute-start.18 = (f32[128,512]{1,0:T(8,128)S(1)}, f32[128,512]{1,0:T(8,128)}, u32[]{:S(2)}, u32[]{:S(2)}) collective-permute-start(f32[128,512]{1,0:T(8,128)S(1)} %get-tuple-element.25), channel_id=1, source_target_pairs={{0,4},{8,12},{16,20},{24,28},{32,36},{40,44},{48,52},{56,60},{64,6... | collective-permute-start | bytes 786440 | tf_op jit(solution)/shard_map/ppermute | solution.py:107
  355.5 4.8 %collective-permute-start.17 = (f32[128,512]{1,0:T(8,128)S(1)}, f32[128,512]{1,0:T(8,128)}, u32[]{:S(2)}, u32[]{:S(2)}) collective-permute-start(f32[128,512]{1,0:T(8,128)S(1)} %get-tuple-element.26), channel_id=1, source_target_pairs={{0,5},{8,13},{16,21},{24,29},{32,37},{40,45},{48,53},{56,61},{64,6... | collective-permute-start | bytes 786440 | tf_op jit(solution)/shard_map/ppermute | solution.py:107
  356.9 3.4 collective-permute-start.16
  362.3 18.2 %collective-permute-start.29 = (f32[128,512]{1,0:T(8,128)S(1)}, f32[128,512]{1,0:T(8,128)S(1)}, u32[]{:S(2)}, u32[]{:S(2)}) collective-permute-start(f32[128,512]{1,0:T(8,128)S(1)} %get-tuple-element.19), channel_id=1, source_target_pairs={{0,0},{1,8},{2,16},{3,24},{4,32},{5,40},{6,48},{7,56},{8,64},{9,72... | collective-permute-start | bytes 786440 | tf_op jit(solution)/shard_map/ppermute | solution.py:116
  381.3 30.9 %collective-permute-start.23 = (f32[128,512]{1,0:T(8,128)S(1)}, f32[128,512]{1,0:T(8,128)S(1)}, u32[]{:S(2)}, u32[]{:S(2)}) collective-permute-start(f32[128,512]{1,0:T(8,128)S(1)} %get-tuple-element.19), channel_id=1, source_target_pairs={{0,6},{1,7},{2,0},{3,1},{4,2},{5,3},{6,4},{7,5},{8,14},{9,15},{10,... | collective-permute-start | bytes 786440 | tf_op jit(solution)/shard_map/ppermute | solution.py:125
  400.0 9.5 %collective-permute-start.22 = (f32[128,512]{1,0:T(8,128)S(1)}, f32[128,512]{1,0:T(8,128)S(1)}, u32[]{:S(2)}, u32[]{:S(2)}) collective-permute-start(f32[128,512]{1,0:T(8,128)S(1)} %get-tuple-element.19), channel_id=1, source_target_pairs={{0,7},{1,0},{2,1},{3,2},{4,3},{5,4},{6,5},{7,6},{8,15},{9,8},{10,9... | collective-permute-start | bytes 786440 | tf_op jit(solution)/shard_map/ppermute | solution.py:125
  407.5 26.9 %collective-permute-start.28 = (f32[128,512]{1,0:T(8,128)S(1)}, f32[128,512]{1,0:T(8,128)S(1)}, u32[]{:S(2)}, u32[]{:S(2)}) collective-permute-start(f32[128,512]{1,0:T(8,128)S(1)} %get-tuple-element.19), channel_id=1, source_target_pairs={{0,1},{1,2},{2,3},{3,4},{4,5},{5,6},{6,7},{7,0},{8,9},{9,10},{10,1... | collective-permute-start | bytes 786440 | tf_op jit(solution)/shard_map/ppermute | solution.py:125
  409.2 25.1 %collective-permute-start.27 = (f32[128,512]{1,0:T(8,128)S(1)}, f32[128,512]{1,0:T(8,128)S(1)}, u32[]{:S(2)}, u32[]{:S(2)}) collective-permute-start(f32[128,512]{1,0:T(8,128)S(1)} %get-tuple-element.19), channel_id=1, source_target_pairs={{0,2},{1,3},{2,4},{3,5},{4,6},{5,7},{6,0},{7,1},{8,10},{9,11},{10,... | collective-permute-start | bytes 786440 | tf_op jit(solution)/shard_map/ppermute | solution.py:125
  409.2 25.1 %collective-permute-start.26 = (f32[128,512]{1,0:T(8,128)S(1)}, f32[128,512]{1,0:T(8,128)S(1)}, u32[]{:S(2)}, u32[]{:S(2)}) collective-permute-start(f32[128,512]{1,0:T(8,128)S(1)} %get-tuple-element.19), channel_id=1, source_target_pairs={{0,3},{1,4},{2,5},{3,6},{4,7},{5,0},{6,1},{7,2},{8,11},{9,12},{10,... | collective-permute-start | bytes 786440 | tf_op jit(solution)/shard_map/ppermute | solution.py:125
  409.5 16.4 %collective-permute-start.24 = (f32[128,512]{1,0:T(8,128)S(1)}, f32[128,512]{1,0:T(8,128)S(1)}, u32[]{:S(2)}, u32[]{:S(2)}) collective-permute-start(f32[128,512]{1,0:T(8,128)S(1)} %get-tuple-element.19), channel_id=1, source_target_pairs={{0,5},{1,6},{2,7},{3,0},{4,1},{5,2},{6,3},{7,4},{8,13},{9,14},{10,... | collective-permute-start | bytes 786440 | tf_op jit(solution)/shard_map/ppermute | solution.py:125
  412.2 19.4 %collective-permute-start.25 = (f32[128,512]{1,0:T(8,128)S(1)}, f32[128,512]{1,0:T(8,128)S(1)}, u32[]{:S(2)}, u32[]{:S(2)}) collective-permute-start(f32[128,512]{1,0:T(8,128)S(1)} %get-tuple-element.19), channel_id=1, source_target_pairs={{0,4},{1,5},{2,6},{3,7},{4,0},{5,1},{6,2},{7,3},{8,12},{9,13},{10,... | collective-permute-start | bytes 786440 | tf_op jit(solution)/shard_map/ppermute | solution.py:125
  (15 other events, 83.9 us)
Sparse Core Ops, SparseCore 0:
  227.9 52.4 all-gather.2
  381.3 62.9 all-gather.4

commit v7 on v6

--- a/solution.py
+++ b/solution.py
@@ -24,33 +24,28 @@
     earlier = positions[:, None] > positions[None, :]
     rank = jnp.sum((same_owner & earlier).astype(jnp.int32), axis=1)
     target = owner * capacity + rank
+    flat = strip_r * strip_c
+    code = jnp.broadcast_to((child_slot + 1).astype(jnp.float32)[:, None], (held, strip_c))
+    payload = jnp.concatenate([child_strips.reshape(held, flat), code], axis=1)
+    width = payload.shape[1]
     route = (target[None, :] == jnp.arange(devices * capacity, dtype=jnp.int32)[:, None]).astype(jnp.float32)
     outgoing = lax.dot_general(
         route,
-        child_strips.reshape(held, strip_r * strip_c),
+        payload,
         (((1,), (0,)), ((), ())),
         precision=lax.Precision.HIGHEST,
         preferred_element_type=jnp.float32,
     )
-    places = jnp.full((devices * capacity,), local_count, jnp.int32).at[target].set(child_slot)
-    arrived, landing = (
-        lax.all_to_all(
-            outgoing.reshape(devices, capacity, strip_r, strip_c),
-            ("row", "col"),
-            split_axis=0,
-            concat_axis=0,
-            tiled=True,
-        ),
-        lax.all_to_all(
-            places.reshape(devices, capacity),
-            ("row", "col"),
-            split_axis=0,
-            concat_axis=0,
-            tiled=True,
-        ),
-    )
-    arrived = arrived.reshape(devices * capacity, strip_r, strip_c)
-    landing = landing.reshape(devices * capacity)
+    got_all = lax.all_to_all(
+        outgoing.reshape(devices, capacity * width),
+        ("row", "col"),
+        split_axis=0,
+        concat_axis=0,
+        tiled=True,
+    ).reshape(devices * capacity, width)
+    arrived = got_all[:, :flat]
+    number = jnp.round(got_all[:, flat]).astype(jnp.int32)
+    landing = jnp.where(number > 0, number - 1, local_count)
     row_id = lax.axis_index("row")
     col_id = lax.axis_index("col")
     first_rows = row_id == 0
@@ -64,7 +59,7 @@
     pick = (spot[None, :] == jnp.arange(strips_down * across, dtype=jnp.int32)[:, None]).astype(jnp.float32)
     part = lax.dot_general(
         pick,
-        arrived.reshape(arrived.shape[0], strip_r * strip_c),
+        arrived,
         (((1,), (0,)), ((), ())),
         precision=lax.Precision.HIGHEST,
         preferred_element_type=jnp.float32,
@@ -87,7 +82,7 @@
     every = (landing[None, :] == jnp.arange(local_count, dtype=jnp.int32)[:, None]).astype(jnp.float32)
     delta = lax.dot_general(
         every,
-        arrived.reshape(arrived.shape[0], strip_r * strip_c),
+        arrived,
         (((1,), (0,)), ((), ())),
         precision=lax.Precision.HIGHEST,
         preferred_element_type=jnp.float32,

time: 476 us -> 475 us (level)
  other arithmetic: 134 us -> 149 us
  starting transfers between devices: 78.7 us -> 69.4 us
  waiting for transfers between devices: 135 us -> 128 us
    all_to_all x1, other arithmetic: 0.83 us -> 14 us  [shards(): lax.all_to_all(outgoing.reshape(devices, capacity * width), ('row', 'col'...]
    dot_general x3 -> x0, local copies, waits for them, and re-layouts: 12 us -> none  [the longest x2 6.35 us: shards(): lax.dot_general(route, child_strips.reshape(held, strip_r * strip_c), (((...]
    transpose x1 -> x2, local copies, waits for them, and re-layouts: 1.35 us -> 12.5 us  [shards(): delta.reshape(strips_down, strips_across, strip_r, strip_c)]
    all_to_all x2 -> x1, starting transfers between devices: 21.7 us -> 11.9 us  [shards(): lax.all_to_all(outgoing.reshape(devices, capacity * width), ('row', 'col'...]
    all_gather x1, waiting for transfers between devices: 9.47 us -> 0.02 us  [shards(): column_panel = lax.all_gather(mine, 'row', axis=0, tiled=True)]
    unnamed x42 -> x43, local copies, waits for them, and re-layouts: 18.9 us -> 11.9 us
    reshape x0 -> x2, local copies, waits for them, and re-layouts: none -> 6.8 us  [the longest x1 5.01 us: shards(): got_all = lax.all_to_all(outgoing.reshape(devices, capacity * width), ('r...]
    all_to_all x2 -> x1, local copies, waits for them, and re-layouts: 1.33 us -> 7.19 us  [shards(): lax.all_to_all(outgoing.reshape(devices, capacity * width), ('row', 'col'...]
  transfers between devices with their start and end apart: 34 -> 33, of which waited for: 7 -> 6; matrix products, arithmetic and copies ran while one was open for 5% -> 5% of each run, Pallas kernels for 0% -> 0%
where the time goes in v7:
time: 475 us; the launch traced here: 469 us
  other arithmetic  149 us (31%)
  waiting for transfers between devices  128 us (27%)
  starting transfers between devices  69.4 us (15%)
  local copies, waits for them, and re-layouts  59 us (12%)
  matrix products  46.4 us (10%)
  between operations  17.8 us (4%)
    another operation x14, other arithmetic, shards(): factor11 = jnp.linalg.cholesky(safe_block)  79.1 us
    all_gather x1, waiting for transfers between devices, shards(): factor_col0 = lax.all_gather(held_l, 'row', axis=0, tiled=True)  52.1 us
    all_to_all x1, waiting for transfers between devices, shards(): lax.all_to_all(outgoing.reshape(devices, capacity * width), ('row', 'col'...  50.5 us
    another operation x4, other arithmetic, shards(): lax.linalg.triangular_solve(factor_col0, panel_cols, left_side=False, low...  42.9 us
    ppermute x7, starting transfers between devices, shards(): shifted.append(lax.ppermute(my_piece, ('row', 'col'), perm))  25 us
    ppermute x7, waiting for transfers between devices, shards(): shifted.append(lax.ppermute(my_piece, ('row', 'col'), perm))  20.1 us
    dot_general x1, matrix products, shards(): lax.dot_general(panel_here, column_panel, (((1,), (1,)), ((), ())), preci...  17.3 us
    all_to_all x1, other arithmetic, shards(): lax.all_to_all(outgoing.reshape(devices, capacity * width), ('row', 'col'...  14 us
  transfers between devices with their start and end apart: 33, of which 6 were waited for; matrix products, arithmetic and copies ran while one was open for 5% of the time, Pallas kernels for 0%

profile of v7, /device:TPU:1, one launch (start us, length us, event | category | flops | bytes accessed | tf_op | source)
XLA Modules:
  0.0 469.3 jit_solution(14749855890979780053)
XLA Ops:
  9.4 3.2 copy.80
  12.7 3.9 fusion.8
  16.6 7.2 %all_to_all.8 = f32[128,1,8448]{2,1,0:T(1,128)} reshape(f32[256,4224]{1,0:T(8,128)} %fusion.8) | data formatting | bytes 8650752 | tf_op jit(solution)/shard_map/all_to_all | solution.py:39
  23.8 11.9 %all-to-all-start = ((f32[128,1,8448]{2,1,0:T(1,128)}), f32[128,1,8448]{2,1,0:T(1,128)}, u32[]{:S(2)}, u32[]{:S(2)}) async-start(f32[128,1,8448]{2,1,0:T(1,128)} %all_to_all.8), calls=%async_computation | async-start | bytes 8650752 | tf_op jit(solution)/shard_map/all_to_all | solution.py:39
  39.1 50.5 %all-to-all-done = f32[128,1,8448]{2,1,0:T(1,128)} async-done(((f32[128,1,8448]{2,1,0:T(1,128)}), f32[128,1,8448]{2,1,0:T(1,128)}, u32[]{:S(2)}, u32[]{:S(2)}) %all-to-all-start) | async-done | bytes 4325408 | tf_op jit(solution)/shard_map/all_to_all | solution.py:39
  89.7 14.0 %reduce.24 = f32[128,8448]{1,0:T(8,128)} reduce(f32[128,1,8448]{2,1,0:T(1,128)} %all-to-all-done, f32[]{:T(128)} %constant.238), dimensions={1}, to_apply=%all_to_all.7.reduce_sub_computation | reduce | bytes 8650756 | tf_op jit(solution)/shard_map/all_to_all | solution.py:39
  103.7 5.0 %reshape.173 = f32[256,4224]{1,0:T(8,128)} reshape(f32[128,8448]{1,0:T(8,128)} %reduce.24) | data formatting | bytes 8650752 | tf_op jit(solution)/shard_map/reshape | solution.py:45
  109.7 3.9 fusion.12
  118.0 2.6 add.175
  127.2 11.7 %cholesky.104 = f32[128,128]{1,0:T(8,128)S(1)} custom-call(f32[128,128]{1,0:T(8,128)S(1)} %cholesky.266), custom_call_target="Cholesky" | custom-call | tf_op jit(solution)/shard_map/jit(cholesky)/cholesky | solution.py:73
  138.9 9.8 %custom-call.30 = f32[1,128,128]{1,2,0:T(8,128)S(1)} custom-call(f32[1,128,128]{2,1,0:T(8,128)S(1)} %get-tuple-element.53), custom_call_target="InvertDiagBlocksLowerTriangular" | custom-call | tf_op jit(solution)/shard_map/jit(cholesky)/cholesky | solution.py:73
  151.4 11.7 %cholesky.217 = f32[128,128]{1,0:T(8,128)S(1)} custom-call(f32[128,128]{1,0:T(8,128)S(1)} %cholesky.270), custom_call_target="Cholesky" | custom-call | tf_op jit(solution)/shard_map/jit(cholesky)/cholesky | solution.py:73
  163.1 10.0 %custom-call.31 = f32[1,128,128]{1,2,0:T(8,128)S(1)} custom-call(f32[1,128,128]{2,1,0:T(8,128)S(1)} %get-tuple-element.50), custom_call_target="InvertDiagBlocksLowerTriangular" | custom-call | tf_op jit(solution)/shard_map/jit(cholesky)/cholesky | solution.py:73
  174.7 11.7 %cholesky.238 = f32[128,128]{1,0:T(8,128)S(1)} custom-call(f32[128,128]{1,0:T(8,128)S(1)} %cholesky.275), custom_call_target="Cholesky" | custom-call | tf_op jit(solution)/shard_map/jit(cholesky)/cholesky | solution.py:73
  187.2 9.8 %custom-call.32 = f32[1,128,128]{1,2,0:T(8,128)S(1)} custom-call(f32[1,128,128]{2,1,0:T(8,128)S(1)} %get-tuple-element.47), custom_call_target="InvertDiagBlocksLowerTriangular" | custom-call | tf_op jit(solution)/shard_map/jit(cholesky)/cholesky | solution.py:73
  198.4 12.2 %cholesky.255 = f32[128,128]{1,0:T(8,128)S(1)} custom-call(f32[128,128]{1,0:T(8,128)S(1)} %convolution_subtract_fusion.4), custom_call_target="Cholesky" | custom-call | tf_op jit(solution)/shard_map/jit(cholesky)/cholesky | solution.py:73
  225.9 52.1 %all-gather.3.cloned.1.call-done = f32[512,512]{1,0:T(8,128)} async-done(((f32[32,512]{1,0:T(8,128)}), f32[512,512]{1,0:T(8,128)}) %all-gather.3.cloned.1.call-update) | async-done | bytes 1048592 | tf_op jit(solution)/shard_map/all_gather | solution.py:80
  279.3 10.9 %while.1 = (s32[]{:T(128)}, f32[512,512]{1,0:T(8,128)S(1)}, s32[4,2]{0,1:T(2,128)S(1)}, f32[4,128,128]{2,1,0:T(8,128)}, s32[]{:T(128)}) while((s32[]{:T(128)}, f32[512,512]{1,0:T(8,128)S(1)}, s32[4,2]{0,1:T(2,128)S(1)}, f32[4,128,128]{2,1,0:T(8,128)}, s32[]{:T(128)}) %tuple.52), condition=%wide.while_cond, body=%wide.while_body.sunk | while | flops 2 | bytes 132205 | solution.py:93
  280.0 2.1 bitcast_dynamic-update-slice_fusion.18
  291.2 40.1 %custom-call.33 = f32[4,128,128]{1,2,0:T(8,128)S(1)} custom-call(f32[4,128,128]{2,1,0:T(8,128)} %get-tuple-element.9), custom_call_target="InvertDiagBlocksLowerTriangular" | custom-call | tf_op jit(solution)/shard_map/triangular_solve | solution.py:93
  339.1 2.9 fusion.21
  343.3 2.2 fusion.49
  360.2 13.1 %collective-permute-start.29 = (f32[128,512]{1,0:T(8,128)S(1)}, f32[128,512]{1,0:T(8,128)S(1)}, u32[]{:S(2)}, u32[]{:S(2)}) collective-permute-start(f32[128,512]{1,0:T(8,128)S(1)} %get-tuple-element.19), channel_id=1, source_target_pairs={{0,0},{1,8},{2,16},{3,24},{4,32},{5,40},{6,48},{7,56},{8,64},{9,72... | collective-permute-start | bytes 786440 | tf_op jit(solution)/shard_map/ppermute | solution.py:111
  373.3 5.0 %collective-permute-done.29 = f32[128,512]{1,0:T(8,128)S(1)} collective-permute-done((f32[128,512]{1,0:T(8,128)S(1)}, f32[128,512]{1,0:T(8,128)S(1)}, u32[]{:S(2)}, u32[]{:S(2)}) %collective-permute-start.29) | collective-permute-done | bytes 262176 | tf_op jit(solution)/shard_map/ppermute | solution.py:111
  379.2 5.7 %fusion.5 = f32[64,8,32,128]{3,1,2,0:T(8,128)S(1)} fusion(f32[256,4224]{1,0:T(8,128)} %reshape.173, s32[256]{0:T(256)S(1)} %select_reduce_fusion), kind=kOutput, calls=%fused_computation.9 | convolution fusion | flops 6442582016 | bytes 12583936 | tf_op jit(solution)/shard_map/dot_general | solution.py:83
  386.7 18.8 %collective-permute-start.23 = (f32[128,512]{1,0:T(8,128)S(1)}, f32[128,512]{1,0:T(8,128)S(1)}, u32[]{:S(2)}, u32[]{:S(2)}) collective-permute-start(f32[128,512]{1,0:T(8,128)S(1)} %get-tuple-element.19), channel_id=1, source_target_pairs={{0,6},{1,7},{2,0},{3,1},{4,2},{5,3},{6,4},{7,5},{8,14},{9,15},{10,... | collective-permute-start | bytes 786440 | tf_op jit(solution)/shard_map/ppermute | solution.py:120
  407.1 10.9 %copy.53 = f32[32,32,16,128]{3,2,1,0:T(8,128)} copy(f32[32,32,16,128]{3,1,2,0:T(8,128)S(1)} %bitcast_bitcast_fusion) | data formatting | bytes 16777216 | tf_op jit(solution)/shard_map/transpose | solution.py:90
  419.9 2.8 collective-permute-start.24
  424.2 12.2 %collective-permute-done.24 = f32[128,512]{1,0:T(8,128)S(1)} collective-permute-done((f32[128,512]{1,0:T(8,128)S(1)}, f32[128,512]{1,0:T(8,128)S(1)}, u32[]{:S(2)}, u32[]{:S(2)}) %collective-permute-start.24) | collective-permute-done | bytes 262176 | tf_op jit(solution)/shard_map/ppermute | solution.py:120
  436.4 5.7 %collective-permute-done.25 = f32[128,512]{1,0:T(8,128)S(1)} collective-permute-done((f32[128,512]{1,0:T(8,128)S(1)}, f32[128,512]{1,0:T(8,128)S(1)}, u32[]{:S(2)}, u32[]{:S(2)}) %collective-permute-start.25) | collective-permute-done | bytes 262176 | tf_op jit(solution)/shard_map/ppermute | solution.py:120
  442.1 2.2 collective-permute-done.26
  444.9 17.3 %fusion = f32[1024,2048]{1,0:T(8,128)} fusion(f32[1024,2048]{1,0:T(8,128)} %param.4, f32[128,8,16,128]{3,2,1,0:T(8,128)} %bitcast.111, pred[2048]{0:T(1024)(128)(4,1)S(1)} %add_compare_fusion, pred[1024]{0:T(1024)(128)(4,1)S(1)} %add_compare_fusion.1, f32[1024,512]{1,0:T(8,128)S(1)} %bitcast.113, f32[2048,512]{1,0:T(8,128)} %all-gather.5.cloned.1.call-done), kind=kOutput, calls=%fused_computation.3 | convolution fusion | flops 6450839552 | bytes 31460352 | tf_op jit(solution)/shard_map/dot_general | solution.py:124
  (168 shorter events, 79.2 us)
Async XLA Ops:
  23.8 65.8 %all-to-all-start = ((f32[128,1,8448]{2,1,0:T(1,128)}), f32[128,1,8448]{2,1,0:T(1,128)}, u32[]{:S(2)}, u32[]{:S(2)}) async-start(f32[128,1,8448]{2,1,0:T(1,128)} %all_to_all.8), calls=%async_computation | async-start | bytes 8650752 | tf_op jit(solution)/shard_map/all_to_all | solution.py:39
  35.7 242.2 %all-gather.3.cloned.1.call-start = ((), (), s32[]{:S(2)}) async-start(), calls=%async_computation.1 | async-start | bytes 1114112 | tf_op jit(solution)/shard_map/all_gather | solution.py:80
  214.8 3.4 collective-permute-start
  215.5 3.4 collective-permute-start.14
  216.1 3.4 collective-permute-start.13
  216.8 3.4 collective-permute-start.12
  217.5 3.4 collective-permute-start.11
  218.2 3.4 collective-permute-start.10
  218.9 3.4 collective-permute-start.9
  219.5 3.4 collective-permute-start.8
  220.2 3.4 collective-permute-start.7
  220.9 3.4 collective-permute-start.6
  221.6 3.4 collective-permute-start.5
  222.3 2.7 collective-permute-start.4
  223.0 2.1 collective-permute-start.3
  223.6 1.4 collective-permute-start.2
  225.8 219.1 %all-gather.5.cloned.1.call-start = ((), (), s32[]{:S(2)}) async-start(), calls=%async_computation.2 | async-start | bytes 4456448 | tf_op jit(solution)/shard_map/all_gather | solution.py:112
  348.7 6.1 %collective-permute-start.21 = (f32[128,512]{1,0:T(8,128)S(1)}, f32[128,512]{1,0:T(8,128)S(1)}, u32[]{:S(2)}, u32[]{:S(2)}) collective-permute-start(f32[128,512]{1,0:T(8,128)S(1)} %get-tuple-element.22), channel_id=1, source_target_pairs={{0,1},{8,9},{16,17},{24,25},{32,33},{40,41},{48,49},{56,57},{64,65... | collective-permute-start | bytes 786440 | tf_op jit(solution)/shard_map/ppermute | solution.py:102
  350.0 6.2 %collective-permute-start.20 = (f32[128,512]{1,0:T(8,128)S(1)}, f32[128,512]{1,0:T(8,128)S(1)}, u32[]{:S(2)}, u32[]{:S(2)}) collective-permute-start(f32[128,512]{1,0:T(8,128)S(1)} %get-tuple-element.23), channel_id=1, source_target_pairs={{0,2},{8,10},{16,18},{24,26},{32,34},{40,42},{48,50},{56,58},{64,6... | collective-permute-start | bytes 786440 | tf_op jit(solution)/shard_map/ppermute | solution.py:102
  350.7 7.6 %collective-permute-start.19 = (f32[128,512]{1,0:T(8,128)S(1)}, f32[128,512]{1,0:T(8,128)}, u32[]{:S(2)}, u32[]{:S(2)}) collective-permute-start(f32[128,512]{1,0:T(8,128)S(1)} %get-tuple-element.24), channel_id=1, source_target_pairs={{0,3},{8,11},{16,19},{24,27},{32,35},{40,43},{48,51},{56,59},{64,6... | collective-permute-start | bytes 786440 | tf_op jit(solution)/shard_map/ppermute | solution.py:102
  352.1 6.2 %collective-permute-start.18 = (f32[128,512]{1,0:T(8,128)S(1)}, f32[128,512]{1,0:T(8,128)}, u32[]{:S(2)}, u32[]{:S(2)}) collective-permute-start(f32[128,512]{1,0:T(8,128)S(1)} %get-tuple-element.25), channel_id=1, source_target_pairs={{0,4},{8,12},{16,20},{24,28},{32,36},{40,44},{48,52},{56,60},{64,6... | collective-permute-start | bytes 786440 | tf_op jit(solution)/shard_map/ppermute | solution.py:102
  353.4 4.9 %collective-permute-start.17 = (f32[128,512]{1,0:T(8,128)S(1)}, f32[128,512]{1,0:T(8,128)}, u32[]{:S(2)}, u32[]{:S(2)}) collective-permute-start(f32[128,512]{1,0:T(8,128)S(1)} %get-tuple-element.26), channel_id=1, source_target_pairs={{0,5},{8,13},{16,21},{24,29},{32,37},{40,45},{48,53},{56,61},{64,6... | collective-permute-start | bytes 786440 | tf_op jit(solution)/shard_map/ppermute | solution.py:102
  354.8 3.5 collective-permute-start.16
  356.9 1.4 collective-permute-start.15
  360.2 18.1 %collective-permute-start.29 = (f32[128,512]{1,0:T(8,128)S(1)}, f32[128,512]{1,0:T(8,128)S(1)}, u32[]{:S(2)}, u32[]{:S(2)}) collective-permute-start(f32[128,512]{1,0:T(8,128)S(1)} %get-tuple-element.19), channel_id=1, source_target_pairs={{0,0},{1,8},{2,16},{3,24},{4,32},{5,40},{6,48},{7,56},{8,64},{9,72... | collective-permute-start | bytes 786440 | tf_op jit(solution)/shard_map/ppermute | solution.py:111
  386.7 36.0 %collective-permute-start.23 = (f32[128,512]{1,0:T(8,128)S(1)}, f32[128,512]{1,0:T(8,128)S(1)}, u32[]{:S(2)}, u32[]{:S(2)}) collective-permute-start(f32[128,512]{1,0:T(8,128)S(1)} %get-tuple-element.19), channel_id=1, source_target_pairs={{0,6},{1,7},{2,0},{3,1},{4,2},{5,3},{6,4},{7,5},{8,14},{9,15},{10,... | collective-permute-start | bytes 786440 | tf_op jit(solution)/shard_map/ppermute | solution.py:120
  405.5 14.4 %collective-permute-start.22 = (f32[128,512]{1,0:T(8,128)S(1)}, f32[128,512]{1,0:T(8,128)S(1)}, u32[]{:S(2)}, u32[]{:S(2)}) collective-permute-start(f32[128,512]{1,0:T(8,128)S(1)} %get-tuple-element.19), channel_id=1, source_target_pairs={{0,7},{1,0},{2,1},{3,2},{4,3},{5,4},{6,5},{7,6},{8,15},{9,8},{10,9... | collective-permute-start | bytes 786440 | tf_op jit(solution)/shard_map/ppermute | solution.py:120
  418.0 26.5 %collective-permute-start.28 = (f32[128,512]{1,0:T(8,128)S(1)}, f32[128,512]{1,0:T(8,128)S(1)}, u32[]{:S(2)}, u32[]{:S(2)}) collective-permute-start(f32[128,512]{1,0:T(8,128)S(1)} %get-tuple-element.19), channel_id=1, source_target_pairs={{0,1},{1,2},{2,3},{3,4},{4,5},{5,6},{6,7},{7,0},{8,9},{9,10},{10,1... | collective-permute-start | bytes 786440 | tf_op jit(solution)/shard_map/ppermute | solution.py:120
  419.7 24.7 %collective-permute-start.27 = (f32[128,512]{1,0:T(8,128)S(1)}, f32[128,512]{1,0:T(8,128)S(1)}, u32[]{:S(2)}, u32[]{:S(2)}) collective-permute-start(f32[128,512]{1,0:T(8,128)S(1)} %get-tuple-element.19), channel_id=1, source_target_pairs={{0,2},{1,3},{2,4},{3,5},{4,6},{5,7},{6,0},{7,1},{8,10},{9,11},{10,... | collective-permute-start | bytes 786440 | tf_op jit(solution)/shard_map/ppermute | solution.py:120
  419.7 24.7 %collective-permute-start.26 = (f32[128,512]{1,0:T(8,128)S(1)}, f32[128,512]{1,0:T(8,128)S(1)}, u32[]{:S(2)}, u32[]{:S(2)}) collective-permute-start(f32[128,512]{1,0:T(8,128)S(1)} %get-tuple-element.19), channel_id=1, source_target_pairs={{0,3},{1,4},{2,5},{3,6},{4,7},{5,0},{6,1},{7,2},{8,11},{9,12},{10,... | collective-permute-start | bytes 786440 | tf_op jit(solution)/shard_map/ppermute | solution.py:120
  419.9 16.5 %collective-permute-start.24 = (f32[128,512]{1,0:T(8,128)S(1)}, f32[128,512]{1,0:T(8,128)S(1)}, u32[]{:S(2)}, u32[]{:S(2)}) collective-permute-start(f32[128,512]{1,0:T(8,128)S(1)} %get-tuple-element.19), channel_id=1, source_target_pairs={{0,5},{1,6},{2,7},{3,0},{4,1},{5,2},{6,3},{7,4},{8,13},{9,14},{10,... | collective-permute-start | bytes 786440 | tf_op jit(solution)/shard_map/ppermute | solution.py:120
  422.7 19.4 %collective-permute-start.25 = (f32[128,512]{1,0:T(8,128)S(1)}, f32[128,512]{1,0:T(8,128)S(1)}, u32[]{:S(2)}, u32[]{:S(2)}) collective-permute-start(f32[128,512]{1,0:T(8,128)S(1)} %get-tuple-element.19), channel_id=1, source_target_pairs={{0,4},{1,5},{2,6},{3,7},{4,0},{5,1},{6,2},{7,3},{8,12},{9,13},{10,... | collective-permute-start | bytes 786440 | tf_op jit(solution)/shard_map/ppermute | solution.py:120
  (14 other events, 58.5 us)
Sparse Core Ops, SparseCore 0:
  225.9 51.9 all-gather.2
  379.2 63.0 all-gather.4

commit v8 on v7

--- a/solution.py
+++ b/solution.py
@@ -72,12 +72,16 @@
     )
     factor11 = jnp.linalg.cholesky(safe_block)
 
-    pieces_l = factor11.reshape(row_count, PANEL // row_count, PANEL)
-    held_l = jnp.where(first_rows, pieces_l[0], 0.0)
-    for r in range(1, row_count):
-        got = lax.ppermute(pieces_l[r], ("row", "col"), [(0, r * col_count)])
-        held_l = held_l + got
-    factor_col0 = lax.all_gather(held_l, "row", axis=0, tiled=True)
+    group = 4 if row_count % 4 == 0 else 1
+    factor_col0 = factor11
+    for m in range(1, row_count // group):
+        got = lax.ppermute(factor11, ("row", "col"), [(0, m * group * col_count)])
+        factor_col0 = jnp.where(row_id == m * group, got, factor_col0)
+    lead = factor_col0
+    for z in range(1, group):
+        perm = [(m * group * col_count, (m * group + z) * col_count) for m in range(row_count // group)]
+        got = lax.ppermute(lead, ("row", "col"), perm)
+        factor_col0 = jnp.where(row_id % group == z, got, factor_col0)
 
     every = (landing[None, :] == jnp.arange(local_count, dtype=jnp.int32)[:, None]).astype(jnp.float32)
     delta = lax.dot_general(

time: 475 us -> 465 us (0.979)
  starting transfers between devices: 69.4 us -> 51 us
  waiting for transfers between devices: 128 us -> 133 us
    all_gather x1 -> x0, waiting for transfers between devices: 52.1 us -> none  [shards(): factor_col0 = lax.all_gather(held_l, 'row', axis=0, tiled=True)]
    ppermute x7, waiting for transfers between devices: 0.02 us -> 38.9 us  [shards(): lax.ppermute(solved[j * piece_rows:(j + 1) * piece_rows], ('row', 'col'),...]
    ppermute x1, waiting for transfers between devices: 5.04 us -> 23.6 us  [shards(): mine = lax.ppermute(my_piece, ('row', 'col'), perm)]
    ppermute x1, starting transfers between devices: 13.1 us -> 3.24 us  [shards(): mine = lax.ppermute(my_piece, ('row', 'col'), perm)]
    ppermute x7, starting transfers between devices: 25 us -> 17.4 us  [shards(): shifted.append(lax.ppermute(my_piece, ('row', 'col'), perm))]
    ppermute x15 -> x6, starting transfers between devices: 9.97 us -> 8.93 us  [the longest x3 4.91 us: shards(): got = lax.ppermute(factor11, ('row', 'col'), [(0, m * group * col_count)])]
    unnamed x43 -> x45, local copies, waits for them, and re-layouts: 11.9 us -> 12.8 us
  transfers between devices with their start and end apart: 33 -> 23, of which waited for: 6 -> 6; matrix products, arithmetic and copies ran while one was open for 5% -> 5% of each run, Pallas kernels for 0% -> 0%
where the time goes in v8:
time: 465 us; the launch traced here: 460 us
  other arithmetic  152 us (33%)
  waiting for transfers between devices  133 us (29%)
  local copies, waits for them, and re-layouts  59.5 us (13%)
  starting transfers between devices  51 us (11%)
  matrix products  46.4 us (10%)
  between operations  17.5 us (4%)
    another operation x14, other arithmetic, shards(): factor11 = jnp.linalg.cholesky(safe_block)  79 us
    all_to_all x1, waiting for transfers between devices, shards(): lax.all_to_all(outgoing.reshape(devices, capacity * width), ('row', 'col'...  50.5 us
    another operation x4, other arithmetic, shards(): lax.linalg.triangular_solve(factor_col0, panel_cols, left_side=False, low...  44.2 us
    ppermute x7, waiting for transfers between devices, shards(): lax.ppermute(solved[j * piece_rows:(j + 1) * piece_rows], ('row', 'col'),...  38.9 us
    ppermute x1, waiting for transfers between devices, shards(): mine = lax.ppermute(my_piece, ('row', 'col'), perm)  23.6 us
    ppermute x7, waiting for transfers between devices, shards(): shifted.append(lax.ppermute(my_piece, ('row', 'col'), perm))  20.1 us
    ppermute x7, starting transfers between devices, shards(): shifted.append(lax.ppermute(my_piece, ('row', 'col'), perm))  17.4 us
    dot_general x1, matrix products, shards(): lax.dot_general(panel_here, column_panel, (((1,), (1,)), ((), ())), preci...  17.3 us
  transfers between devices with their start and end apart: 23, of which 6 were waited for; matrix products, arithmetic and copies ran while one was open for 5% of the time, Pallas kernels for 0%

profile of v8, /device:TPU:1, one launch (start us, length us, event | category | flops | bytes accessed | tf_op | source)
XLA Modules:
  0.0 459.5 jit_solution(11387287400015850546)
XLA Ops:
  9.4 3.2 copy.80
  12.7 3.9 fusion.8
  16.6 7.2 %all_to_all.8 = f32[128,1,8448]{2,1,0:T(1,128)} reshape(f32[256,4224]{1,0:T(8,128)} %fusion.8) | data formatting | bytes 8650752 | tf_op jit(solution)/shard_map/all_to_all | solution.py:39
  23.9 11.9 %all-to-all-start = ((f32[128,1,8448]{2,1,0:T(1,128)}), f32[128,1,8448]{2,1,0:T(1,128)}, u32[]{:S(2)}, u32[]{:S(2)}) async-start(f32[128,1,8448]{2,1,0:T(1,128)} %all_to_all.8), calls=%async_computation | async-start | bytes 8650752 | tf_op jit(solution)/shard_map/all_to_all | solution.py:39
  39.1 50.5 %all-to-all-done = f32[128,1,8448]{2,1,0:T(1,128)} async-done(((f32[128,1,8448]{2,1,0:T(1,128)}), f32[128,1,8448]{2,1,0:T(1,128)}, u32[]{:S(2)}, u32[]{:S(2)}) %all-to-all-start) | async-done | bytes 4325408 | tf_op jit(solution)/shard_map/all_to_all | solution.py:39
  89.7 14.0 %reduce.24 = f32[128,8448]{1,0:T(8,128)} reduce(f32[128,1,8448]{2,1,0:T(1,128)} %all-to-all-done, f32[]{:T(128)} %constant.251), dimensions={1}, to_apply=%all_to_all.7.reduce_sub_computation | reduce | bytes 8650756 | tf_op jit(solution)/shard_map/all_to_all | solution.py:39
  103.7 5.0 %reshape.140 = f32[256,4224]{1,0:T(8,128)} reshape(f32[128,8448]{1,0:T(8,128)} %reduce.24) | data formatting | bytes 8650752 | tf_op jit(solution)/shard_map/reshape | solution.py:45
  109.7 3.9 fusion.12
  117.9 2.6 add.136
  127.2 11.7 %cholesky.104 = f32[128,128]{1,0:T(8,128)S(1)} custom-call(f32[128,128]{1,0:T(8,128)S(1)} %cholesky.266), custom_call_target="Cholesky" | custom-call | tf_op jit(solution)/shard_map/jit(cholesky)/cholesky | solution.py:73
  138.9 9.8 %custom-call.30 = f32[1,128,128]{1,2,0:T(8,128)S(1)} custom-call(f32[1,128,128]{2,1,0:T(8,128)S(1)} %get-tuple-element.40), custom_call_target="InvertDiagBlocksLowerTriangular" | custom-call | tf_op jit(solution)/shard_map/jit(cholesky)/cholesky | solution.py:73
  151.4 11.7 %cholesky.217 = f32[128,128]{1,0:T(8,128)S(1)} custom-call(f32[128,128]{1,0:T(8,128)S(1)} %cholesky.270), custom_call_target="Cholesky" | custom-call | tf_op jit(solution)/shard_map/jit(cholesky)/cholesky | solution.py:73
  163.1 10.0 %custom-call.31 = f32[1,128,128]{1,2,0:T(8,128)S(1)} custom-call(f32[1,128,128]{2,1,0:T(8,128)S(1)} %get-tuple-element.37), custom_call_target="InvertDiagBlocksLowerTriangular" | custom-call | tf_op jit(solution)/shard_map/jit(cholesky)/cholesky | solution.py:73
  174.7 11.7 %cholesky.238 = f32[128,128]{1,0:T(8,128)S(1)} custom-call(f32[128,128]{1,0:T(8,128)S(1)} %cholesky.275), custom_call_target="Cholesky" | custom-call | tf_op jit(solution)/shard_map/jit(cholesky)/cholesky | solution.py:73
  187.2 9.8 %custom-call.32 = f32[1,128,128]{1,2,0:T(8,128)S(1)} custom-call(f32[1,128,128]{2,1,0:T(8,128)S(1)} %get-tuple-element.34), custom_call_target="InvertDiagBlocksLowerTriangular" | custom-call | tf_op jit(solution)/shard_map/jit(cholesky)/cholesky | solution.py:73
  198.4 12.2 %cholesky.255 = f32[128,128]{1,0:T(8,128)S(1)} custom-call(f32[128,128]{1,0:T(8,128)S(1)} %convolution_subtract_fusion.4), custom_call_target="Cholesky" | custom-call | tf_op jit(solution)/shard_map/jit(cholesky)/cholesky | solution.py:73
  226.9 2.7 fusion.30
  229.7 10.6 %while.1 = (s32[]{:T(128)}, f32[512,512]{1,0:T(8,128)S(1)}, s32[4,2]{0,1:T(2,128)S(1)}, f32[4,128,128]{2,1,0:T(8,128)}, s32[]{:T(128)}) while((s32[]{:T(128)}, f32[512,512]{1,0:T(8,128)S(1)}, s32[4,2]{0,1:T(2,128)S(1)}, f32[4,128,128]{2,1,0:T(8,128)}, s32[]{:T(128)}) %tuple.39), condition=%wide.while_cond, body=%wide.while_body.sunk | while | flops 2 | bytes 132205 | solution.py:97
  235.6 2.0 bitcast_dynamic-update-slice_fusion.18
  241.2 40.1 %custom-call.33 = f32[4,128,128]{1,2,0:T(8,128)S(1)} custom-call(f32[4,128,128]{2,1,0:T(8,128)} %get-tuple-element.9), custom_call_target="InvertDiagBlocksLowerTriangular" | custom-call | tf_op jit(solution)/shard_map/triangular_solve | solution.py:97
  289.1 2.9 fusion.21
  293.4 2.2 fusion.49
  304.8 38.9 %collective-permute-done.12 = f32[128,512]{1,0:T(8,128)S(1)} collective-permute-done((f32[128,512]{1,0:T(8,128)S(1)}, f32[128,512]{1,0:T(8,128)S(1)}, u32[]{:S(2)}, u32[]{:S(2)}) %collective-permute-start.12) | collective-permute-done | bytes 262176 | tf_op jit(solution)/shard_map/ppermute | solution.py:106
  349.3 3.2 collective-permute-start.20
  352.6 23.6 %collective-permute-done.20 = f32[128,512]{1,0:T(8,128)S(1)} collective-permute-done((f32[128,512]{1,0:T(8,128)S(1)}, f32[128,512]{1,0:T(8,128)S(1)}, u32[]{:S(2)}, u32[]{:S(2)}) %collective-permute-start.20) | collective-permute-done | bytes 262176 | tf_op jit(solution)/shard_map/ppermute | solution.py:115
  377.0 5.7 %fusion.5 = f32[64,8,32,128]{3,1,2,0:T(8,128)S(1)} fusion(f32[256,4224]{1,0:T(8,128)} %reshape.140, s32[256]{0:T(256)S(1)} %select_reduce_fusion), kind=kOutput, calls=%fused_computation.9 | convolution fusion | flops 6442582016 | bytes 12583936 | tf_op jit(solution)/shard_map/dot_general | solution.py:87
  387.4 10.9 %copy.53 = f32[32,32,16,128]{3,2,1,0:T(8,128)} copy(f32[32,32,16,128]{3,1,2,0:T(8,128)S(1)} %bitcast_bitcast_fusion) | data formatting | bytes 16777216 | tf_op jit(solution)/shard_map/transpose | solution.py:94
  401.2 8.8 %collective-permute-start.17 = (f32[128,512]{1,0:T(8,128)S(1)}, f32[128,512]{1,0:T(8,128)S(1)}, u32[]{:S(2)}, u32[]{:S(2)}) collective-permute-start(f32[128,512]{1,0:T(8,128)S(1)} %get-tuple-element.19), channel_id=1, source_target_pairs={{0,3},{1,4},{2,5},{3,6},{4,7},{5,0},{6,1},{7,2},{8,11},{9,12},{10,... | collective-permute-start | bytes 786440 | tf_op jit(solution)/shard_map/ppermute | solution.py:124
  411.5 2.9 collective-permute-start.16
  414.4 13.8 %collective-permute-done.15 = f32[128,512]{1,0:T(8,128)S(1)} collective-permute-done((f32[128,512]{1,0:T(8,128)S(1)}, f32[128,512]{1,0:T(8,128)S(1)}, u32[]{:S(2)}, u32[]{:S(2)}) %collective-permute-start.15) | collective-permute-done | bytes 262176 | tf_op jit(solution)/shard_map/ppermute | solution.py:124
  428.3 4.5 collective-permute-done.16
  435.1 17.3 %fusion = f32[1024,2048]{1,0:T(8,128)} fusion(f32[1024,2048]{1,0:T(8,128)} %param.4, f32[128,8,16,128]{3,2,1,0:T(8,128)} %bitcast.111, pred[2048]{0:T(1024)(128)(4,1)S(1)} %add_compare_fusion, pred[1024]{0:T(1024)(128)(4,1)S(1)} %add_compare_fusion.1, f32[1024,512]{1,0:T(8,128)S(1)} %bitcast.113, f32[2048,512]{1,0:T(8,128)} %all-gather.2.cloned.1.call-done), kind=kOutput, calls=%fused_computation.3 | convolution fusion | flops 6450839552 | bytes 31460352 | tf_op jit(solution)/shard_map/dot_general | solution.py:128
  (148 shorter events, 83.1 us)
Async XLA Ops:
  23.9 65.8 %all-to-all-start = ((f32[128,1,8448]{2,1,0:T(1,128)}), f32[128,1,8448]{2,1,0:T(1,128)}, u32[]{:S(2)}, u32[]{:S(2)}) async-start(f32[128,1,8448]{2,1,0:T(1,128)} %all_to_all.8), calls=%async_computation | async-start | bytes 8650752 | tf_op jit(solution)/shard_map/all_to_all | solution.py:39
  35.7 1.6 slice-start
  35.8 399.4 %all-gather.2.cloned.1.call-start = ((), (), s32[]{:S(2)}) async-start(), calls=%async_computation.1 | async-start | bytes 4456448 | tf_op jit(solution)/shard_map/all_gather | solution.py:116
  126.2 1.0 copy-start.7
  215.6 4.9 %collective-permute-start.2 = (f32[512,512]{1,0:T(8,128)}, f32[512,512]{1,0:T(8,128)}, u32[]{:S(2)}, u32[]{:S(2)}) collective-permute-start(f32[512,512]{1,0:T(8,128)} %select_select_fusion.2), channel_id=1, source_target_pairs={{0,32}} | collective-permute-start | bytes 3145736 | tf_op jit(solution)/shard_map/ppermute | solution.py:78
  217.2 3.3 collective-permute-start.1
  218.8 1.7 collective-permute-start
  221.9 4.0 collective-permute-start.5
  222.7 3.3 collective-permute-start.4
  224.3 2.6 collective-permute-start.3
  292.0 5.1 %copy-start.2 = (f32[1024,128]{1,0:T(8,128)S(1)}, f32[1024,128]{1,0:T(8,128)}, u32[]{:S(2)}) copy-start(f32[1024,128]{1,0:T(8,128)} %copy.62) | copy-start | bytes 1572868
  292.0 5.1 %copy-start.3 = (f32[1024,128]{1,0:T(8,128)S(1)}, f32[1024,128]{1,0:T(8,128)}, u32[]{:S(2)}) copy-start(f32[1024,128]{1,0:T(8,128)} %copy.63) | copy-start | bytes 1572868
  293.3 3.8 copy-start.4
  293.3 3.8 copy-start.5
  298.7 45.0 %collective-permute-start.12 = (f32[128,512]{1,0:T(8,128)S(1)}, f32[128,512]{1,0:T(8,128)S(1)}, u32[]{:S(2)}, u32[]{:S(2)}) collective-permute-start(f32[128,512]{1,0:T(8,128)S(1)} %get-tuple-element.24), channel_id=1, source_target_pairs={{0,1},{8,9},{16,17},{24,25},{32,33},{40,41},{48,49},{56,57},{64,65... | collective-permute-start | bytes 786440 | tf_op jit(solution)/shard_map/ppermute | solution.py:106
  300.0 45.1 %collective-permute-start.11 = (f32[128,512]{1,0:T(8,128)S(1)}, f32[128,512]{1,0:T(8,128)S(1)}, u32[]{:S(2)}, u32[]{:S(2)}) collective-permute-start(f32[128,512]{1,0:T(8,128)S(1)} %get-tuple-element.25), channel_id=1, source_target_pairs={{0,2},{8,10},{16,18},{24,26},{32,34},{40,42},{48,50},{56,58},{64,6... | collective-permute-start | bytes 786440 | tf_op jit(solution)/shard_map/ppermute | solution.py:106
  300.7 46.7 %collective-permute-start.10 = (f32[128,512]{1,0:T(8,128)S(1)}, f32[128,512]{1,0:T(8,128)}, u32[]{:S(2)}, u32[]{:S(2)}) collective-permute-start(f32[128,512]{1,0:T(8,128)S(1)} %get-tuple-element.26), channel_id=1, source_target_pairs={{0,3},{8,11},{16,19},{24,27},{32,35},{40,43},{48,51},{56,59},{64,6... | collective-permute-start | bytes 786440 | tf_op jit(solution)/shard_map/ppermute | solution.py:106
  302.1 45.3 %collective-permute-start.9 = (f32[128,512]{1,0:T(8,128)S(1)}, f32[128,512]{1,0:T(8,128)}, u32[]{:S(2)}, u32[]{:S(2)}) collective-permute-start(f32[128,512]{1,0:T(8,128)S(1)} %get-tuple-element.27), channel_id=1, source_target_pairs={{0,4},{8,12},{16,20},{24,28},{32,36},{40,44},{48,52},{56,60},{64,6... | collective-permute-start | bytes 786440 | tf_op jit(solution)/shard_map/ppermute | solution.py:106
  303.5 43.9 %collective-permute-start.8 = (f32[128,512]{1,0:T(8,128)S(1)}, f32[128,512]{1,0:T(8,128)}, u32[]{:S(2)}, u32[]{:S(2)}) collective-permute-start(f32[128,512]{1,0:T(8,128)S(1)} %get-tuple-element.28), channel_id=1, source_target_pairs={{0,5},{8,13},{16,21},{24,29},{32,37},{40,45},{48,53},{56,61},{64,6... | collective-permute-start | bytes 786440 | tf_op jit(solution)/shard_map/ppermute | solution.py:106
  343.8 1.4 copy-start.10
  343.8 3.6 collective-permute-start.7
  345.8 1.6 collective-permute-start.6
  349.3 26.8 %collective-permute-start.20 = (f32[128,512]{1,0:T(8,128)S(1)}, f32[128,512]{1,0:T(8,128)S(1)}, u32[]{:S(2)}, u32[]{:S(2)}) collective-permute-start(f32[128,512]{1,0:T(8,128)S(1)} %get-tuple-element.19), channel_id=1, source_target_pairs={{0,0},{1,8},{2,16},{3,24},{4,32},{5,40},{6,48},{7,56},{8,64},{9,72... | collective-permute-start | bytes 786440 | tf_op jit(solution)/shard_map/ppermute | solution.py:115
  384.5 27.0 %collective-permute-start.14 = (f32[128,512]{1,0:T(8,128)S(1)}, f32[128,512]{1,0:T(8,128)S(1)}, u32[]{:S(2)}, u32[]{:S(2)}) collective-permute-start(f32[128,512]{1,0:T(8,128)S(1)} %get-tuple-element.19), channel_id=1, source_target_pairs={{0,6},{1,7},{2,0},{3,1},{4,2},{5,3},{6,4},{7,5},{8,14},{9,15},{10,... | collective-permute-start | bytes 786440 | tf_op jit(solution)/shard_map/ppermute | solution.py:124
  385.8 24.3 %collective-permute-start.13 = (f32[128,512]{1,0:T(8,128)S(1)}, f32[128,512]{1,0:T(8,128)S(1)}, u32[]{:S(2)}, u32[]{:S(2)}) collective-permute-start(f32[128,512]{1,0:T(8,128)S(1)} %get-tuple-element.19), channel_id=1, source_target_pairs={{0,7},{1,0},{2,1},{3,2},{4,3},{5,4},{6,5},{7,6},{8,15},{9,8},{10,9... | collective-permute-start | bytes 786440 | tf_op jit(solution)/shard_map/ppermute | solution.py:124
  387.4 24.1 %copy-start.8 = (f32[16,128,512]{2,1,0:T(8,128)S(1)}, f32[16,128,512]{2,1,0:T(8,128)}, u32[]{:S(2)}) copy-start(f32[16,128,512]{2,1,0:T(8,128)} %get-tuple-element.18) | copy-start | bytes 12582916
  398.3 36.4 %collective-permute-start.19 = (f32[128,512]{1,0:T(8,128)S(1)}, f32[128,512]{1,0:T(8,128)S(1)}, u32[]{:S(2)}, u32[]{:S(2)}) collective-permute-start(f32[128,512]{1,0:T(8,128)S(1)} %get-tuple-element.19), channel_id=1, source_target_pairs={{0,1},{1,2},{2,3},{3,4},{4,5},{5,6},{6,7},{7,0},{8,9},{9,10},{10,1... | collective-permute-start | bytes 786440 | tf_op jit(solution)/shard_map/ppermute | solution.py:124
  400.0 34.6 %collective-permute-start.18 = (f32[128,512]{1,0:T(8,128)S(1)}, f32[128,512]{1,0:T(8,128)S(1)}, u32[]{:S(2)}, u32[]{:S(2)}) collective-permute-start(f32[128,512]{1,0:T(8,128)S(1)} %get-tuple-element.19), channel_id=1, source_target_pairs={{0,2},{1,3},{2,4},{3,5},{4,6},{5,7},{6,0},{7,1},{8,10},{9,11},{10,... | collective-permute-start | bytes 786440 | tf_op jit(solution)/shard_map/ppermute | solution.py:124
  401.2 33.3 %collective-permute-start.17 = (f32[128,512]{1,0:T(8,128)S(1)}, f32[128,512]{1,0:T(8,128)S(1)}, u32[]{:S(2)}, u32[]{:S(2)}) collective-permute-start(f32[128,512]{1,0:T(8,128)S(1)} %get-tuple-element.19), channel_id=1, source_target_pairs={{0,3},{1,4},{2,5},{3,6},{4,7},{5,0},{6,1},{7,2},{8,11},{9,12},{10,... | collective-permute-start | bytes 786440 | tf_op jit(solution)/shard_map/ppermute | solution.py:124
  410.1 18.2 %collective-permute-start.15 = (f32[128,512]{1,0:T(8,128)S(1)}, f32[128,512]{1,0:T(8,128)S(1)}, u32[]{:S(2)}, u32[]{:S(2)}) collective-permute-start(f32[128,512]{1,0:T(8,128)S(1)} %get-tuple-element.19), channel_id=1, source_target_pairs={{0,5},{1,6},{2,7},{3,0},{4,1},{5,2},{6,3},{7,4},{8,13},{9,14},{10,... | collective-permute-start | bytes 786440 | tf_op jit(solution)/shard_map/ppermute | solution.py:124
  411.5 21.3 %collective-permute-start.16 = (f32[128,512]{1,0:T(8,128)S(1)}, f32[128,512]{1,0:T(8,128)S(1)}, u32[]{:S(2)}, u32[]{:S(2)}) collective-permute-start(f32[128,512]{1,0:T(8,128)S(1)} %get-tuple-element.19), channel_id=1, source_target_pairs={{0,4},{1,5},{2,6},{3,7},{4,0},{5,1},{6,2},{7,3},{8,12},{9,13},{10,... | collective-permute-start | bytes 786440 | tf_op jit(solution)/shard_map/ppermute | solution.py:124
  435.1 17.4 %copy-start = (f32[8,128,512]{2,1,0:T(8,128)}, f32[8,128,512]{2,1,0:T(8,128)S(1)}, u32[]{:S(2)}) copy-start(f32[8,128,512]{2,1,0:T(8,128)S(1)} %constant_dynamic-slice_fusion.1) | copy-start | bytes 6291460
  (5 other events, 4.2 us)
Sparse Core Ops, SparseCore 0:
  377.0 55.1 all-gather.1

commit v9 on v8

--- a/solution.py
+++ b/solution.py
@@ -113,7 +113,17 @@
         for j in range(col_count):
             perm.append((k * col_count + j, (col_count * b + j) * col_count + c))
     mine = lax.ppermute(my_piece, ("row", "col"), perm)
-    column_panel = lax.all_gather(mine, "row", axis=0, tiled=True)
+    moved = [mine]
+    for s_ in range(1, row_count):
+        perm = [
+            (k * col_count + j, ((k + s_) % row_count) * col_count + j)
+            for k in range(row_count)
+            for j in range(col_count)
+        ]
+        moved.append(lax.ppermute(mine, ("row", "col"), perm))
+    turned_rows = jnp.stack([moved[(row_count - m) % row_count] for m in range(row_count)] * 2)
+    column_panel = lax.dynamic_slice_in_dim(turned_rows, (row_count - row_id) % row_count, row_count, 0)
+    column_panel = column_panel.reshape(row_count * piece_rows, PANEL)
     shifted = [my_piece]
     for s_ in range(1, col_count):
         perm = [

time: 465 us -> 515 us (1.11)
  waiting for transfers between devices: 133 us -> 178 us
  starting transfers between devices: 51 us -> 69.9 us
  between operations: 17.5 us -> 4.22 us
  local copies, waits for them, and re-layouts: 59.5 us -> 65.5 us
    ppermute x0 -> x15, waiting for transfers between devices: none -> 65 us  [shards(): moved.append(lax.ppermute(mine, ('row', 'col'), perm))]
    ppermute x1, waiting for transfers between devices: 23.6 us -> 0.01 us  [shards(): mine = lax.ppermute(my_piece, ('row', 'col'), perm)]
    ppermute x0 -> x15, starting transfers between devices: none -> 16.4 us  [shards(): moved.append(lax.ppermute(mine, ('row', 'col'), perm))]
    unnamed x45 -> x66, local copies, waits for them, and re-layouts: 12.8 us -> 21.8 us
    another operation x12 -> x13, local copies, waits for them, and re-layouts: 10.6 us -> 10.1 us
  transfers between devices with their start and end apart: 23 -> 37, of which waited for: 6 -> 12; matrix products, arithmetic and copies ran while one was open for 5% -> 6% of each run, Pallas kernels for 0% -> 0%
where the time goes in v9:
time: 515 us; the launch traced here: 509 us
  waiting for transfers between devices  178 us (35%)
  other arithmetic  150 us (29%)
  starting transfers between devices  69.9 us (14%)
  local copies, waits for them, and re-layouts  65.5 us (13%)
  matrix products  42.2 us (8%)
    another operation x14, other arithmetic, shards(): factor11 = jnp.linalg.cholesky(safe_block)  78.9 us
    ppermute x15, waiting for transfers between devices, shards(): moved.append(lax.ppermute(mine, ('row', 'col'), perm))  65 us
    all_to_all x1, waiting for transfers between devices, shards(): lax.all_to_all(outgoing.reshape(devices, capacity * width), ('row', 'col'...  51.9 us
    another operation x4, other arithmetic, shards(): lax.linalg.triangular_solve(factor_col0, panel_cols, left_side=False, low...  43 us
    ppermute x7, waiting for transfers between devices, shards(): lax.ppermute(solved[j * piece_rows:(j + 1) * piece_rows], ('row', 'col'),...  39.3 us
    unnamed x66, local copies, waits for them, and re-layouts  21.8 us
    ppermute x7, waiting for transfers between devices, shards(): shifted.append(lax.ppermute(my_piece, ('row', 'col'), perm))  21.6 us
    ppermute x7, starting transfers between devices, shards(): shifted.append(lax.ppermute(my_piece, ('row', 'col'), perm))  21.4 us
  transfers between devices with their start and end apart: 37, of which 12 were waited for; matrix products, arithmetic and copies ran while one was open for 6% of the time, Pallas kernels for 0%

profile of v9, /device:TPU:1, one launch (start us, length us, event | category | flops | bytes accessed | tf_op | source)
XLA Modules:
  0.0 509.3 jit_solution(760194912496084120)
XLA Ops:
  6.2 3.9 fusion.8
  10.1 7.2 %all_to_all.8 = f32[128,1,8448]{2,1,0:T(1,128)} reshape(f32[256,4224]{1,0:T(8,128)} %fusion.8) | data formatting | bytes 8650752 | tf_op jit(solution)/shard_map/all_to_all | solution.py:39
  17.3 12.4 %all-to-all-start = ((f32[128,1,8448]{2,1,0:T(1,128)}), f32[128,1,8448]{2,1,0:T(1,128)}, u32[]{:S(2)}, u32[]{:S(2)}) async-start(f32[128,1,8448]{2,1,0:T(1,128)} %all_to_all.8), calls=%async_computation | async-start | bytes 8650752 | tf_op jit(solution)/shard_map/all_to_all | solution.py:39
  31.5 51.9 %all-to-all-done = f32[128,1,8448]{2,1,0:T(1,128)} async-done(((f32[128,1,8448]{2,1,0:T(1,128)}), f32[128,1,8448]{2,1,0:T(1,128)}, u32[]{:S(2)}, u32[]{:S(2)}) %all-to-all-start) | async-done | bytes 4325408 | tf_op jit(solution)/shard_map/all_to_all | solution.py:39
  83.5 14.0 %reduce.24 = f32[128,8448]{1,0:T(8,128)} reduce(f32[128,1,8448]{2,1,0:T(1,128)} %all-to-all-done, f32[]{:T(128)} %constant.256), dimensions={1}, to_apply=%all_to_all.7.reduce_sub_computation | reduce | bytes 8650756 | tf_op jit(solution)/shard_map/all_to_all | solution.py:39
  97.5 5.0 reshape.143
  103.5 3.9 fusion.12
  121.4 11.7 %cholesky.104 = f32[128,128]{1,0:T(8,128)S(1)} custom-call(f32[128,128]{1,0:T(8,128)S(1)} %cholesky.266), custom_call_target="Cholesky" | custom-call | tf_op jit(solution)/shard_map/jit(cholesky)/cholesky | solution.py:73
  133.1 9.8 %custom-call.30 = f32[1,128,128]{1,2,0:T(8,128)S(1)} custom-call(f32[1,128,128]{2,1,0:T(8,128)S(1)} %get-tuple-element.40), custom_call_target="InvertDiagBlocksLowerTriangular" | custom-call | tf_op jit(solution)/shard_map/jit(cholesky)/cholesky | solution.py:73
  145.6 11.7 %cholesky.217 = f32[128,128]{1,0:T(8,128)S(1)} custom-call(f32[128,128]{1,0:T(8,128)S(1)} %cholesky.270), custom_call_target="Cholesky" | custom-call | tf_op jit(solution)/shard_map/jit(cholesky)/cholesky | solution.py:73
  157.3 10.0 %custom-call.31 = f32[1,128,128]{1,2,0:T(8,128)S(1)} custom-call(f32[1,128,128]{2,1,0:T(8,128)S(1)} %get-tuple-element.37), custom_call_target="InvertDiagBlocksLowerTriangular" | custom-call | tf_op jit(solution)/shard_map/jit(cholesky)/cholesky | solution.py:73
  168.8 11.7 %cholesky.238 = f32[128,128]{1,0:T(8,128)S(1)} custom-call(f32[128,128]{1,0:T(8,128)S(1)} %cholesky.275), custom_call_target="Cholesky" | custom-call | tf_op jit(solution)/shard_map/jit(cholesky)/cholesky | solution.py:73
  181.2 9.8 %custom-call.32 = f32[1,128,128]{1,2,0:T(8,128)S(1)} custom-call(f32[1,128,128]{2,1,0:T(8,128)S(1)} %get-tuple-element.34), custom_call_target="InvertDiagBlocksLowerTriangular" | custom-call | tf_op jit(solution)/shard_map/jit(cholesky)/cholesky | solution.py:73
  192.5 12.1 %cholesky.255 = f32[128,128]{1,0:T(8,128)S(1)} custom-call(f32[128,128]{1,0:T(8,128)S(1)} %convolution_subtract_fusion.4), custom_call_target="Cholesky" | custom-call | tf_op jit(solution)/shard_map/jit(cholesky)/cholesky | solution.py:73
  223.7 10.1 %while.1 = (s32[]{:T(128)}, f32[512,512]{1,0:T(8,128)S(1)}, s32[4,2]{0,1:T(2,128)S(1)}, f32[4,128,128]{2,1,0:T(8,128)}, s32[]{:T(128)}) while((s32[]{:T(128)}, f32[512,512]{1,0:T(8,128)S(1)}, s32[4,2]{0,1:T(2,128)S(1)}, f32[4,128,128]{2,1,0:T(8,128)}, s32[]{:T(128)}) %tuple.39), condition=%wide.while_cond, body=%wide.while_body.sunk | while | flops 2 | bytes 132705 | solution.py:97
  234.8 40.1 %custom-call.33 = f32[4,128,128]{1,2,0:T(8,128)S(1)} custom-call(f32[4,128,128]{2,1,0:T(8,128)} %get-tuple-element.9), custom_call_target="InvertDiagBlocksLowerTriangular" | custom-call | tf_op jit(solution)/shard_map/triangular_solve | solution.py:97
  297.1 5.7 %fusion.5 = f32[64,8,32,128]{3,1,2,0:T(8,128)S(1)} fusion(f32[256,4224]{1,0:T(8,128)} %reshape.143, s32[256]{0:T(256)S(1)} %select_reduce_fusion), kind=kOutput, calls=%fused_computation.9 | convolution fusion | flops 6442582016 | bytes 12583936 | tf_op jit(solution)/shard_map/dot_general | solution.py:87
  304.6 39.2 %collective-permute-done.12 = f32[128,512]{1,0:T(8,128)S(1)} collective-permute-done((f32[128,512]{1,0:T(8,128)S(1)}, f32[128,512]{1,0:T(8,128)S(1)}, u32[]{:S(2)}, u32[]{:S(2)}) %collective-permute-start.12) | collective-permute-done | bytes 262176 | tf_op jit(solution)/shard_map/ppermute | solution.py:106
  344.8 11.8 %collective-permute-start.13 = (f32[128,512]{1,0:T(8,128)S(1)}, f32[128,512]{1,0:T(8,128)S(1)}, u32[]{:S(2)}, u32[]{:S(2)}) collective-permute-start(f32[128,512]{1,0:T(8,128)S(1)} %get-tuple-element.19), channel_id=1, source_target_pairs={{0,7},{1,0},{2,1},{3,2},{4,3},{5,4},{6,5},{7,6},{8,15},{9,8},{10,9... | collective-permute-start | bytes 786440 | tf_op jit(solution)/shard_map/ppermute | solution.py:134
  357.9 7.6 %copy.53 = f32[32,32,16,128]{3,2,1,0:T(8,128)S(1)} copy(f32[32,32,16,128]{3,1,2,0:T(8,128)S(1)} %bitcast_bitcast_fusion) | data formatting | bytes 16777216 | tf_op jit(solution)/shard_map/transpose | solution.py:94
  365.5 4.0 collective-permute-start.20
  369.6 5.9 %collective-permute-start.16 = (f32[128,512]{1,0:T(8,128)S(1)}, f32[128,512]{1,0:T(8,128)S(1)}, u32[]{:S(2)}, u32[]{:S(2)}) collective-permute-start(f32[128,512]{1,0:T(8,128)S(1)} %get-tuple-element.19), channel_id=1, source_target_pairs={{0,4},{1,5},{2,6},{3,7},{4,0},{5,1},{6,2},{7,3},{8,12},{9,13},{10,... | collective-permute-start | bytes 786440 | tf_op jit(solution)/shard_map/ppermute | solution.py:134
  375.5 3.4 collective-permute-start.17
  380.4 13.9 %collective-permute-done.15 = f32[128,512]{1,0:T(8,128)S(1)} collective-permute-done((f32[128,512]{1,0:T(8,128)S(1)}, f32[128,512]{1,0:T(8,128)S(1)}, u32[]{:S(2)}, u32[]{:S(2)}) %collective-permute-start.15) | collective-permute-done | bytes 262176 | tf_op jit(solution)/shard_map/ppermute | solution.py:134
  400.0 4.9 collective-permute-done.19
  415.8 5.5 %collective-permute-start.25 = (f32[128,512]{1,0:T(8,128)S(1)}, f32[128,512]{1,0:T(8,128)S(1)}, u32[]{:S(2)}, u32[]{:S(2)}) collective-permute-start(f32[128,512]{1,0:T(8,128)S(1)} %collective-permute-done.20), channel_id=1, source_target_pairs={{0,88},{1,89},{2,90},{3,91},{4,92},{5,93},{6,94},{7,95},{8,96},{9,... | collective-permute-start | bytes 786440 | tf_op jit(solution)/shard_map/ppermute | solution.py:123
  425.2 28.1 %collective-permute-done.24 = f32[128,512]{1,0:T(8,128)S(1)} collective-permute-done((f32[128,512]{1,0:T(8,128)S(1)}, f32[128,512]{1,0:T(8,128)S(1)}, u32[]{:S(2)}, u32[]{:S(2)}) %collective-permute-start.24) | collective-permute-done | bytes 262176 | tf_op jit(solution)/shard_map/ppermute | solution.py:123
  453.4 5.0 collective-permute-start.31
  461.8 3.9 collective-permute-done.30
  469.0 9.5 %collective-permute-done.32 = f32[128,512]{1,0:T(8,128)S(1)} collective-permute-done((f32[128,512]{1,0:T(8,128)S(1)}, f32[128,512]{1,0:T(8,128)S(1)}, u32[]{:S(2)}, u32[]{:S(2)}) %collective-permute-start.32) | collective-permute-done | bytes 262176 | tf_op jit(solution)/shard_map/ppermute | solution.py:123
  478.5 16.4 %collective-permute-done.34 = f32[128,512]{1,0:T(8,128)S(1)} collective-permute-done((f32[128,512]{1,0:T(8,128)S(1)}, f32[128,512]{1,0:T(8,128)S(1)}, u32[]{:S(2)}, u32[]{:S(2)}) %collective-permute-start.34) | collective-permute-done | bytes 262176 | tf_op jit(solution)/shard_map/ppermute | solution.py:123
  495.9 13.2 %fusion = f32[1024,2048]{1,0:T(8,128)} fusion(f32[1024,2048]{1,0:T(8,128)} %param.4, f32[128,8,16,128]{3,2,1,0:T(8,128)S(1)} %bitcast.160, pred[2048]{0:T(1024)(128)(4,1)S(1)} %add_compare_fusion, pred[1024]{0:T(1024)(128)(4,1)S(1)} %add_compare_fusion.1, f32[1024,512]{1,0:T(8,128)S(1)} %bitcast.163, f32[2048,512]{1,0:T(8,128)S(1)} %bitcast.162), kind=kOutput, calls=%fused_computation.3 | convolution fusion | flops 6450839552 | bytes 31460352 | tf_op jit(solution)/shard_map/dot_general | solution.py:138
  (198 shorter events, 111.9 us)
Async XLA Ops:
  17.3 66.2 %all-to-all-start = ((f32[128,1,8448]{2,1,0:T(1,128)}), f32[128,1,8448]{2,1,0:T(1,128)}, u32[]{:S(2)}, u32[]{:S(2)}) async-start(f32[128,1,8448]{2,1,0:T(1,128)} %all_to_all.8), calls=%async_computation | async-start | bytes 8650752 | tf_op jit(solution)/shard_map/all_to_all | solution.py:39
  209.5 5.0 collective-permute-start
  290.3 5.4 %collective-permute-start.10 = (f32[128,512]{1,0:T(8,128)}, f32[128,512]{1,0:T(8,128)}, u32[]{:S(2)}, u32[]{:S(2)}) collective-permute-start(f32[128,512]{1,0:T(8,128)} %get-tuple-element.26), channel_id=1, source_target_pairs={{0,3},{8,11},{16,19},{24,27},{32,35},{40,43},{48,51},{56,59},{64,6... | collective-permute-start | bytes 786440 | tf_op jit(solution)/shard_map/ppermute | solution.py:106
  291.6 4.7 collective-permute-start.11
  293.0 50.8 %collective-permute-start.12 = (f32[128,512]{1,0:T(8,128)S(1)}, f32[128,512]{1,0:T(8,128)S(1)}, u32[]{:S(2)}, u32[]{:S(2)}) collective-permute-start(f32[128,512]{1,0:T(8,128)S(1)} %get-tuple-element.24), channel_id=1, source_target_pairs={{0,1},{8,9},{16,17},{24,25},{32,33},{40,41},{48,49},{56,57},{64,65... | collective-permute-start | bytes 786440 | tf_op jit(solution)/shard_map/ppermute | solution.py:106
  294.3 49.5 %collective-permute-start.6 = (f32[128,512]{1,0:T(8,128)S(1)}, f32[128,512]{1,0:T(8,128)S(1)}, u32[]{:S(2)}, u32[]{:S(2)}) collective-permute-start(f32[128,512]{1,0:T(8,128)S(1)} %get-tuple-element.30), channel_id=1, source_target_pairs={{0,7},{8,15},{16,23},{24,31},{32,39},{40,47},{48,55},{56,63},{64,7... | collective-permute-start | bytes 786440 | tf_op jit(solution)/shard_map/ppermute | solution.py:106
  295.0 48.9 %collective-permute-start.7 = (f32[128,512]{1,0:T(8,128)S(1)}, f32[128,512]{1,0:T(8,128)S(1)}, u32[]{:S(2)}, u32[]{:S(2)}) collective-permute-start(f32[128,512]{1,0:T(8,128)S(1)} %get-tuple-element.29), channel_id=1, source_target_pairs={{0,6},{8,14},{16,22},{24,30},{32,38},{40,46},{48,54},{56,62},{64,7... | collective-permute-start | bytes 786440 | tf_op jit(solution)/shard_map/ppermute | solution.py:106
  295.7 48.2 %collective-permute-start.8 = (f32[128,512]{1,0:T(8,128)S(1)}, f32[128,512]{1,0:T(8,128)S(1)}, u32[]{:S(2)}, u32[]{:S(2)}) collective-permute-start(f32[128,512]{1,0:T(8,128)S(1)} %get-tuple-element.28), channel_id=1, source_target_pairs={{0,5},{8,13},{16,21},{24,29},{32,37},{40,45},{48,53},{56,61},{64,6... | collective-permute-start | bytes 786440 | tf_op jit(solution)/shard_map/ppermute | solution.py:106
  296.4 47.5 %collective-permute-start.9 = (f32[128,512]{1,0:T(8,128)S(1)}, f32[128,512]{1,0:T(8,128)S(1)}, u32[]{:S(2)}, u32[]{:S(2)}) collective-permute-start(f32[128,512]{1,0:T(8,128)S(1)} %get-tuple-element.27), channel_id=1, source_target_pairs={{0,4},{8,12},{16,20},{24,28},{32,36},{40,44},{48,52},{56,60},{64,6... | collective-permute-start | bytes 786440 | tf_op jit(solution)/shard_map/ppermute | solution.py:106
  344.8 30.7 %collective-permute-start.13 = (f32[128,512]{1,0:T(8,128)S(1)}, f32[128,512]{1,0:T(8,128)S(1)}, u32[]{:S(2)}, u32[]{:S(2)}) collective-permute-start(f32[128,512]{1,0:T(8,128)S(1)} %get-tuple-element.19), channel_id=1, source_target_pairs={{0,7},{1,0},{2,1},{3,2},{4,3},{5,4},{6,5},{7,6},{8,15},{9,8},{10,9... | collective-permute-start | bytes 786440 | tf_op jit(solution)/shard_map/ppermute | solution.py:134
  356.7 23.0 %collective-permute-start.14 = (f32[128,512]{1,0:T(8,128)S(1)}, f32[128,512]{1,0:T(8,128)S(1)}, u32[]{:S(2)}, u32[]{:S(2)}) collective-permute-start(f32[128,512]{1,0:T(8,128)S(1)} %get-tuple-element.19), channel_id=1, source_target_pairs={{0,6},{1,7},{2,0},{3,1},{4,2},{5,3},{6,4},{7,5},{8,14},{9,15},{10,... | collective-permute-start | bytes 786440 | tf_op jit(solution)/shard_map/ppermute | solution.py:134
  365.5 40.8 %collective-permute-start.20 = (f32[128,512]{1,0:T(8,128)S(1)}, f32[128,512]{1,0:T(8,128)S(1)}, u32[]{:S(2)}, u32[]{:S(2)}) collective-permute-start(f32[128,512]{1,0:T(8,128)S(1)} %get-tuple-element.19), channel_id=1, source_target_pairs={{0,0},{1,8},{2,16},{3,24},{4,32},{5,40},{6,48},{7,56},{8,64},{9,72... | collective-permute-start | bytes 786440 | tf_op jit(solution)/shard_map/ppermute | solution.py:115
  369.5 24.8 %collective-permute-start.15 = (f32[128,512]{1,0:T(8,128)S(1)}, f32[128,512]{1,0:T(8,128)S(1)}, u32[]{:S(2)}, u32[]{:S(2)}) collective-permute-start(f32[128,512]{1,0:T(8,128)S(1)} %get-tuple-element.19), channel_id=1, source_target_pairs={{0,5},{1,6},{2,7},{3,0},{4,1},{5,2},{6,3},{7,4},{8,13},{9,14},{10,... | collective-permute-start | bytes 786440 | tf_op jit(solution)/shard_map/ppermute | solution.py:134
  369.6 25.4 %collective-permute-start.16 = (f32[128,512]{1,0:T(8,128)S(1)}, f32[128,512]{1,0:T(8,128)S(1)}, u32[]{:S(2)}, u32[]{:S(2)}) collective-permute-start(f32[128,512]{1,0:T(8,128)S(1)} %get-tuple-element.19), channel_id=1, source_target_pairs={{0,4},{1,5},{2,6},{3,7},{4,0},{5,1},{6,2},{7,3},{8,12},{9,13},{10,... | collective-permute-start | bytes 786440 | tf_op jit(solution)/shard_map/ppermute | solution.py:134
  375.5 20.2 %collective-permute-start.17 = (f32[128,512]{1,0:T(8,128)S(1)}, f32[128,512]{1,0:T(8,128)S(1)}, u32[]{:S(2)}, u32[]{:S(2)}) collective-permute-start(f32[128,512]{1,0:T(8,128)S(1)} %get-tuple-element.19), channel_id=1, source_target_pairs={{0,3},{1,4},{2,5},{3,6},{4,7},{5,0},{6,1},{7,2},{8,11},{9,12},{10,... | collective-permute-start | bytes 786440 | tf_op jit(solution)/shard_map/ppermute | solution.py:134
  379.7 19.6 %collective-permute-start.18 = (f32[128,512]{1,0:T(8,128)S(1)}, f32[128,512]{1,0:T(8,128)S(1)}, u32[]{:S(2)}, u32[]{:S(2)}) collective-permute-start(f32[128,512]{1,0:T(8,128)S(1)} %get-tuple-element.19), channel_id=1, source_target_pairs={{0,2},{1,3},{2,4},{3,5},{4,6},{5,7},{6,0},{7,1},{8,10},{9,11},{10,... | collective-permute-start | bytes 786440 | tf_op jit(solution)/shard_map/ppermute | solution.py:134
  394.3 10.6 %collective-permute-start.19 = (f32[128,512]{1,0:T(8,128)S(1)}, f32[128,512]{1,0:T(8,128)S(1)}, u32[]{:S(2)}, u32[]{:S(2)}) collective-permute-start(f32[128,512]{1,0:T(8,128)S(1)} %get-tuple-element.19), channel_id=1, source_target_pairs={{0,1},{1,2},{2,3},{3,4},{4,5},{5,6},{6,7},{7,0},{8,9},{9,10},{10,1... | collective-permute-start | bytes 786440 | tf_op jit(solution)/shard_map/ppermute | solution.py:134
  406.4 15.0 %collective-permute-start.21 = (f32[128,512]{1,0:T(8,128)S(1)}, f32[128,512]{1,0:T(8,128)S(1)}, u32[]{:S(2)}, u32[]{:S(2)}) collective-permute-start(f32[128,512]{1,0:T(8,128)S(1)} %collective-permute-done.20), channel_id=1, source_target_pairs={{0,120},{1,121},{2,122},{3,123},{4,124},{5,125},{6,126},{7,127},{8... | collective-permute-start | bytes 786440 | tf_op jit(solution)/shard_map/ppermute | solution.py:123
  406.4 14.9 %collective-permute-start.22 = (f32[128,512]{1,0:T(8,128)S(1)}, f32[128,512]{1,0:T(8,128)S(1)}, u32[]{:S(2)}, u32[]{:S(2)}) collective-permute-start(f32[128,512]{1,0:T(8,128)S(1)} %collective-permute-done.20), channel_id=1, source_target_pairs={{0,112},{1,113},{2,114},{3,115},{4,116},{5,117},{6,118},{7,119},{8... | collective-permute-start | bytes 786440 | tf_op jit(solution)/shard_map/ppermute | solution.py:123
  413.4 11.8 %collective-permute-start.23 = (f32[128,512]{1,0:T(8,128)S(1)}, f32[128,512]{1,0:T(8,128)S(1)}, u32[]{:S(2)}, u32[]{:S(2)}) collective-permute-start(f32[128,512]{1,0:T(8,128)S(1)} %collective-permute-done.20), channel_id=1, source_target_pairs={{0,104},{1,105},{2,106},{3,107},{4,108},{5,109},{6,110},{7,111},{8... | collective-permute-start | bytes 786440 | tf_op jit(solution)/shard_map/ppermute | solution.py:123
  413.6 39.6 %collective-permute-start.24 = (f32[128,512]{1,0:T(8,128)S(1)}, f32[128,512]{1,0:T(8,128)S(1)}, u32[]{:S(2)}, u32[]{:S(2)}) collective-permute-start(f32[128,512]{1,0:T(8,128)S(1)} %collective-permute-done.20), channel_id=1, source_target_pairs={{0,96},{1,97},{2,98},{3,99},{4,100},{5,101},{6,102},{7,103},{8,104... | collective-permute-start | bytes 786440 | tf_op jit(solution)/shard_map/ppermute | solution.py:123
  415.8 37.5 %collective-permute-start.25 = (f32[128,512]{1,0:T(8,128)S(1)}, f32[128,512]{1,0:T(8,128)S(1)}, u32[]{:S(2)}, u32[]{:S(2)}) collective-permute-start(f32[128,512]{1,0:T(8,128)S(1)} %collective-permute-done.20), channel_id=1, source_target_pairs={{0,88},{1,89},{2,90},{3,91},{4,92},{5,93},{6,94},{7,95},{8,96},{9,... | collective-permute-start | bytes 786440 | tf_op jit(solution)/shard_map/ppermute | solution.py:123
  421.3 32.1 %collective-permute-start.26 = (f32[128,512]{1,0:T(8,128)S(1)}, f32[128,512]{1,0:T(8,128)S(1)}, u32[]{:S(2)}, u32[]{:S(2)}) collective-permute-start(f32[128,512]{1,0:T(8,128)S(1)} %collective-permute-done.20), channel_id=1, source_target_pairs={{0,80},{1,81},{2,82},{3,83},{4,84},{5,85},{6,86},{7,87},{8,88},{9,... | collective-permute-start | bytes 786440 | tf_op jit(solution)/shard_map/ppermute | solution.py:123
  421.4 37.0 %collective-permute-start.27 = (f32[128,512]{1,0:T(8,128)S(1)}, f32[128,512]{1,0:T(8,128)S(1)}, u32[]{:S(2)}, u32[]{:S(2)}) collective-permute-start(f32[128,512]{1,0:T(8,128)S(1)} %collective-permute-done.20), channel_id=1, source_target_pairs={{0,72},{1,73},{2,74},{3,75},{4,76},{5,77},{6,78},{7,79},{8,80},{9,... | collective-permute-start | bytes 786440 | tf_op jit(solution)/shard_map/ppermute | solution.py:123
  425.2 33.3 %collective-permute-start.28 = (f32[128,512]{1,0:T(8,128)S(1)}, f32[128,512]{1,0:T(8,128)S(1)}, u32[]{:S(2)}, u32[]{:S(2)}) collective-permute-start(f32[128,512]{1,0:T(8,128)S(1)} %collective-permute-done.20), channel_id=1, source_target_pairs={{0,64},{1,65},{2,66},{3,67},{4,68},{5,69},{6,70},{7,71},{8,72},{9,... | collective-permute-start | bytes 786440 | tf_op jit(solution)/shard_map/ppermute | solution.py:123
  453.3 8.5 %collective-permute-start.29 = (f32[128,512]{1,0:T(8,128)S(1)}, f32[128,512]{1,0:T(8,128)S(1)}, u32[]{:S(2)}, u32[]{:S(2)}) collective-permute-start(f32[128,512]{1,0:T(8,128)S(1)} %collective-permute-done.20), channel_id=1, source_target_pairs={{0,56},{1,57},{2,58},{3,59},{4,60},{5,61},{6,62},{7,63},{8,64},{9,... | collective-permute-start | bytes 786440 | tf_op jit(solution)/shard_map/ppermute | solution.py:123
  453.3 12.4 %collective-permute-start.30 = (f32[128,512]{1,0:T(8,128)S(1)}, f32[128,512]{1,0:T(8,128)S(1)}, u32[]{:S(2)}, u32[]{:S(2)}) collective-permute-start(f32[128,512]{1,0:T(8,128)S(1)} %collective-permute-done.20), channel_id=1, source_target_pairs={{0,48},{1,49},{2,50},{3,51},{4,52},{5,53},{6,54},{7,55},{8,56},{9,... | collective-permute-start | bytes 786440 | tf_op jit(solution)/shard_map/ppermute | solution.py:123
  453.4 15.6 %collective-permute-start.31 = (f32[128,512]{1,0:T(8,128)S(1)}, f32[128,512]{1,0:T(8,128)S(1)}, u32[]{:S(2)}, u32[]{:S(2)}) collective-permute-start(f32[128,512]{1,0:T(8,128)S(1)} %collective-permute-done.20), channel_id=1, source_target_pairs={{0,40},{1,41},{2,42},{3,43},{4,44},{5,45},{6,46},{7,47},{8,48},{9,... | collective-permute-start | bytes 786440 | tf_op jit(solution)/shard_map/ppermute | solution.py:123
  458.4 20.1 %collective-permute-start.32 = (f32[128,512]{1,0:T(8,128)S(1)}, f32[128,512]{1,0:T(8,128)S(1)}, u32[]{:S(2)}, u32[]{:S(2)}) collective-permute-start(f32[128,512]{1,0:T(8,128)S(1)} %collective-permute-done.20), channel_id=1, source_target_pairs={{0,32},{1,33},{2,34},{3,35},{4,36},{5,37},{6,38},{7,39},{8,40},{9,... | collective-permute-start | bytes 786440 | tf_op jit(solution)/shard_map/ppermute | solution.py:123
  458.5 20.0 %collective-permute-start.33 = (f32[128,512]{1,0:T(8,128)S(1)}, f32[128,512]{1,0:T(8,128)S(1)}, u32[]{:S(2)}, u32[]{:S(2)}) collective-permute-start(f32[128,512]{1,0:T(8,128)S(1)} %collective-permute-done.20), channel_id=1, source_target_pairs={{0,24},{1,25},{2,26},{3,27},{4,28},{5,29},{6,30},{7,31},{8,32},{9,... | collective-permute-start | bytes 786440 | tf_op jit(solution)/shard_map/ppermute | solution.py:123
  461.8 33.1 %collective-permute-start.34 = (f32[128,512]{1,0:T(8,128)S(1)}, f32[128,512]{1,0:T(8,128)S(1)}, u32[]{:S(2)}, u32[]{:S(2)}) collective-permute-start(f32[128,512]{1,0:T(8,128)S(1)} %collective-permute-done.20), channel_id=1, source_target_pairs={{0,16},{1,17},{2,18},{3,19},{4,20},{5,21},{6,22},{7,23},{8,24},{9,... | collective-permute-start | bytes 786440 | tf_op jit(solution)/shard_map/ppermute | solution.py:123
  465.7 29.2 %collective-permute-start.35 = (f32[128,512]{1,0:T(8,128)S(1)}, f32[128,512]{1,0:T(8,128)S(1)}, u32[]{:S(2)}, u32[]{:S(2)}) collective-permute-start(f32[128,512]{1,0:T(8,128)S(1)} %collective-permute-done.20), channel_id=1, source_target_pairs={{0,8},{1,9},{2,10},{3,11},{4,12},{5,13},{6,14},{7,15},{8,16},{9,17... | collective-permute-start | bytes 786440 | tf_op jit(solution)/shard_map/ppermute | solution.py:123
  (14 other events, 121.4 us)

commit v10 on v8

--- a/solution.py
+++ b/solution.py
@@ -72,16 +72,21 @@
     )
     factor11 = jnp.linalg.cholesky(safe_block)
 
+    band = PANEL // 4
+    sent = tuple(factor11[i * band:(i + 1) * band, :(i + 1) * band] for i in range(4))
     group = 4 if row_count % 4 == 0 else 1
-    factor_col0 = factor11
+    held_l = sent
     for m in range(1, row_count // group):
-        got = lax.ppermute(factor11, ("row", "col"), [(0, m * group * col_count)])
-        factor_col0 = jnp.where(row_id == m * group, got, factor_col0)
-    lead = factor_col0
+        got = lax.ppermute(sent, ("row", "col"), [(0, m * group * col_count)])
+        held_l = tuple(jnp.where(row_id == m * group, g, h) for g, h in zip(got, held_l))
+    lead = held_l
     for z in range(1, group):
         perm = [(m * group * col_count, (m * group + z) * col_count) for m in range(row_count // group)]
         got = lax.ppermute(lead, ("row", "col"), perm)
-        factor_col0 = jnp.where(row_id % group == z, got, factor_col0)
+        held_l = tuple(jnp.where(row_id % group == z, g, h) for g, h in zip(got, held_l))
+    factor_col0 = jnp.concatenate(
+        [jnp.pad(p, ((0, 0), (0, PANEL - p.shape[1]))) for p in held_l], axis=0
+    )
 
     every = (landing[None, :] == jnp.arange(local_count, dtype=jnp.int32)[:, None]).astype(jnp.float32)
     delta = lax.dot_general(
@@ -97,7 +102,7 @@
     solved = lax.linalg.triangular_solve(
         factor_col0, panel_cols, left_side=False, lower=True, transpose_a=True
     )
-    headed = jnp.concatenate([factor_col0, solved[PANEL:]], axis=0)
+    headed = jnp.concatenate([factor11, solved[PANEL:]], axis=0)
     solved = jnp.where(first_rows, headed, solved)
     piece_rows = rows_dev // col_count
     my_piece = solved[:piece_rows]

time: 465 us -> 446 us (0.959)
  waiting for transfers between devices: 133 us -> 102 us
  starting transfers between devices: 51 us -> 66.9 us
  other arithmetic: 152 us -> 147 us
    ppermute x7, waiting for transfers between devices: 38.9 us -> 20.6 us  [shards(): lax.ppermute(solved[j * piece_rows:(j + 1) * piece_rows], ('row', 'col'),...]
    ppermute x1, waiting for transfers between devices: 23.6 us -> 9.48 us  [shards(): mine = lax.ppermute(my_piece, ('row', 'col'), perm)]
    ppermute x1, starting transfers between devices: 3.24 us -> 10.4 us  [shards(): mine = lax.ppermute(my_piece, ('row', 'col'), perm)]
  transfers between devices with their start and end apart: 23 -> 41, of which waited for: 6 -> 7; matrix products, arithmetic and copies ran while one was open for 5% -> 5% of each run, Pallas kernels for 0% -> 0%
where the time goes in v10:
time: 446 us; the launch traced here: 440 us
  other arithmetic  147 us (33%)
  waiting for transfers between devices  102 us (23%)
  starting transfers between devices  66.9 us (15%)
  local copies, waits for them, and re-layouts  59.5 us (13%)
  matrix products  45.8 us (10%)
  between operations  18 us (4%)
    another operation x14, other arithmetic, shards(): factor11 = jnp.linalg.cholesky(safe_block)  79 us
    all_to_all x1, waiting for transfers between devices, shards(): lax.all_to_all(outgoing.reshape(devices, capacity * width), ('row', 'col'...  50.5 us
    another operation x4, other arithmetic, shards(): lax.linalg.triangular_solve(factor_col0, panel_cols, left_side=False, low...  41.6 us
    ppermute x7, waiting for transfers between devices, shards(): lax.ppermute(solved[j * piece_rows:(j + 1) * piece_rows], ('row', 'col'),...  20.6 us
    ppermute x7, waiting for transfers between devices, shards(): shifted.append(lax.ppermute(my_piece, ('row', 'col'), perm))  20.5 us
    ppermute x7, starting transfers between devices, shards(): shifted.append(lax.ppermute(my_piece, ('row', 'col'), perm))  19.4 us
    dot_general x1, matrix products, shards(): lax.dot_general(panel_here, column_panel, (((1,), (1,)), ((), ())), preci...  16.6 us
    all_to_all x1, other arithmetic, shards(): lax.all_to_all(outgoing.reshape(devices, capacity * width), ('row', 'col'...  14 us
  transfers between devices with their start and end apart: 41, of which 7 were waited for; matrix products, arithmetic and copies ran while one was open for 5% of the time, Pallas kernels for 0%

profile of v10, /device:TPU:1, one launch (start us, length us, event | category | flops | bytes accessed | tf_op | source)
XLA Modules:
  0.0 439.9 jit_solution(16980719214403848207)
XLA Ops:
  9.4 3.2 copy.80
  12.7 3.9 fusion.8
  16.6 7.2 %all_to_all.8 = f32[128,1,8448]{2,1,0:T(1,128)} reshape(f32[256,4224]{1,0:T(8,128)} %fusion.8) | data formatting | bytes 8650752 | tf_op jit(solution)/shard_map/all_to_all | solution.py:39
  23.8 11.9 %all-to-all-start = ((f32[128,1,8448]{2,1,0:T(1,128)}), f32[128,1,8448]{2,1,0:T(1,128)}, u32[]{:S(2)}, u32[]{:S(2)}) async-start(f32[128,1,8448]{2,1,0:T(1,128)} %all_to_all.8), calls=%async_computation | async-start | bytes 8650752 | tf_op jit(solution)/shard_map/all_to_all | solution.py:39
  39.1 50.5 %all-to-all-done = f32[128,1,8448]{2,1,0:T(1,128)} async-done(((f32[128,1,8448]{2,1,0:T(1,128)}), f32[128,1,8448]{2,1,0:T(1,128)}, u32[]{:S(2)}, u32[]{:S(2)}) %all-to-all-start) | async-done | bytes 4325408 | tf_op jit(solution)/shard_map/all_to_all | solution.py:39
  89.7 14.0 %reduce.24 = f32[128,8448]{1,0:T(8,128)} reduce(f32[128,1,8448]{2,1,0:T(1,128)} %all-to-all-done, f32[]{:T(128)} %constant.276), dimensions={1}, to_apply=%all_to_all.7.reduce_sub_computation | reduce | bytes 8650756 | tf_op jit(solution)/shard_map/all_to_all | solution.py:39
  103.6 5.0 %reshape.140 = f32[256,4224]{1,0:T(8,128)} reshape(f32[128,8448]{1,0:T(8,128)} %reduce.24) | data formatting | bytes 8650752 | tf_op jit(solution)/shard_map/reshape | solution.py:45
  109.7 3.9 fusion.12
  116.0 2.2 copy.56
  118.2 2.6 add.150
  127.4 11.7 %cholesky.104 = f32[128,128]{1,0:T(8,128)S(1)} custom-call(f32[128,128]{1,0:T(8,128)S(1)} %cholesky.266), custom_call_target="Cholesky" | custom-call | tf_op jit(solution)/shard_map/jit(cholesky)/cholesky | solution.py:73
  139.2 9.8 %custom-call.30 = f32[1,128,128]{1,2,0:T(8,128)S(1)} custom-call(f32[1,128,128]{2,1,0:T(8,128)S(1)} %get-tuple-element.38), custom_call_target="InvertDiagBlocksLowerTriangular" | custom-call | tf_op jit(solution)/shard_map/jit(cholesky)/cholesky | solution.py:73
  151.6 11.7 %cholesky.217 = f32[128,128]{1,0:T(8,128)S(1)} custom-call(f32[128,128]{1,0:T(8,128)S(1)} %cholesky.270), custom_call_target="Cholesky" | custom-call | tf_op jit(solution)/shard_map/jit(cholesky)/cholesky | solution.py:73
  163.4 10.0 %custom-call.31 = f32[1,128,128]{1,2,0:T(8,128)S(1)} custom-call(f32[1,128,128]{2,1,0:T(8,128)S(1)} %get-tuple-element.35), custom_call_target="InvertDiagBlocksLowerTriangular" | custom-call | tf_op jit(solution)/shard_map/jit(cholesky)/cholesky | solution.py:73
  174.9 11.7 %cholesky.238 = f32[128,128]{1,0:T(8,128)S(1)} custom-call(f32[128,128]{1,0:T(8,128)S(1)} %cholesky.275), custom_call_target="Cholesky" | custom-call | tf_op jit(solution)/shard_map/jit(cholesky)/cholesky | solution.py:73
  187.4 9.8 %custom-call.32 = f32[1,128,128]{1,2,0:T(8,128)S(1)} custom-call(f32[1,128,128]{2,1,0:T(8,128)S(1)} %get-tuple-element.32), custom_call_target="InvertDiagBlocksLowerTriangular" | custom-call | tf_op jit(solution)/shard_map/jit(cholesky)/cholesky | solution.py:73
  198.6 12.1 %cholesky.255 = f32[128,128]{1,0:T(8,128)S(1)} custom-call(f32[128,128]{1,0:T(8,128)S(1)} %convolution_subtract_fusion.4), custom_call_target="Cholesky" | custom-call | tf_op jit(solution)/shard_map/jit(cholesky)/cholesky | solution.py:73
  232.1 10.9 %while.1 = (s32[]{:T(128)}, f32[512,512]{1,0:T(8,128)S(1)}, s32[4,2]{0,1:T(2,128)S(1)}, f32[4,128,128]{2,1,0:T(8,128)}, s32[]{:T(128)}) while((s32[]{:T(128)}, f32[512,512]{1,0:T(8,128)S(1)}, s32[4,2]{0,1:T(2,128)S(1)}, f32[4,128,128]{2,1,0:T(8,128)}, s32[]{:T(128)}) %tuple.38), condition=%wide.while_cond, body=%wide.while_body.sunk | while | flops 2 | bytes 132205 | solution.py:102
  243.9 40.1 %custom-call.33 = f32[4,128,128]{1,2,0:T(8,128)S(1)} custom-call(f32[4,128,128]{2,1,0:T(8,128)} %get-tuple-element.9), custom_call_target="InvertDiagBlocksLowerTriangular" | custom-call | tf_op jit(solution)/shard_map/triangular_solve | solution.py:102
  291.9 2.9 fusion.21
  296.1 2.2 fusion.52
  307.6 20.6 %collective-permute-done.30 = f32[128,512]{1,0:T(8,128)S(1)} collective-permute-done((f32[128,512]{1,0:T(8,128)S(1)}, f32[128,512]{1,0:T(8,128)S(1)}, u32[]{:S(2)}, u32[]{:S(2)}) %collective-permute-start.30) | collective-permute-done | bytes 262176 | tf_op jit(solution)/shard_map/ppermute | solution.py:111
  333.7 10.4 %collective-permute-start.38 = (f32[128,512]{1,0:T(8,128)S(1)}, f32[128,512]{1,0:T(8,128)S(1)}, u32[]{:S(2)}, u32[]{:S(2)}) collective-permute-start(f32[128,512]{1,0:T(8,128)S(1)} %get-tuple-element.19), channel_id=1, source_target_pairs={{0,0},{1,8},{2,16},{3,24},{4,32},{5,40},{6,48},{7,56},{8,64},{9,72... | collective-permute-start | bytes 786440 | tf_op jit(solution)/shard_map/ppermute | solution.py:120
  344.0 9.5 %collective-permute-done.38 = f32[128,512]{1,0:T(8,128)S(1)} collective-permute-done((f32[128,512]{1,0:T(8,128)S(1)}, f32[128,512]{1,0:T(8,128)S(1)}, u32[]{:S(2)}, u32[]{:S(2)}) %collective-permute-start.38) | collective-permute-done | bytes 262176 | tf_op jit(solution)/shard_map/ppermute | solution.py:120
  354.3 5.9 %fusion.5 = f32[64,8,32,128]{3,1,2,0:T(8,128)S(1)} fusion(f32[256,4224]{1,0:T(8,128)} %reshape.140, s32[256]{0:T(256)S(1)} %select_reduce_fusion), kind=kOutput, calls=%fused_computation.9 | convolution fusion | flops 6442582016 | bytes 12583936 | tf_op jit(solution)/shard_map/dot_general | solution.py:92
  362.0 12.4 %collective-permute-start.32 = (f32[128,512]{1,0:T(8,128)S(1)}, f32[128,512]{1,0:T(8,128)S(1)}, u32[]{:S(2)}, u32[]{:S(2)}) collective-permute-start(f32[128,512]{1,0:T(8,128)S(1)} %get-tuple-element.19), channel_id=1, source_target_pairs={{0,6},{1,7},{2,0},{3,1},{4,2},{5,3},{6,4},{7,5},{8,14},{9,15},{10,... | collective-permute-start | bytes 786440 | tf_op jit(solution)/shard_map/ppermute | solution.py:129
  376.0 10.9 %copy.53 = f32[32,32,16,128]{3,2,1,0:T(8,128)} copy(f32[32,32,16,128]{3,1,2,0:T(8,128)S(1)} %bitcast_bitcast_fusion) | data formatting | bytes 16777216 | tf_op jit(solution)/shard_map/transpose | solution.py:99
  391.7 2.3 collective-permute-start.34
  394.0 13.8 %collective-permute-done.33 = f32[128,512]{1,0:T(8,128)S(1)} collective-permute-done((f32[128,512]{1,0:T(8,128)S(1)}, f32[128,512]{1,0:T(8,128)S(1)}, u32[]{:S(2)}, u32[]{:S(2)}) %collective-permute-start.33) | collective-permute-done | bytes 262176 | tf_op jit(solution)/shard_map/ppermute | solution.py:129
  407.9 4.5 %collective-permute-done.34 = f32[128,512]{1,0:T(8,128)S(1)} collective-permute-done((f32[128,512]{1,0:T(8,128)S(1)}, f32[128,512]{1,0:T(8,128)S(1)}, u32[]{:S(2)}, u32[]{:S(2)}) %collective-permute-start.34) | collective-permute-done | bytes 262176 | tf_op jit(solution)/shard_map/ppermute | solution.py:129
  412.4 2.2 collective-permute-done.35
  416.2 16.6 %fusion = f32[1024,2048]{1,0:T(8,128)} fusion(f32[1024,2048]{1,0:T(8,128)} %param.4, f32[128,8,16,128]{3,2,1,0:T(8,128)} %bitcast.111, pred[2048]{0:T(1024)(128)(4,1)S(1)} %add_compare_fusion, pred[1024]{0:T(1024)(128)(4,1)S(1)} %add_compare_fusion.1, f32[1024,512]{1,0:T(8,128)S(1)} %bitcast.113, f32[2048,512]{1,0:T(8,128)} %all-gather.2.cloned.1.call-done), kind=kOutput, calls=%fused_computation.3 | convolution fusion | flops 6450839552 | bytes 31460352 | tf_op jit(solution)/shard_map/dot_general | solution.py:133
  (195 shorter events, 86.2 us)
Async XLA Ops:
  23.8 65.8 %all-to-all-start = ((f32[128,1,8448]{2,1,0:T(1,128)}), f32[128,1,8448]{2,1,0:T(1,128)}, u32[]{:S(2)}, u32[]{:S(2)}) async-start(f32[128,1,8448]{2,1,0:T(1,128)} %all_to_all.8), calls=%async_computation | async-start | bytes 8650752 | tf_op jit(solution)/shard_map/all_to_all | solution.py:39
  35.7 380.5 %all-gather.2.cloned.1.call-start = ((), (), s32[]{:S(2)}) async-start(), calls=%async_computation.1 | async-start | bytes 4456448 | tf_op jit(solution)/shard_map/all_gather | solution.py:121
  215.5 3.5 collective-permute-start.1
  216.2 3.5 collective-permute-start
  216.9 3.5 collective-permute-start.8
  217.6 3.5 collective-permute-start.7
  218.3 3.5 collective-permute-start.6
  219.0 5.6 %collective-permute-start.14 = (f32[128,384]{1,0:T(8,128)S(1)}, f32[128,384]{1,0:T(8,128)S(1)}, u32[]{:S(2)}, u32[]{:S(2)}) collective-permute-start(f32[128,384]{1,0:T(8,128)S(1)} %slice.187), channel_id=1, source_target_pairs={{0,32}} | collective-permute-start | bytes 589832 | tf_op jit(solution)/shard_map/ppermute | solution.py:80
  219.7 5.6 %collective-permute-start.13 = (f32[128,384]{1,0:T(8,128)S(1)}, f32[128,384]{1,0:T(8,128)S(1)}, u32[]{:S(2)}, u32[]{:S(2)}) collective-permute-start(f32[128,384]{1,0:T(8,128)S(1)} %slice.187), channel_id=1, source_target_pairs={{0,64}} | collective-permute-start | bytes 589832 | tf_op jit(solution)/shard_map/ppermute | solution.py:80
  222.5 3.5 collective-permute-start.12
  223.2 3.5 collective-permute-start.20
  223.9 3.5 collective-permute-start.19
  224.6 3.5 collective-permute-start.18
  225.3 3.6 collective-permute-start.11
  226.0 3.6 collective-permute-start.10
  226.7 3.6 collective-permute-start.9
  227.4 3.6 collective-permute-start.17
  228.1 3.6 collective-permute-start.16
  301.5 26.7 %collective-permute-start.30 = (f32[128,512]{1,0:T(8,128)S(1)}, f32[128,512]{1,0:T(8,128)S(1)}, u32[]{:S(2)}, u32[]{:S(2)}) collective-permute-start(f32[128,512]{1,0:T(8,128)S(1)} %get-tuple-element.22), channel_id=1, source_target_pairs={{0,1},{8,9},{16,17},{24,25},{32,33},{40,41},{48,49},{56,57},{64,65... | collective-permute-start | bytes 786440 | tf_op jit(solution)/shard_map/ppermute | solution.py:111
  302.8 26.8 %collective-permute-start.29 = (f32[128,512]{1,0:T(8,128)S(1)}, f32[128,512]{1,0:T(8,128)S(1)}, u32[]{:S(2)}, u32[]{:S(2)}) collective-permute-start(f32[128,512]{1,0:T(8,128)S(1)} %get-tuple-element.23), channel_id=1, source_target_pairs={{0,2},{8,10},{16,18},{24,26},{32,34},{40,42},{48,50},{56,58},{64,6... | collective-permute-start | bytes 786440 | tf_op jit(solution)/shard_map/ppermute | solution.py:111
  303.5 28.2 %collective-permute-start.28 = (f32[128,512]{1,0:T(8,128)S(1)}, f32[128,512]{1,0:T(8,128)}, u32[]{:S(2)}, u32[]{:S(2)}) collective-permute-start(f32[128,512]{1,0:T(8,128)S(1)} %get-tuple-element.24), channel_id=1, source_target_pairs={{0,3},{8,11},{16,19},{24,27},{32,35},{40,43},{48,51},{56,59},{64,6... | collective-permute-start | bytes 786440 | tf_op jit(solution)/shard_map/ppermute | solution.py:111
  304.9 26.8 %collective-permute-start.27 = (f32[128,512]{1,0:T(8,128)S(1)}, f32[128,512]{1,0:T(8,128)}, u32[]{:S(2)}, u32[]{:S(2)}) collective-permute-start(f32[128,512]{1,0:T(8,128)S(1)} %get-tuple-element.25), channel_id=1, source_target_pairs={{0,4},{8,12},{16,20},{24,28},{32,36},{40,44},{48,52},{56,60},{64,6... | collective-permute-start | bytes 786440 | tf_op jit(solution)/shard_map/ppermute | solution.py:111
  306.2 25.5 %collective-permute-start.26 = (f32[128,512]{1,0:T(8,128)S(1)}, f32[128,512]{1,0:T(8,128)}, u32[]{:S(2)}, u32[]{:S(2)}) collective-permute-start(f32[128,512]{1,0:T(8,128)S(1)} %get-tuple-element.26), channel_id=1, source_target_pairs={{0,5},{8,13},{16,21},{24,29},{32,37},{40,45},{48,53},{56,61},{64,6... | collective-permute-start | bytes 786440 | tf_op jit(solution)/shard_map/ppermute | solution.py:111
  328.3 3.5 collective-permute-start.25
  333.7 19.9 %collective-permute-start.38 = (f32[128,512]{1,0:T(8,128)S(1)}, f32[128,512]{1,0:T(8,128)S(1)}, u32[]{:S(2)}, u32[]{:S(2)}) collective-permute-start(f32[128,512]{1,0:T(8,128)S(1)} %get-tuple-element.19), channel_id=1, source_target_pairs={{0,0},{1,8},{2,16},{3,24},{4,32},{5,40},{6,48},{7,56},{8,64},{9,72... | collective-permute-start | bytes 786440 | tf_op jit(solution)/shard_map/ppermute | solution.py:120
  362.0 29.6 %collective-permute-start.32 = (f32[128,512]{1,0:T(8,128)S(1)}, f32[128,512]{1,0:T(8,128)S(1)}, u32[]{:S(2)}, u32[]{:S(2)}) collective-permute-start(f32[128,512]{1,0:T(8,128)S(1)} %get-tuple-element.19), channel_id=1, source_target_pairs={{0,6},{1,7},{2,0},{3,1},{4,2},{5,3},{6,4},{7,5},{8,14},{9,15},{10,... | collective-permute-start | bytes 786440 | tf_op jit(solution)/shard_map/ppermute | solution.py:129
  374.4 15.2 %collective-permute-start.31 = (f32[128,512]{1,0:T(8,128)S(1)}, f32[128,512]{1,0:T(8,128)S(1)}, u32[]{:S(2)}, u32[]{:S(2)}) collective-permute-start(f32[128,512]{1,0:T(8,128)S(1)} %get-tuple-element.19), channel_id=1, source_target_pairs={{0,7},{1,0},{2,1},{3,2},{4,3},{5,4},{6,5},{7,6},{8,15},{9,8},{10,9... | collective-permute-start | bytes 786440 | tf_op jit(solution)/shard_map/ppermute | solution.py:129
  386.9 27.7 %collective-permute-start.37 = (f32[128,512]{1,0:T(8,128)S(1)}, f32[128,512]{1,0:T(8,128)S(1)}, u32[]{:S(2)}, u32[]{:S(2)}) collective-permute-start(f32[128,512]{1,0:T(8,128)S(1)} %get-tuple-element.19), channel_id=1, source_target_pairs={{0,1},{1,2},{2,3},{3,4},{4,5},{5,6},{6,7},{7,0},{8,9},{9,10},{10,1... | collective-permute-start | bytes 786440 | tf_op jit(solution)/shard_map/ppermute | solution.py:129
  388.7 25.9 %collective-permute-start.36 = (f32[128,512]{1,0:T(8,128)S(1)}, f32[128,512]{1,0:T(8,128)S(1)}, u32[]{:S(2)}, u32[]{:S(2)}) collective-permute-start(f32[128,512]{1,0:T(8,128)S(1)} %get-tuple-element.19), channel_id=1, source_target_pairs={{0,2},{1,3},{2,4},{3,5},{4,6},{5,7},{6,0},{7,1},{8,10},{9,11},{10,... | collective-permute-start | bytes 786440 | tf_op jit(solution)/shard_map/ppermute | solution.py:129
  388.7 25.9 %collective-permute-start.35 = (f32[128,512]{1,0:T(8,128)S(1)}, f32[128,512]{1,0:T(8,128)S(1)}, u32[]{:S(2)}, u32[]{:S(2)}) collective-permute-start(f32[128,512]{1,0:T(8,128)S(1)} %get-tuple-element.19), channel_id=1, source_target_pairs={{0,3},{1,4},{2,5},{3,6},{4,7},{5,0},{6,1},{7,2},{8,11},{9,12},{10,... | collective-permute-start | bytes 786440 | tf_op jit(solution)/shard_map/ppermute | solution.py:129
  389.7 18.2 %collective-permute-start.33 = (f32[128,512]{1,0:T(8,128)S(1)}, f32[128,512]{1,0:T(8,128)S(1)}, u32[]{:S(2)}, u32[]{:S(2)}) collective-permute-start(f32[128,512]{1,0:T(8,128)S(1)} %get-tuple-element.19), channel_id=1, source_target_pairs={{0,5},{1,6},{2,7},{3,0},{4,1},{5,2},{6,3},{7,4},{8,13},{9,14},{10,... | collective-permute-start | bytes 786440 | tf_op jit(solution)/shard_map/ppermute | solution.py:129
  391.7 20.7 %collective-permute-start.34 = (f32[128,512]{1,0:T(8,128)S(1)}, f32[128,512]{1,0:T(8,128)S(1)}, u32[]{:S(2)}, u32[]{:S(2)}) collective-permute-start(f32[128,512]{1,0:T(8,128)S(1)} %get-tuple-element.19), channel_id=1, source_target_pairs={{0,4},{1,5},{2,6},{3,7},{4,0},{5,1},{6,2},{7,3},{8,12},{9,13},{10,... | collective-permute-start | bytes 786440 | tf_op jit(solution)/shard_map/ppermute | solution.py:129
  (23 other events, 89.4 us)
Sparse Core Ops, SparseCore 0:
  354.4 61.8 all-gather.1

commit v11 on v10

--- a/solution.py
+++ b/solution.py
@@ -72,18 +72,26 @@
     )
     factor11 = jnp.linalg.cholesky(safe_block)
 
-    band = PANEL // 4
-    sent = tuple(factor11[i * band:(i + 1) * band, :(i + 1) * band] for i in range(4))
+    bands = 8
+    band = PANEL // bands
+    sent = tuple(factor11[i * band:(i + 1) * band, :(i + 1) * band] for i in range(bands))
     group = 4 if row_count % 4 == 0 else 1
+    relay = 1 if col_count > 1 and group > 1 else 0
     held_l = sent
+    if relay:
+        got = lax.ppermute(sent, ("row", "col"), [(0, relay)])
+        held_l = tuple(jnp.where(col_id == relay, g, h) for g, h in zip(got, held_l))
     for m in range(1, row_count // group):
         got = lax.ppermute(sent, ("row", "col"), [(0, m * group * col_count)])
         held_l = tuple(jnp.where(row_id == m * group, g, h) for g, h in zip(got, held_l))
     lead = held_l
     for z in range(1, group):
-        perm = [(m * group * col_count, (m * group + z) * col_count) for m in range(row_count // group)]
+        perm = [
+            (relay if m == 0 else m * group * col_count, (m * group + z) * col_count)
+            for m in range(row_count // group)
+        ]
         got = lax.ppermute(lead, ("row", "col"), perm)
-        held_l = tuple(jnp.where(row_id % group == z, g, h) for g, h in zip(got, held_l))
+        held_l = tuple(jnp.where((row_id % group == z) & (col_id == 0), g, h) for g, h in zip(got, held_l))
     factor_col0 = jnp.concatenate(
         [jnp.pad(p, ((0, 0), (0, PANEL - p.shape[1]))) for p in held_l], axis=0
     )

time: 446 us -> 492 us (1.10)
  starting transfers between devices: 66.9 us -> 112 us
    ppermute x12 -> x24, starting transfers between devices: 8.05 us -> 35.7 us  [shards(): got = lax.ppermute(lead, ('row', 'col'), perm)]
    ppermute x7, waiting for transfers between devices: 20.6 us -> 0.02 us  [shards(): lax.ppermute(solved[j * piece_rows:(j + 1) * piece_rows], ('row', 'col'),...]
    ppermute x0 -> x8, waiting for transfers between devices: none -> 16.1 us  [shards(): got = lax.ppermute(sent, ('row', 'col'), [(0, relay)])]
    ppermute x0 -> x8, starting transfers between devices: none -> 10.3 us  [shards(): got = lax.ppermute(sent, ('row', 'col'), [(0, relay)])]
    ppermute x12 -> x24, starting transfers between devices: 8.05 us -> 15.9 us  [shards(): got = lax.ppermute(sent, ('row', 'col'), [(0, m * group * col_count)])]
    unnamed x45 -> x50, local copies, waits for them, and re-layouts: 11.9 us -> 13.8 us
  transfers between devices with their start and end apart: 41 -> 73, of which waited for: 7 -> 11; matrix products, arithmetic and copies ran while one was open for 5% -> 5% of each run, Pallas kernels for 0% -> 0%
where the time goes in v11:
time: 492 us; the launch traced here: 486 us
  other arithmetic  148 us (30%)
  starting transfers between devices  112 us (23%)
  waiting for transfers between devices  99 us (20%)
  local copies, waits for them, and re-layouts  62.6 us (13%)
  matrix products  45.6 us (9%)
  between operations  18.7 us (4%)
    another operation x14, other arithmetic, shards(): factor11 = jnp.linalg.cholesky(safe_block)  79.1 us
    all_to_all x1, waiting for transfers between devices, shards(): lax.all_to_all(outgoing.reshape(devices, capacity * width), ('row', 'col'...  50.5 us
    another operation x4, other arithmetic, shards(): lax.linalg.triangular_solve(factor_col0, panel_cols, left_side=False, low...  41.6 us
    ppermute x24, starting transfers between devices, shards(): got = lax.ppermute(lead, ('row', 'col'), perm)  35.7 us
    ppermute x7, starting transfers between devices, shards(): shifted.append(lax.ppermute(my_piece, ('row', 'col'), perm))  21.6 us
    ppermute x7, waiting for transfers between devices, shards(): shifted.append(lax.ppermute(my_piece, ('row', 'col'), perm))  20.5 us
    dot_general x1, matrix products, shards(): lax.dot_general(panel_here, column_panel, (((1,), (1,)), ((), ())), preci...  16.6 us
    ppermute x8, waiting for transfers between devices, shards(): got = lax.ppermute(sent, ('row', 'col'), [(0, relay)])  16.1 us
  transfers between devices with their start and end apart: 73, of which 11 were waited for; matrix products, arithmetic and copies ran while one was open for 5% of the time, Pallas kernels for 0%

profile of v11, /device:TPU:1, one launch (start us, length us, event | category | flops | bytes accessed | tf_op | source)
XLA Modules:
  0.0 485.6 jit_solution(16997440891115897001)
XLA Ops:
  9.4 3.2 copy.80
  12.7 3.9 fusion.8
  16.6 7.2 %all_to_all.8 = f32[128,1,8448]{2,1,0:T(1,128)} reshape(f32[256,4224]{1,0:T(8,128)} %fusion.8) | data formatting | bytes 8650752 | tf_op jit(solution)/shard_map/all_to_all | solution.py:39
  23.8 11.9 %all-to-all-start = ((f32[128,1,8448]{2,1,0:T(1,128)}), f32[128,1,8448]{2,1,0:T(1,128)}, u32[]{:S(2)}, u32[]{:S(2)}) async-start(f32[128,1,8448]{2,1,0:T(1,128)} %all_to_all.8), calls=%async_computation | async-start | bytes 8650752 | tf_op jit(solution)/shard_map/all_to_all | solution.py:39
  39.1 50.5 %all-to-all-done = f32[128,1,8448]{2,1,0:T(1,128)} async-done(((f32[128,1,8448]{2,1,0:T(1,128)}), f32[128,1,8448]{2,1,0:T(1,128)}, u32[]{:S(2)}, u32[]{:S(2)}) %all-to-all-start) | async-done | bytes 4325408 | tf_op jit(solution)/shard_map/all_to_all | solution.py:39
  89.7 14.0 %reduce.24 = f32[128,8448]{1,0:T(8,128)} reduce(f32[128,1,8448]{2,1,0:T(1,128)} %all-to-all-done, f32[]{:T(128)} %constant.308), dimensions={1}, to_apply=%all_to_all.7.reduce_sub_computation | reduce | bytes 8650756 | tf_op jit(solution)/shard_map/all_to_all | solution.py:39
  103.7 5.0 %reshape.140 = f32[256,4224]{1,0:T(8,128)} reshape(f32[128,8448]{1,0:T(8,128)} %reduce.24) | data formatting | bytes 8650752 | tf_op jit(solution)/shard_map/reshape | solution.py:45
  109.7 3.9 fusion.12
  117.3 3.4 copy.56
  130.1 11.7 %cholesky.104 = f32[128,128]{1,0:T(8,128)S(1)} custom-call(f32[128,128]{1,0:T(8,128)S(1)} %cholesky.266), custom_call_target="Cholesky" | custom-call | tf_op jit(solution)/shard_map/jit(cholesky)/cholesky | solution.py:73
  141.8 9.8 %custom-call.30 = f32[1,128,128]{1,2,0:T(8,128)S(1)} custom-call(f32[1,128,128]{2,1,0:T(8,128)S(1)} %get-tuple-element.38), custom_call_target="InvertDiagBlocksLowerTriangular" | custom-call | tf_op jit(solution)/shard_map/jit(cholesky)/cholesky | solution.py:73
  154.3 11.7 %cholesky.217 = f32[128,128]{1,0:T(8,128)S(1)} custom-call(f32[128,128]{1,0:T(8,128)S(1)} %cholesky.270), custom_call_target="Cholesky" | custom-call | tf_op jit(solution)/shard_map/jit(cholesky)/cholesky | solution.py:73
  166.0 10.0 %custom-call.31 = f32[1,128,128]{1,2,0:T(8,128)S(1)} custom-call(f32[1,128,128]{2,1,0:T(8,128)S(1)} %get-tuple-element.35), custom_call_target="InvertDiagBlocksLowerTriangular" | custom-call | tf_op jit(solution)/shard_map/jit(cholesky)/cholesky | solution.py:73
  177.6 11.7 %cholesky.238 = f32[128,128]{1,0:T(8,128)S(1)} custom-call(f32[128,128]{1,0:T(8,128)S(1)} %cholesky.275), custom_call_target="Cholesky" | custom-call | tf_op jit(solution)/shard_map/jit(cholesky)/cholesky | solution.py:73
  190.0 9.8 %custom-call.32 = f32[1,128,128]{1,2,0:T(8,128)S(1)} custom-call(f32[1,128,128]{2,1,0:T(8,128)S(1)} %get-tuple-element.32), custom_call_target="InvertDiagBlocksLowerTriangular" | custom-call | tf_op jit(solution)/shard_map/jit(cholesky)/cholesky | solution.py:73
  201.3 12.1 %cholesky.255 = f32[128,128]{1,0:T(8,128)S(1)} custom-call(f32[128,128]{1,0:T(8,128)S(1)} %convolution_subtract_fusion.4), custom_call_target="Cholesky" | custom-call | tf_op jit(solution)/shard_map/jit(cholesky)/cholesky | solution.py:73
  235.7 6.0 %collective-permute-done.17 = f32[64,192]{1,0:T(8,128)S(1)} collective-permute-done((f32[64,192]{1,0:T(8,128)S(1)}, f32[64,192]{1,0:T(8,128)S(1)}, u32[]{:S(2)}, u32[]{:S(2)}) %collective-permute-start.17) | collective-permute-done | bytes 49184 | tf_op jit(solution)/shard_map/ppermute | solution.py:82
  252.4 4.9 %collective-permute-done.31 = f32[64,320]{1,0:T(8,128)S(1)} collective-permute-done((f32[64,320]{1,0:T(8,128)S(1)}, f32[64,320]{1,0:T(8,128)S(1)}, u32[]{:S(2)}, u32[]{:S(2)}) %collective-permute-start.31) | collective-permute-done | bytes 81952 | tf_op jit(solution)/shard_map/ppermute | solution.py:82
  268.1 5.2 %collective-permute-done.45 = f32[64,448]{1,0:T(8,128)S(1)} collective-permute-done((f32[64,448]{1,0:T(8,128)S(1)}, f32[64,448]{1,0:T(8,128)S(1)}, u32[]{:S(2)}, u32[]{:S(2)}) %collective-permute-start.45) | collective-permute-done | bytes 114720 | tf_op jit(solution)/shard_map/ppermute | solution.py:82
  279.3 2.9 collective-permute-start.34
  300.6 10.7 %while.1 = (s32[]{:T(128)}, f32[512,512]{1,0:T(8,128)S(1)}, s32[4,2]{0,1:T(2,128)S(1)}, f32[4,128,128]{2,1,0:T(8,128)}, s32[]{:T(128)}) while((s32[]{:T(128)}, f32[512,512]{1,0:T(8,128)S(1)}, s32[4,2]{0,1:T(2,128)S(1)}, f32[4,128,128]{2,1,0:T(8,128)}, s32[]{:T(128)}) %tuple.38), condition=%wide.while_cond, body=%wide.while_body.sunk | while | flops 2 | bytes 132205 | solution.py:110
  312.3 40.1 %custom-call.33 = f32[4,128,128]{1,2,0:T(8,128)S(1)} custom-call(f32[4,128,128]{2,1,0:T(8,128)} %get-tuple-element.9), custom_call_target="InvertDiagBlocksLowerTriangular" | custom-call | tf_op jit(solution)/shard_map/triangular_solve | solution.py:110
  360.2 2.9 fusion.21
  377.3 11.1 %collective-permute-start.70 = (f32[128,512]{1,0:T(8,128)S(1)}, f32[128,512]{1,0:T(8,128)S(1)}, u32[]{:S(2)}, u32[]{:S(2)}) collective-permute-start(f32[128,512]{1,0:T(8,128)S(1)} %get-tuple-element.19), channel_id=1, source_target_pairs={{0,0},{1,8},{2,16},{3,24},{4,32},{5,40},{6,48},{7,56},{8,64},{9,72... | collective-permute-start | bytes 786440 | tf_op jit(solution)/shard_map/ppermute | solution.py:128
  388.4 6.9 %collective-permute-done.70 = f32[128,512]{1,0:T(8,128)S(1)} collective-permute-done((f32[128,512]{1,0:T(8,128)S(1)}, f32[128,512]{1,0:T(8,128)S(1)}, u32[]{:S(2)}, u32[]{:S(2)}) %collective-permute-start.70) | collective-permute-done | bytes 262176 | tf_op jit(solution)/shard_map/ppermute | solution.py:128
  396.1 5.9 %fusion.5 = f32[64,8,32,128]{3,1,2,0:T(8,128)S(1)} fusion(f32[256,4224]{1,0:T(8,128)} %reshape.140, s32[256]{0:T(256)S(1)} %select_reduce_fusion), kind=kOutput, calls=%fused_computation.9 | convolution fusion | flops 6442582016 | bytes 12583936 | tf_op jit(solution)/shard_map/dot_general | solution.py:100
  403.8 14.7 %collective-permute-start.64 = (f32[128,512]{1,0:T(8,128)S(1)}, f32[128,512]{1,0:T(8,128)S(1)}, u32[]{:S(2)}, u32[]{:S(2)}) collective-permute-start(f32[128,512]{1,0:T(8,128)S(1)} %get-tuple-element.19), channel_id=1, source_target_pairs={{0,6},{1,7},{2,0},{3,1},{4,2},{5,3},{6,4},{7,5},{8,14},{9,15},{10,... | collective-permute-start | bytes 786440 | tf_op jit(solution)/shard_map/ppermute | solution.py:137
  420.1 10.9 %copy.53 = f32[32,32,16,128]{3,2,1,0:T(8,128)} copy(f32[32,32,16,128]{3,1,2,0:T(8,128)S(1)} %bitcast_bitcast_fusion) | data formatting | bytes 16777216 | tf_op jit(solution)/shard_map/transpose | solution.py:107
  438.0 13.8 %collective-permute-done.65 = f32[128,512]{1,0:T(8,128)S(1)} collective-permute-done((f32[128,512]{1,0:T(8,128)S(1)}, f32[128,512]{1,0:T(8,128)S(1)}, u32[]{:S(2)}, u32[]{:S(2)}) %collective-permute-start.65) | collective-permute-done | bytes 262176 | tf_op jit(solution)/shard_map/ppermute | solution.py:137
  451.8 4.5 collective-permute-done.66
  459.1 2.9 all-gather.2.cloned.1.call-done
  462.0 16.6 %fusion = f32[1024,2048]{1,0:T(8,128)} fusion(f32[1024,2048]{1,0:T(8,128)} %param.4, f32[128,8,16,128]{3,2,1,0:T(8,128)} %bitcast.111, pred[2048]{0:T(1024)(128)(4,1)S(1)} %add_compare_fusion, pred[1024]{0:T(1024)(128)(4,1)S(1)} %add_compare_fusion.1, f32[1024,512]{1,0:T(8,128)S(1)} %bitcast.113, f32[2048,512]{1,0:T(8,128)} %all-gather.2.cloned.1.call-done), kind=kOutput, calls=%fused_computation.3 | convolution fusion | flops 6450839552 | bytes 31460352 | tf_op jit(solution)/shard_map/dot_general | solution.py:141
  (276 shorter events, 137.8 us)
Async XLA Ops:
  23.8 65.8 %all-to-all-start = ((f32[128,1,8448]{2,1,0:T(1,128)}), f32[128,1,8448]{2,1,0:T(1,128)}, u32[]{:S(2)}, u32[]{:S(2)}) async-start(f32[128,1,8448]{2,1,0:T(1,128)} %all_to_all.8), calls=%async_computation | async-start | bytes 8650752 | tf_op jit(solution)/shard_map/all_to_all | solution.py:39
  35.7 426.2 %all-gather.2.cloned.1.call-start = ((), (), s32[]{:S(2)}) async-start(), calls=%async_computation.1 | async-start | bytes 4456448 | tf_op jit(solution)/shard_map/all_gather | solution.py:129
  230.9 10.7 %collective-permute-start.17 = (f32[64,192]{1,0:T(8,128)S(1)}, f32[64,192]{1,0:T(8,128)S(1)}, u32[]{:S(2)}, u32[]{:S(2)}) collective-permute-start(f32[64,192]{1,0:T(8,128)S(1)} %slice.203), channel_id=1, source_target_pairs={{0,1}} | collective-permute-start | bytes 147464 | tf_op jit(solution)/shard_map/ppermute | solution.py:82
  232.3 10.0 %collective-permute-start.16 = (f32[64,192]{1,0:T(8,128)S(1)}, f32[64,192]{1,0:T(8,128)S(1)}, u32[]{:S(2)}, u32[]{:S(2)}) collective-permute-start(f32[64,192]{1,0:T(8,128)S(1)} %slice.203), channel_id=1, source_target_pairs={{0,32}} | collective-permute-start | bytes 147464 | tf_op jit(solution)/shard_map/ppermute | solution.py:85
  233.0 10.7 %collective-permute-start.15 = (f32[64,192]{1,0:T(8,128)S(1)}, f32[64,192]{1,0:T(8,128)S(1)}, u32[]{:S(2)}, u32[]{:S(2)}) collective-permute-start(f32[64,192]{1,0:T(8,128)S(1)} %slice.203), channel_id=1, source_target_pairs={{0,64}} | collective-permute-start | bytes 147464 | tf_op jit(solution)/shard_map/ppermute | solution.py:85
  233.7 11.3 %collective-permute-start.14 = (f32[64,192]{1,0:T(8,128)S(1)}, f32[64,192]{1,0:T(8,128)S(1)}, u32[]{:S(2)}, u32[]{:S(2)}) collective-permute-start(f32[64,192]{1,0:T(8,128)S(1)} %slice.203), channel_id=1, source_target_pairs={{0,96}} | collective-permute-start | bytes 147464 | tf_op jit(solution)/shard_map/ppermute | solution.py:85
  234.3 14.6 %collective-permute-start.24 = (f32[64,256]{1,0:T(8,128)S(1)}, f32[64,256]{1,0:T(8,128)S(1)}, u32[]{:S(2)}, u32[]{:S(2)}) collective-permute-start(f32[64,256]{1,0:T(8,128)S(1)} %slice.204), channel_id=1, source_target_pairs={{0,1}} | collective-permute-start | bytes 196616 | tf_op jit(solution)/shard_map/ppermute | solution.py:82
  241.7 8.0 %collective-permute-start.23 = (f32[64,256]{1,0:T(8,128)S(1)}, f32[64,256]{1,0:T(8,128)S(1)}, u32[]{:S(2)}, u32[]{:S(2)}) collective-permute-start(f32[64,256]{1,0:T(8,128)S(1)} %slice.204), channel_id=1, source_target_pairs={{0,32}} | collective-permute-start | bytes 196616 | tf_op jit(solution)/shard_map/ppermute | solution.py:85
  247.7 9.6 %collective-permute-start.31 = (f32[64,320]{1,0:T(8,128)S(1)}, f32[64,320]{1,0:T(8,128)S(1)}, u32[]{:S(2)}, u32[]{:S(2)}) collective-permute-start(f32[64,320]{1,0:T(8,128)S(1)} %slice.205), channel_id=1, source_target_pairs={{0,1}} | collective-permute-start | bytes 245768 | tf_op jit(solution)/shard_map/ppermute | solution.py:82
  249.0 9.0 %collective-permute-start.30 = (f32[64,320]{1,0:T(8,128)S(1)}, f32[64,320]{1,0:T(8,128)S(1)}, u32[]{:S(2)}, u32[]{:S(2)}) collective-permute-start(f32[64,320]{1,0:T(8,128)S(1)} %slice.205), channel_id=1, source_target_pairs={{0,32}} | collective-permute-start | bytes 245768 | tf_op jit(solution)/shard_map/ppermute | solution.py:85
  249.7 9.6 %collective-permute-start.29 = (f32[64,320]{1,0:T(8,128)S(1)}, f32[64,320]{1,0:T(8,128)S(1)}, u32[]{:S(2)}, u32[]{:S(2)}) collective-permute-start(f32[64,320]{1,0:T(8,128)S(1)} %slice.205), channel_id=1, source_target_pairs={{0,64}} | collective-permute-start | bytes 245768 | tf_op jit(solution)/shard_map/ppermute | solution.py:85
  250.4 10.2 %collective-permute-start.28 = (f32[64,320]{1,0:T(8,128)S(1)}, f32[64,320]{1,0:T(8,128)S(1)}, u32[]{:S(2)}, u32[]{:S(2)}) collective-permute-start(f32[64,320]{1,0:T(8,128)S(1)} %slice.205), channel_id=1, source_target_pairs={{0,96}} | collective-permute-start | bytes 245768 | tf_op jit(solution)/shard_map/ppermute | solution.py:85
  251.0 13.6 %collective-permute-start.38 = (f32[64,384]{1,0:T(8,128)S(1)}, f32[64,384]{1,0:T(8,128)S(1)}, u32[]{:S(2)}, u32[]{:S(2)}) collective-permute-start(f32[64,384]{1,0:T(8,128)S(1)} %slice.206), channel_id=1, source_target_pairs={{0,1}} | collective-permute-start | bytes 294920 | tf_op jit(solution)/shard_map/ppermute | solution.py:82
  257.3 8.1 %collective-permute-start.37 = (f32[64,384]{1,0:T(8,128)S(1)}, f32[64,384]{1,0:T(8,128)S(1)}, u32[]{:S(2)}, u32[]{:S(2)}) collective-permute-start(f32[64,384]{1,0:T(8,128)S(1)} %slice.206), channel_id=1, source_target_pairs={{0,32}} | collective-permute-start | bytes 294920 | tf_op jit(solution)/shard_map/ppermute | solution.py:85
  263.3 10.0 %collective-permute-start.45 = (f32[64,448]{1,0:T(8,128)S(1)}, f32[64,448]{1,0:T(8,128)S(1)}, u32[]{:S(2)}, u32[]{:S(2)}) collective-permute-start(f32[64,448]{1,0:T(8,128)S(1)} %slice.207), channel_id=1, source_target_pairs={{0,1}} | collective-permute-start | bytes 344072 | tf_op jit(solution)/shard_map/ppermute | solution.py:82
  264.7 9.3 %collective-permute-start.44 = (f32[64,448]{1,0:T(8,128)S(1)}, f32[64,448]{1,0:T(8,128)S(1)}, u32[]{:S(2)}, u32[]{:S(2)}) collective-permute-start(f32[64,448]{1,0:T(8,128)S(1)} %slice.207), channel_id=1, source_target_pairs={{0,32}} | collective-permute-start | bytes 344072 | tf_op jit(solution)/shard_map/ppermute | solution.py:85
  265.4 9.9 %collective-permute-start.43 = (f32[64,448]{1,0:T(8,128)S(1)}, f32[64,448]{1,0:T(8,128)S(1)}, u32[]{:S(2)}, u32[]{:S(2)}) collective-permute-start(f32[64,448]{1,0:T(8,128)S(1)} %slice.207), channel_id=1, source_target_pairs={{0,64}} | collective-permute-start | bytes 344072 | tf_op jit(solution)/shard_map/ppermute | solution.py:85
  266.0 10.5 %collective-permute-start.42 = (f32[64,448]{1,0:T(8,128)S(1)}, f32[64,448]{1,0:T(8,128)S(1)}, u32[]{:S(2)}, u32[]{:S(2)}) collective-permute-start(f32[64,448]{1,0:T(8,128)S(1)} %slice.207), channel_id=1, source_target_pairs={{0,96}} | collective-permute-start | bytes 344072 | tf_op jit(solution)/shard_map/ppermute | solution.py:85
  266.7 15.5 %collective-permute-start.52 = (f32[64,512]{1,0:T(8,128)S(1)}, f32[64,512]{1,0:T(8,128)S(1)}, u32[]{:S(2)}, u32[]{:S(2)}) collective-permute-start(f32[64,512]{1,0:T(8,128)S(1)} %slice.208), channel_id=1, source_target_pairs={{0,1}} | collective-permute-start | bytes 393224 | tf_op jit(solution)/shard_map/ppermute | solution.py:82
  273.3 11.8 %collective-permute-start.51 = (f32[64,512]{1,0:T(8,128)S(1)}, f32[64,512]{1,0:T(8,128)S(1)}, u32[]{:S(2)}, u32[]{:S(2)}) collective-permute-start(f32[64,512]{1,0:T(8,128)S(1)} %slice.208), channel_id=1, source_target_pairs={{0,32}} | collective-permute-start | bytes 393224 | tf_op jit(solution)/shard_map/ppermute | solution.py:85
  277.9 8.4 %collective-permute-start.50 = (f32[64,512]{1,0:T(8,128)S(1)}, f32[64,512]{1,0:T(8,128)S(1)}, u32[]{:S(2)}, u32[]{:S(2)}) collective-permute-start(f32[64,512]{1,0:T(8,128)S(1)} %slice.208), channel_id=1, source_target_pairs={{0,64}} | collective-permute-start | bytes 393224 | tf_op jit(solution)/shard_map/ppermute | solution.py:85
  278.6 9.0 %collective-permute-start.49 = (f32[64,512]{1,0:T(8,128)S(1)}, f32[64,512]{1,0:T(8,128)S(1)}, u32[]{:S(2)}, u32[]{:S(2)}) collective-permute-start(f32[64,512]{1,0:T(8,128)S(1)} %slice.208), channel_id=1, source_target_pairs={{0,96}} | collective-permute-start | bytes 393224 | tf_op jit(solution)/shard_map/ppermute | solution.py:85
  279.3 9.7 %collective-permute-start.34 = (f32[64,320]{1,0:T(8,128)S(1)}, f32[64,320]{1,0:T(8,128)S(1)}, u32[]{:S(2)}, u32[]{:S(2)}) collective-permute-start(f32[64,320]{1,0:T(8,128)S(1)} %select_select_fusion.7), channel_id=1, source_target_pairs={{1,8},{32,40},{64,72},{96,104}} | collective-permute-start | bytes 245768 | tf_op jit(solution)/shard_map/ppermute | solution.py:93
  282.2 8.1 %collective-permute-start.33 = (f32[64,320]{1,0:T(8,128)S(1)}, f32[64,320]{1,0:T(8,128)S(1)}, u32[]{:S(2)}, u32[]{:S(2)}) collective-permute-start(f32[64,320]{1,0:T(8,128)S(1)} %select_select_fusion.7), channel_id=1, source_target_pairs={{1,16},{32,48},{64,80},{96,112}} | collective-permute-start | bytes 245768 | tf_op jit(solution)/shard_map/ppermute | solution.py:93
  377.3 18.0 %collective-permute-start.70 = (f32[128,512]{1,0:T(8,128)S(1)}, f32[128,512]{1,0:T(8,128)S(1)}, u32[]{:S(2)}, u32[]{:S(2)}) collective-permute-start(f32[128,512]{1,0:T(8,128)S(1)} %get-tuple-element.19), channel_id=1, source_target_pairs={{0,0},{1,8},{2,16},{3,24},{4,32},{5,40},{6,48},{7,56},{8,64},{9,72... | collective-permute-start | bytes 786440 | tf_op jit(solution)/shard_map/ppermute | solution.py:128
  403.8 32.0 %collective-permute-start.64 = (f32[128,512]{1,0:T(8,128)S(1)}, f32[128,512]{1,0:T(8,128)S(1)}, u32[]{:S(2)}, u32[]{:S(2)}) collective-permute-start(f32[128,512]{1,0:T(8,128)S(1)} %get-tuple-element.19), channel_id=1, source_target_pairs={{0,6},{1,7},{2,0},{3,1},{4,2},{5,3},{6,4},{7,5},{8,14},{9,15},{10,... | collective-permute-start | bytes 786440 | tf_op jit(solution)/shard_map/ppermute | solution.py:137
  418.5 15.1 %collective-permute-start.63 = (f32[128,512]{1,0:T(8,128)S(1)}, f32[128,512]{1,0:T(8,128)S(1)}, u32[]{:S(2)}, u32[]{:S(2)}) collective-permute-start(f32[128,512]{1,0:T(8,128)S(1)} %get-tuple-element.19), channel_id=1, source_target_pairs={{0,7},{1,0},{2,1},{3,2},{4,3},{5,4},{6,5},{7,6},{8,15},{9,8},{10,9... | collective-permute-start | bytes 786440 | tf_op jit(solution)/shard_map/ppermute | solution.py:137
  431.0 27.5 %collective-permute-start.69 = (f32[128,512]{1,0:T(8,128)S(1)}, f32[128,512]{1,0:T(8,128)S(1)}, u32[]{:S(2)}, u32[]{:S(2)}) collective-permute-start(f32[128,512]{1,0:T(8,128)S(1)} %get-tuple-element.19), channel_id=1, source_target_pairs={{0,1},{1,2},{2,3},{3,4},{4,5},{5,6},{6,7},{7,0},{8,9},{9,10},{10,1... | collective-permute-start | bytes 786440 | tf_op jit(solution)/shard_map/ppermute | solution.py:137
  432.7 25.8 %collective-permute-start.68 = (f32[128,512]{1,0:T(8,128)S(1)}, f32[128,512]{1,0:T(8,128)S(1)}, u32[]{:S(2)}, u32[]{:S(2)}) collective-permute-start(f32[128,512]{1,0:T(8,128)S(1)} %get-tuple-element.19), channel_id=1, source_target_pairs={{0,2},{1,3},{2,4},{3,5},{4,6},{5,7},{6,0},{7,1},{8,10},{9,11},{10,... | collective-permute-start | bytes 786440 | tf_op jit(solution)/shard_map/ppermute | solution.py:137
  432.8 25.7 %collective-permute-start.67 = (f32[128,512]{1,0:T(8,128)S(1)}, f32[128,512]{1,0:T(8,128)S(1)}, u32[]{:S(2)}, u32[]{:S(2)}) collective-permute-start(f32[128,512]{1,0:T(8,128)S(1)} %get-tuple-element.19), channel_id=1, source_target_pairs={{0,3},{1,4},{2,5},{3,6},{4,7},{5,0},{6,1},{7,2},{8,11},{9,12},{10,... | collective-permute-start | bytes 786440 | tf_op jit(solution)/shard_map/ppermute | solution.py:137
  433.6 18.2 %collective-permute-start.65 = (f32[128,512]{1,0:T(8,128)S(1)}, f32[128,512]{1,0:T(8,128)S(1)}, u32[]{:S(2)}, u32[]{:S(2)}) collective-permute-start(f32[128,512]{1,0:T(8,128)S(1)} %get-tuple-element.19), channel_id=1, source_target_pairs={{0,5},{1,6},{2,7},{3,0},{4,1},{5,2},{6,3},{7,4},{8,13},{9,14},{10,... | collective-permute-start | bytes 786440 | tf_op jit(solution)/shard_map/ppermute | solution.py:137
  435.7 20.6 %collective-permute-start.66 = (f32[128,512]{1,0:T(8,128)S(1)}, f32[128,512]{1,0:T(8,128)S(1)}, u32[]{:S(2)}, u32[]{:S(2)}) collective-permute-start(f32[128,512]{1,0:T(8,128)S(1)} %get-tuple-element.19), channel_id=1, source_target_pairs={{0,4},{1,5},{2,6},{3,7},{4,0},{5,1},{6,2},{7,3},{8,12},{9,13},{10,... | collective-permute-start | bytes 786440 | tf_op jit(solution)/shard_map/ppermute | solution.py:137
  (54 other events, 302.0 us)
Sparse Core Ops, SparseCore 0:
  396.2 65.7 all-gather.1

commit v12 on v10

--- a/solution.py
+++ b/solution.py
@@ -72,8 +72,9 @@
     )
     factor11 = jnp.linalg.cholesky(safe_block)
 
-    band = PANEL // 4
-    sent = tuple(factor11[i * band:(i + 1) * band, :(i + 1) * band] for i in range(4))
+    bands = 8
+    band = PANEL // bands
+    sent = tuple(factor11[i * band:(i + 1) * band, :(i + 1) * band] for i in range(bands))
     group = 4 if row_count % 4 == 0 else 1
     held_l = sent
     for m in range(1, row_count // group):

time: 446 us -> 487 us (1.092)
  waiting for transfers between devices: 102 us -> 122 us
  starting transfers between devices: 66.9 us -> 83.5 us
    ppermute x7, waiting for transfers between devices: 20.6 us -> 44 us  [shards(): lax.ppermute(solved[j * piece_rows:(j + 1) * piece_rows], ('row', 'col'),...]
    ppermute x12 -> x24, starting transfers between devices: 8.05 us -> 16 us  [shards(): got = lax.ppermute(sent, ('row', 'col'), [(0, m * group * col_count)])]
    ppermute x12 -> x24, starting transfers between devices: 8.05 us -> 16 us  [shards(): got = lax.ppermute(lead, ('row', 'col'), perm)]
    unnamed x45 -> x50, local copies, waits for them, and re-layouts: 11.9 us -> 13.8 us
  transfers between devices with their start and end apart: 41 -> 65, of which waited for: 7 -> 6; matrix products, arithmetic and copies ran while one was open for 5% -> 5% of each run, Pallas kernels for 0% -> 0%
where the time goes in v12:
time: 487 us; the launch traced here: 480 us
  other arithmetic  148 us (30%)
  waiting for transfers between devices  122 us (25%)
  starting transfers between devices  83.5 us (17%)
  local copies, waits for them, and re-layouts  62.4 us (13%)
  matrix products  46.3 us (10%)
  between operations  18.5 us (4%)
    another operation x14, other arithmetic, shards(): factor11 = jnp.linalg.cholesky(safe_block)  79 us
    all_to_all x1, waiting for transfers between devices, shards(): lax.all_to_all(outgoing.reshape(devices, capacity * width), ('row', 'col'...  50.5 us
    ppermute x7, waiting for transfers between devices, shards(): lax.ppermute(solved[j * piece_rows:(j + 1) * piece_rows], ('row', 'col'),...  44 us
    another operation x4, other arithmetic, shards(): lax.linalg.triangular_solve(factor_col0, panel_cols, left_side=False, low...  41.6 us
    ppermute x7, starting transfers between devices, shards(): shifted.append(lax.ppermute(my_piece, ('row', 'col'), perm))  21.6 us
    ppermute x7, waiting for transfers between devices, shards(): shifted.append(lax.ppermute(my_piece, ('row', 'col'), perm))  20.5 us
    dot_general x1, matrix products, shards(): lax.dot_general(panel_here, column_panel, (((1,), (1,)), ((), ())), preci...  17.3 us
    ppermute x24, starting transfers between devices, shards(): got = lax.ppermute(sent, ('row', 'col'), [(0, m * group * col_count)])  16 us
  transfers between devices with their start and end apart: 65, of which 6 were waited for; matrix products, arithmetic and copies ran while one was open for 5% of the time, Pallas kernels for 0%

profile of v12, /device:TPU:1, one launch (start us, length us, event | category | flops | bytes accessed | tf_op | source)
XLA Modules:
  0.0 480.3 jit_solution(10259773680782876569)
XLA Ops:
  9.4 3.2 copy.80
  12.7 3.9 fusion.8
  16.6 7.2 %all_to_all.8 = f32[128,1,8448]{2,1,0:T(1,128)} reshape(f32[256,4224]{1,0:T(8,128)} %fusion.8) | data formatting | bytes 8650752 | tf_op jit(solution)/shard_map/all_to_all | solution.py:39
  23.8 11.9 %all-to-all-start = ((f32[128,1,8448]{2,1,0:T(1,128)}), f32[128,1,8448]{2,1,0:T(1,128)}, u32[]{:S(2)}, u32[]{:S(2)}) async-start(f32[128,1,8448]{2,1,0:T(1,128)} %all_to_all.8), calls=%async_computation | async-start | bytes 8650752 | tf_op jit(solution)/shard_map/all_to_all | solution.py:39
  39.1 50.5 %all-to-all-done = f32[128,1,8448]{2,1,0:T(1,128)} async-done(((f32[128,1,8448]{2,1,0:T(1,128)}), f32[128,1,8448]{2,1,0:T(1,128)}, u32[]{:S(2)}, u32[]{:S(2)}) %all-to-all-start) | async-done | bytes 4325408 | tf_op jit(solution)/shard_map/all_to_all | solution.py:39
  89.7 14.0 %reduce.24 = f32[128,8448]{1,0:T(8,128)} reduce(f32[128,1,8448]{2,1,0:T(1,128)} %all-to-all-done, f32[]{:T(128)} %constant.308), dimensions={1}, to_apply=%all_to_all.7.reduce_sub_computation | reduce | bytes 8650756 | tf_op jit(solution)/shard_map/all_to_all | solution.py:39
  103.7 5.0 %reshape.140 = f32[256,4224]{1,0:T(8,128)} reshape(f32[128,8448]{1,0:T(8,128)} %reduce.24) | data formatting | bytes 8650752 | tf_op jit(solution)/shard_map/reshape | solution.py:45
  109.7 3.9 fusion.12
  117.3 3.3 copy.56
  120.6 2.8 add.170
  130.0 11.7 %cholesky.104 = f32[128,128]{1,0:T(8,128)S(1)} custom-call(f32[128,128]{1,0:T(8,128)S(1)} %cholesky.266), custom_call_target="Cholesky" | custom-call | tf_op jit(solution)/shard_map/jit(cholesky)/cholesky | solution.py:73
  141.7 9.8 %custom-call.30 = f32[1,128,128]{1,2,0:T(8,128)S(1)} custom-call(f32[1,128,128]{2,1,0:T(8,128)S(1)} %get-tuple-element.38), custom_call_target="InvertDiagBlocksLowerTriangular" | custom-call | tf_op jit(solution)/shard_map/jit(cholesky)/cholesky | solution.py:73
  154.2 11.7 %cholesky.217 = f32[128,128]{1,0:T(8,128)S(1)} custom-call(f32[128,128]{1,0:T(8,128)S(1)} %cholesky.270), custom_call_target="Cholesky" | custom-call | tf_op jit(solution)/shard_map/jit(cholesky)/cholesky | solution.py:73
  165.9 10.0 %custom-call.31 = f32[1,128,128]{1,2,0:T(8,128)S(1)} custom-call(f32[1,128,128]{2,1,0:T(8,128)S(1)} %get-tuple-element.35), custom_call_target="InvertDiagBlocksLowerTriangular" | custom-call | tf_op jit(solution)/shard_map/jit(cholesky)/cholesky | solution.py:73
  177.5 11.7 %cholesky.238 = f32[128,128]{1,0:T(8,128)S(1)} custom-call(f32[128,128]{1,0:T(8,128)S(1)} %cholesky.275), custom_call_target="Cholesky" | custom-call | tf_op jit(solution)/shard_map/jit(cholesky)/cholesky | solution.py:73
  189.9 9.8 %custom-call.32 = f32[1,128,128]{1,2,0:T(8,128)S(1)} custom-call(f32[1,128,128]{2,1,0:T(8,128)S(1)} %get-tuple-element.32), custom_call_target="InvertDiagBlocksLowerTriangular" | custom-call | tf_op jit(solution)/shard_map/jit(cholesky)/cholesky | solution.py:73
  201.1 12.1 %cholesky.255 = f32[128,128]{1,0:T(8,128)S(1)} custom-call(f32[128,128]{1,0:T(8,128)S(1)} %convolution_subtract_fusion.4), custom_call_target="Cholesky" | custom-call | tf_op jit(solution)/shard_map/jit(cholesky)/cholesky | solution.py:73
  252.3 10.5 %while.1 = (s32[]{:T(128)}, f32[512,512]{1,0:T(8,128)S(1)}, s32[4,2]{0,1:T(2,128)S(1)}, f32[4,128,128]{2,1,0:T(8,128)}, s32[]{:T(128)}) while((s32[]{:T(128)}, f32[512,512]{1,0:T(8,128)S(1)}, s32[4,2]{0,1:T(2,128)S(1)}, f32[4,128,128]{2,1,0:T(8,128)}, s32[]{:T(128)}) %tuple.38), condition=%wide.while_cond, body=%wide.while_body.sunk | while | flops 2 | bytes 132205 | solution.py:103
  263.8 40.1 %custom-call.33 = f32[4,128,128]{1,2,0:T(8,128)S(1)} custom-call(f32[4,128,128]{2,1,0:T(8,128)} %get-tuple-element.9), custom_call_target="InvertDiagBlocksLowerTriangular" | custom-call | tf_op jit(solution)/shard_map/triangular_solve | solution.py:103
  311.7 2.9 fusion.21
  316.0 2.0 fusion.49
  325.5 44.0 %collective-permute-done.54 = f32[128,512]{1,0:T(8,128)S(1)} collective-permute-done((f32[128,512]{1,0:T(8,128)S(1)}, f32[128,512]{1,0:T(8,128)S(1)}, u32[]{:S(2)}, u32[]{:S(2)}) %collective-permute-start.54) | collective-permute-done | bytes 262176 | tf_op jit(solution)/shard_map/ppermute | solution.py:112
  372.8 12.5 %collective-permute-start.62 = (f32[128,512]{1,0:T(8,128)S(1)}, f32[128,512]{1,0:T(8,128)S(1)}, u32[]{:S(2)}, u32[]{:S(2)}) collective-permute-start(f32[128,512]{1,0:T(8,128)S(1)} %get-tuple-element.19), channel_id=1, source_target_pairs={{0,0},{1,8},{2,16},{3,24},{4,32},{5,40},{6,48},{7,56},{8,64},{9,72... | collective-permute-start | bytes 786440 | tf_op jit(solution)/shard_map/ppermute | solution.py:121
  385.2 6.9 %collective-permute-done.62 = f32[128,512]{1,0:T(8,128)S(1)} collective-permute-done((f32[128,512]{1,0:T(8,128)S(1)}, f32[128,512]{1,0:T(8,128)S(1)}, u32[]{:S(2)}, u32[]{:S(2)}) %collective-permute-start.62) | collective-permute-done | bytes 262176 | tf_op jit(solution)/shard_map/ppermute | solution.py:121
  392.9 5.9 %fusion.5 = f32[64,8,32,128]{3,1,2,0:T(8,128)S(1)} fusion(f32[256,4224]{1,0:T(8,128)} %reshape.140, s32[256]{0:T(256)S(1)} %select_reduce_fusion), kind=kOutput, calls=%fused_computation.9 | convolution fusion | flops 6442582016 | bytes 12583936 | tf_op jit(solution)/shard_map/dot_general | solution.py:93
  400.6 15.0 %collective-permute-start.56 = (f32[128,512]{1,0:T(8,128)S(1)}, f32[128,512]{1,0:T(8,128)S(1)}, u32[]{:S(2)}, u32[]{:S(2)}) collective-permute-start(f32[128,512]{1,0:T(8,128)S(1)} %get-tuple-element.19), channel_id=1, source_target_pairs={{0,6},{1,7},{2,0},{3,1},{4,2},{5,3},{6,4},{7,5},{8,14},{9,15},{10,... | collective-permute-start | bytes 786440 | tf_op jit(solution)/shard_map/ppermute | solution.py:130
  417.2 10.9 %copy.53 = f32[32,32,16,128]{3,2,1,0:T(8,128)} copy(f32[32,32,16,128]{3,1,2,0:T(8,128)S(1)} %bitcast_bitcast_fusion) | data formatting | bytes 16777216 | tf_op jit(solution)/shard_map/transpose | solution.py:100
  430.4 2.4 collective-permute-start.57
  434.8 13.8 %collective-permute-done.57 = f32[128,512]{1,0:T(8,128)S(1)} collective-permute-done((f32[128,512]{1,0:T(8,128)S(1)}, f32[128,512]{1,0:T(8,128)S(1)}, u32[]{:S(2)}, u32[]{:S(2)}) %collective-permute-start.57) | collective-permute-done | bytes 262176 | tf_op jit(solution)/shard_map/ppermute | solution.py:130
  448.6 4.5 collective-permute-done.58
  453.1 2.1 collective-permute-done.59
  455.9 17.3 %fusion = f32[1024,2048]{1,0:T(8,128)} fusion(f32[1024,2048]{1,0:T(8,128)} %param.4, f32[128,8,16,128]{3,2,1,0:T(8,128)} %bitcast.111, pred[2048]{0:T(1024)(128)(4,1)S(1)} %add_compare_fusion, pred[1024]{0:T(1024)(128)(4,1)S(1)} %add_compare_fusion.1, f32[1024,512]{1,0:T(8,128)S(1)} %bitcast.113, f32[2048,512]{1,0:T(8,128)} %all-gather.2.cloned.1.call-done), kind=kOutput, calls=%fused_computation.3 | convolution fusion | flops 6450839552 | bytes 31460352 | tf_op jit(solution)/shard_map/dot_general | solution.py:134
  (260 shorter events, 98.9 us)
Async XLA Ops:
  23.8 65.8 %all-to-all-start = ((f32[128,1,8448]{2,1,0:T(1,128)}), f32[128,1,8448]{2,1,0:T(1,128)}, u32[]{:S(2)}, u32[]{:S(2)}) async-start(f32[128,1,8448]{2,1,0:T(1,128)} %all_to_all.8), calls=%async_computation | async-start | bytes 8650752 | tf_op jit(solution)/shard_map/all_to_all | solution.py:39
  35.8 420.1 %all-gather.2.cloned.1.call-start = ((), (), s32[]{:S(2)}) async-start(), calls=%async_computation.1 | async-start | bytes 4456448 | tf_op jit(solution)/shard_map/all_gather | solution.py:122
  220.6 3.5 collective-permute-start.5
  221.3 3.5 collective-permute-start.4
  221.9 3.5 collective-permute-start.3
  222.7 3.5 collective-permute-start.8
  223.3 3.5 collective-permute-start.7
  226.9 5.5 %collective-permute-start.20 = (f32[64,256]{1,0:T(8,128)S(1)}, f32[64,256]{1,0:T(8,128)S(1)}, u32[]{:S(2)}, u32[]{:S(2)}) collective-permute-start(f32[64,256]{1,0:T(8,128)S(1)} %slice.204), channel_id=1, source_target_pairs={{0,32}} | collective-permute-start | bytes 196616 | tf_op jit(solution)/shard_map/ppermute | solution.py:81
  227.6 5.5 %collective-permute-start.19 = (f32[64,256]{1,0:T(8,128)S(1)}, f32[64,256]{1,0:T(8,128)S(1)}, u32[]{:S(2)}, u32[]{:S(2)}) collective-permute-start(f32[64,256]{1,0:T(8,128)S(1)} %slice.204), channel_id=1, source_target_pairs={{0,64}} | collective-permute-start | bytes 196616 | tf_op jit(solution)/shard_map/ppermute | solution.py:81
  233.1 5.6 %collective-permute-start.32 = (f32[64,384]{1,0:T(8,128)S(1)}, f32[64,384]{1,0:T(8,128)S(1)}, u32[]{:S(2)}, u32[]{:S(2)}) collective-permute-start(f32[64,384]{1,0:T(8,128)S(1)} %slice.206), channel_id=1, source_target_pairs={{0,32}} | collective-permute-start | bytes 294920 | tf_op jit(solution)/shard_map/ppermute | solution.py:81
  233.8 5.6 %collective-permute-start.31 = (f32[64,384]{1,0:T(8,128)S(1)}, f32[64,384]{1,0:T(8,128)S(1)}, u32[]{:S(2)}, u32[]{:S(2)}) collective-permute-start(f32[64,384]{1,0:T(8,128)S(1)} %slice.206), channel_id=1, source_target_pairs={{0,64}} | collective-permute-start | bytes 294920 | tf_op jit(solution)/shard_map/ppermute | solution.py:81
  239.4 5.6 %collective-permute-start.44 = (f32[64,512]{1,0:T(8,128)S(1)}, f32[64,512]{1,0:T(8,128)S(1)}, u32[]{:S(2)}, u32[]{:S(2)}) collective-permute-start(f32[64,512]{1,0:T(8,128)S(1)} %slice.208), channel_id=1, source_target_pairs={{0,32}} | collective-permute-start | bytes 393224 | tf_op jit(solution)/shard_map/ppermute | solution.py:81
  240.1 5.6 %collective-permute-start.43 = (f32[64,512]{1,0:T(8,128)S(1)}, f32[64,512]{1,0:T(8,128)S(1)}, u32[]{:S(2)}, u32[]{:S(2)}) collective-permute-start(f32[64,512]{1,0:T(8,128)S(1)} %slice.208), channel_id=1, source_target_pairs={{0,64}} | collective-permute-start | bytes 393224 | tf_op jit(solution)/shard_map/ppermute | solution.py:81
  243.6 3.5 collective-permute-start.29
  244.3 3.5 collective-permute-start.28
  245.7 3.5 collective-permute-start.35
  246.4 3.5 collective-permute-start.34
  247.8 3.5 collective-permute-start.41
  248.5 3.5 collective-permute-start.40
  321.4 48.0 %collective-permute-start.54 = (f32[128,512]{1,0:T(8,128)S(1)}, f32[128,512]{1,0:T(8,128)S(1)}, u32[]{:S(2)}, u32[]{:S(2)}) collective-permute-start(f32[128,512]{1,0:T(8,128)S(1)} %get-tuple-element.22), channel_id=1, source_target_pairs={{0,1},{8,9},{16,17},{24,25},{32,33},{40,41},{48,49},{56,57},{64,65... | collective-permute-start | bytes 786440 | tf_op jit(solution)/shard_map/ppermute | solution.py:112
  322.7 47.4 %collective-permute-start.53 = (f32[128,512]{1,0:T(8,128)S(1)}, f32[128,512]{1,0:T(8,128)S(1)}, u32[]{:S(2)}, u32[]{:S(2)}) collective-permute-start(f32[128,512]{1,0:T(8,128)S(1)} %get-tuple-element.23), channel_id=1, source_target_pairs={{0,2},{8,10},{16,18},{24,26},{32,34},{40,42},{48,50},{56,58},{64,6... | collective-permute-start | bytes 786440 | tf_op jit(solution)/shard_map/ppermute | solution.py:112
  323.4 47.4 %collective-permute-start.52 = (f32[128,512]{1,0:T(8,128)S(1)}, f32[128,512]{1,0:T(8,128)S(1)}, u32[]{:S(2)}, u32[]{:S(2)}) collective-permute-start(f32[128,512]{1,0:T(8,128)S(1)} %get-tuple-element.24), channel_id=1, source_target_pairs={{0,3},{8,11},{16,19},{24,27},{32,35},{40,43},{48,51},{56,59},{64,6... | collective-permute-start | bytes 786440 | tf_op jit(solution)/shard_map/ppermute | solution.py:112
  324.1 46.8 %collective-permute-start.51 = (f32[128,512]{1,0:T(8,128)S(1)}, f32[128,512]{1,0:T(8,128)S(1)}, u32[]{:S(2)}, u32[]{:S(2)}) collective-permute-start(f32[128,512]{1,0:T(8,128)S(1)} %get-tuple-element.25), channel_id=1, source_target_pairs={{0,4},{8,12},{16,20},{24,28},{32,36},{40,44},{48,52},{56,60},{64,6... | collective-permute-start | bytes 786440 | tf_op jit(solution)/shard_map/ppermute | solution.py:112
  324.8 46.1 %collective-permute-start.50 = (f32[128,512]{1,0:T(8,128)S(1)}, f32[128,512]{1,0:T(8,128)S(1)}, u32[]{:S(2)}, u32[]{:S(2)}) collective-permute-start(f32[128,512]{1,0:T(8,128)S(1)} %get-tuple-element.26), channel_id=1, source_target_pairs={{0,5},{8,13},{16,21},{24,29},{32,37},{40,45},{48,53},{56,61},{64,6... | collective-permute-start | bytes 786440 | tf_op jit(solution)/shard_map/ppermute | solution.py:112
  372.8 19.4 %collective-permute-start.62 = (f32[128,512]{1,0:T(8,128)S(1)}, f32[128,512]{1,0:T(8,128)S(1)}, u32[]{:S(2)}, u32[]{:S(2)}) collective-permute-start(f32[128,512]{1,0:T(8,128)S(1)} %get-tuple-element.19), channel_id=1, source_target_pairs={{0,0},{1,8},{2,16},{3,24},{4,32},{5,40},{6,48},{7,56},{8,64},{9,72... | collective-permute-start | bytes 786440 | tf_op jit(solution)/shard_map/ppermute | solution.py:121
  400.6 32.2 %collective-permute-start.56 = (f32[128,512]{1,0:T(8,128)S(1)}, f32[128,512]{1,0:T(8,128)S(1)}, u32[]{:S(2)}, u32[]{:S(2)}) collective-permute-start(f32[128,512]{1,0:T(8,128)S(1)} %get-tuple-element.19), channel_id=1, source_target_pairs={{0,6},{1,7},{2,0},{3,1},{4,2},{5,3},{6,4},{7,5},{8,14},{9,15},{10,... | collective-permute-start | bytes 786440 | tf_op jit(solution)/shard_map/ppermute | solution.py:130
  415.6 14.8 %collective-permute-start.55 = (f32[128,512]{1,0:T(8,128)S(1)}, f32[128,512]{1,0:T(8,128)S(1)}, u32[]{:S(2)}, u32[]{:S(2)}) collective-permute-start(f32[128,512]{1,0:T(8,128)S(1)} %get-tuple-element.19), channel_id=1, source_target_pairs={{0,7},{1,0},{2,1},{3,2},{4,3},{5,4},{6,5},{7,6},{8,15},{9,8},{10,9... | collective-permute-start | bytes 786440 | tf_op jit(solution)/shard_map/ppermute | solution.py:130
  428.2 27.2 %collective-permute-start.61 = (f32[128,512]{1,0:T(8,128)S(1)}, f32[128,512]{1,0:T(8,128)S(1)}, u32[]{:S(2)}, u32[]{:S(2)}) collective-permute-start(f32[128,512]{1,0:T(8,128)S(1)} %get-tuple-element.19), channel_id=1, source_target_pairs={{0,1},{1,2},{2,3},{3,4},{4,5},{5,6},{6,7},{7,0},{8,9},{9,10},{10,1... | collective-permute-start | bytes 786440 | tf_op jit(solution)/shard_map/ppermute | solution.py:130
  429.9 25.4 %collective-permute-start.60 = (f32[128,512]{1,0:T(8,128)S(1)}, f32[128,512]{1,0:T(8,128)S(1)}, u32[]{:S(2)}, u32[]{:S(2)}) collective-permute-start(f32[128,512]{1,0:T(8,128)S(1)} %get-tuple-element.19), channel_id=1, source_target_pairs={{0,2},{1,3},{2,4},{3,5},{4,6},{5,7},{6,0},{7,1},{8,10},{9,11},{10,... | collective-permute-start | bytes 786440 | tf_op jit(solution)/shard_map/ppermute | solution.py:130
  429.9 25.4 %collective-permute-start.59 = (f32[128,512]{1,0:T(8,128)S(1)}, f32[128,512]{1,0:T(8,128)S(1)}, u32[]{:S(2)}, u32[]{:S(2)}) collective-permute-start(f32[128,512]{1,0:T(8,128)S(1)} %get-tuple-element.19), channel_id=1, source_target_pairs={{0,3},{1,4},{2,5},{3,6},{4,7},{5,0},{6,1},{7,2},{8,11},{9,12},{10,... | collective-permute-start | bytes 786440 | tf_op jit(solution)/shard_map/ppermute | solution.py:130
  430.4 18.2 %collective-permute-start.57 = (f32[128,512]{1,0:T(8,128)S(1)}, f32[128,512]{1,0:T(8,128)S(1)}, u32[]{:S(2)}, u32[]{:S(2)}) collective-permute-start(f32[128,512]{1,0:T(8,128)S(1)} %get-tuple-element.19), channel_id=1, source_target_pairs={{0,5},{1,6},{2,7},{3,0},{4,1},{5,2},{6,3},{7,4},{8,13},{9,14},{10,... | collective-permute-start | bytes 786440 | tf_op jit(solution)/shard_map/ppermute | solution.py:130
  432.9 20.2 %collective-permute-start.58 = (f32[128,512]{1,0:T(8,128)S(1)}, f32[128,512]{1,0:T(8,128)S(1)}, u32[]{:S(2)}, u32[]{:S(2)}) collective-permute-start(f32[128,512]{1,0:T(8,128)S(1)} %get-tuple-element.19), channel_id=1, source_target_pairs={{0,4},{1,5},{2,6},{3,7},{4,0},{5,1},{6,2},{7,3},{8,12},{9,13},{10,... | collective-permute-start | bytes 786440 | tf_op jit(solution)/shard_map/ppermute | solution.py:130
  (46 other events, 175.9 us)
Sparse Core Ops, SparseCore 0:
  393.0 62.0 all-gather.1

commit v13 on v10

--- a/solution.py
+++ b/solution.py
@@ -73,19 +73,28 @@
     factor11 = jnp.linalg.cholesky(safe_block)
 
     band = PANEL // 4
-    sent = tuple(factor11[i * band:(i + 1) * band, :(i + 1) * band] for i in range(4))
+    low = [factor11[i * band:(i + 1) * band, :(i + 1) * band] for i in range(4)]
+    sent = jnp.concatenate(
+        [jnp.concatenate([low[0], low[2]], axis=1), low[3], low[1].reshape(band // 2, PANEL)], axis=0
+    )
     group = 4 if row_count % 4 == 0 else 1
     held_l = sent
     for m in range(1, row_count // group):
         got = lax.ppermute(sent, ("row", "col"), [(0, m * group * col_count)])
-        held_l = tuple(jnp.where(row_id == m * group, g, h) for g, h in zip(got, held_l))
+        held_l = jnp.where(row_id == m * group, got, held_l)
     lead = held_l
     for z in range(1, group):
         perm = [(m * group * col_count, (m * group + z) * col_count) for m in range(row_count // group)]
         got = lax.ppermute(lead, ("row", "col"), perm)
-        held_l = tuple(jnp.where(row_id % group == z, g, h) for g, h in zip(got, held_l))
+        held_l = jnp.where(row_id % group == z, got, held_l)
+    parts = [
+        held_l[:band, :band],
+        held_l[2 * band:2 * band + band // 2].reshape(band, 2 * band),
+        held_l[:band, band:],
+        held_l[band:2 * band],
+    ]
     factor_col0 = jnp.concatenate(
-        [jnp.pad(p, ((0, 0), (0, PANEL - p.shape[1]))) for p in held_l], axis=0
+        [jnp.pad(p, ((0, 0), (0, PANEL - p.shape[1]))) for p in parts], axis=0
     )
 
     every = (landing[None, :] == jnp.arange(local_count, dtype=jnp.int32)[:, None]).astype(jnp.float32)

time: 446 us -> 448 us (level)
  starting transfers between devices: 66.9 us -> 52.1 us
  waiting for transfers between devices: 102 us -> 115 us
    ppermute x1, waiting for transfers between devices: 9.48 us -> 20.5 us  [shards(): mine = lax.ppermute(my_piece, ('row', 'col'), perm)]
    unnamed x45 -> x47, local copies, waits for them, and re-layouts: 11.9 us -> 13.6 us
  transfers between devices with their start and end apart: 41 -> 23, of which waited for: 7 -> 6; matrix products, arithmetic and copies ran while one was open for 5% -> 5% of each run, Pallas kernels for 0% -> 0%
where the time goes in v13:
time: 448 us; the launch traced here: 442 us
  other arithmetic  149 us (33%)
  waiting for transfers between devices  115 us (26%)
  local copies, waits for them, and re-layouts  61.8 us (14%)
  starting transfers between devices  52.1 us (12%)
  matrix products  46.4 us (10%)
  between operations  17.6 us (4%)
    another operation x14, other arithmetic, shards(): factor11 = jnp.linalg.cholesky(safe_block)  79 us
    all_to_all x1, waiting for transfers between devices, shards(): lax.all_to_all(outgoing.reshape(devices, capacity * width), ('row', 'col'...  50.5 us
    another operation x4, other arithmetic, shards(): lax.linalg.triangular_solve(factor_col0, panel_cols, left_side=False, low...  42.6 us
    ppermute x7, waiting for transfers between devices, shards(): lax.ppermute(solved[j * piece_rows:(j + 1) * piece_rows], ('row', 'col'),...  23.3 us
    ppermute x1, waiting for transfers between devices, shards(): mine = lax.ppermute(my_piece, ('row', 'col'), perm)  20.5 us
    ppermute x7, waiting for transfers between devices, shards(): shifted.append(lax.ppermute(my_piece, ('row', 'col'), perm))  20.1 us
    dot_general x1, matrix products, shards(): lax.dot_general(panel_here, column_panel, (((1,), (1,)), ((), ())), preci...  17.3 us
    ppermute x7, starting transfers between devices, shards(): shifted.append(lax.ppermute(my_piece, ('row', 'col'), perm))  16.6 us
  transfers between devices with their start and end apart: 23, of which 6 were waited for; matrix products, arithmetic and copies ran while one was open for 5% of the time, Pallas kernels for 0%

profile of v13, /device:TPU:1, one launch (start us, length us, event | category | flops | bytes accessed | tf_op | source)
XLA Modules:
  0.0 441.8 jit_solution(8930906701796355453)
XLA Ops:
  9.4 3.2 copy.80
  12.7 3.9 fusion.8
  16.6 7.2 %all_to_all.8 = f32[128,1,8448]{2,1,0:T(1,128)} reshape(f32[256,4224]{1,0:T(8,128)} %fusion.8) | data formatting | bytes 8650752 | tf_op jit(solution)/shard_map/all_to_all | solution.py:39
  23.9 11.9 %all-to-all-start = ((f32[128,1,8448]{2,1,0:T(1,128)}), f32[128,1,8448]{2,1,0:T(1,128)}, u32[]{:S(2)}, u32[]{:S(2)}) async-start(f32[128,1,8448]{2,1,0:T(1,128)} %all_to_all.8), calls=%async_computation | async-start | bytes 8650752 | tf_op jit(solution)/shard_map/all_to_all | solution.py:39
  39.1 50.5 %all-to-all-done = f32[128,1,8448]{2,1,0:T(1,128)} async-done(((f32[128,1,8448]{2,1,0:T(1,128)}), f32[128,1,8448]{2,1,0:T(1,128)}, u32[]{:S(2)}, u32[]{:S(2)}) %all-to-all-start) | async-done | bytes 4325408 | tf_op jit(solution)/shard_map/all_to_all | solution.py:39
  89.7 14.0 %reduce.24 = f32[128,8448]{1,0:T(8,128)} reduce(f32[128,1,8448]{2,1,0:T(1,128)} %all-to-all-done, f32[]{:T(128)} %constant.258), dimensions={1}, to_apply=%all_to_all.7.reduce_sub_computation | reduce | bytes 8650756 | tf_op jit(solution)/shard_map/all_to_all | solution.py:39
  103.7 5.0 %reshape.146 = f32[256,4224]{1,0:T(8,128)} reshape(f32[128,8448]{1,0:T(8,128)} %reduce.24) | data formatting | bytes 8650752 | tf_op jit(solution)/shard_map/reshape | solution.py:45
  109.7 3.9 fusion.12
  117.9 2.6 add.141
  127.2 11.7 %cholesky.104 = f32[128,128]{1,0:T(8,128)S(1)} custom-call(f32[128,128]{1,0:T(8,128)S(1)} %cholesky.266), custom_call_target="Cholesky" | custom-call | tf_op jit(solution)/shard_map/jit(cholesky)/cholesky | solution.py:73
  138.9 9.8 %custom-call.30 = f32[1,128,128]{1,2,0:T(8,128)S(1)} custom-call(f32[1,128,128]{2,1,0:T(8,128)S(1)} %get-tuple-element.38), custom_call_target="InvertDiagBlocksLowerTriangular" | custom-call | tf_op jit(solution)/shard_map/jit(cholesky)/cholesky | solution.py:73
  151.4 11.7 %cholesky.217 = f32[128,128]{1,0:T(8,128)S(1)} custom-call(f32[128,128]{1,0:T(8,128)S(1)} %cholesky.270), custom_call_target="Cholesky" | custom-call | tf_op jit(solution)/shard_map/jit(cholesky)/cholesky | solution.py:73
  163.1 10.0 %custom-call.31 = f32[1,128,128]{1,2,0:T(8,128)S(1)} custom-call(f32[1,128,128]{2,1,0:T(8,128)S(1)} %get-tuple-element.35), custom_call_target="InvertDiagBlocksLowerTriangular" | custom-call | tf_op jit(solution)/shard_map/jit(cholesky)/cholesky | solution.py:73
  174.7 11.7 %cholesky.238 = f32[128,128]{1,0:T(8,128)S(1)} custom-call(f32[128,128]{1,0:T(8,128)S(1)} %cholesky.275), custom_call_target="Cholesky" | custom-call | tf_op jit(solution)/shard_map/jit(cholesky)/cholesky | solution.py:73
  187.2 9.8 %custom-call.32 = f32[1,128,128]{1,2,0:T(8,128)S(1)} custom-call(f32[1,128,128]{2,1,0:T(8,128)S(1)} %get-tuple-element.32), custom_call_target="InvertDiagBlocksLowerTriangular" | custom-call | tf_op jit(solution)/shard_map/jit(cholesky)/cholesky | solution.py:73
  198.4 12.2 %cholesky.255 = f32[128,128]{1,0:T(8,128)S(1)} custom-call(f32[128,128]{1,0:T(8,128)S(1)} %convolution_subtract_fusion.4), custom_call_target="Cholesky" | custom-call | tf_op jit(solution)/shard_map/jit(cholesky)/cholesky | solution.py:73
  228.0 10.6 %while.1 = (s32[]{:T(128)}, f32[512,512]{1,0:T(8,128)S(1)}, s32[4,2]{0,1:T(2,128)S(1)}, f32[4,128,128]{2,1,0:T(8,128)}, s32[]{:T(128)}) while((s32[]{:T(128)}, f32[512,512]{1,0:T(8,128)S(1)}, s32[4,2]{0,1:T(2,128)S(1)}, f32[4,128,128]{2,1,0:T(8,128)}, s32[]{:T(128)}) %tuple.38), condition=%wide.while_cond, body=%wide.while_body.sunk | while | flops 2 | bytes 132205 | solution.py:111
  228.7 2.0 bitcast_dynamic-update-slice_fusion.18
  233.9 2.0 bitcast_dynamic-update-slice_fusion.18
  239.6 40.1 %custom-call.33 = f32[4,128,128]{1,2,0:T(8,128)S(1)} custom-call(f32[4,128,128]{2,1,0:T(8,128)} %get-tuple-element.9), custom_call_target="InvertDiagBlocksLowerTriangular" | custom-call | tf_op jit(solution)/shard_map/triangular_solve | solution.py:111
  287.4 2.9 fusion.21
  291.7 2.2 fusion.52
  303.2 23.3 %collective-permute-done.12 = f32[128,512]{1,0:T(8,128)S(1)} collective-permute-done((f32[128,512]{1,0:T(8,128)S(1)}, f32[128,512]{1,0:T(8,128)S(1)}, u32[]{:S(2)}, u32[]{:S(2)}) %collective-permute-start.12) | collective-permute-done | bytes 262176 | tf_op jit(solution)/shard_map/ppermute | solution.py:120
  332.1 6.6 %collective-permute-start.20 = (f32[128,512]{1,0:T(8,128)S(1)}, f32[128,512]{1,0:T(8,128)S(1)}, u32[]{:S(2)}, u32[]{:S(2)}) collective-permute-start(f32[128,512]{1,0:T(8,128)S(1)} %get-tuple-element.19), channel_id=1, source_target_pairs={{0,0},{1,8},{2,16},{3,24},{4,32},{5,40},{6,48},{7,56},{8,64},{9,72... | collective-permute-start | bytes 786440 | tf_op jit(solution)/shard_map/ppermute | solution.py:129
  338.7 20.5 %collective-permute-done.20 = f32[128,512]{1,0:T(8,128)S(1)} collective-permute-done((f32[128,512]{1,0:T(8,128)S(1)}, f32[128,512]{1,0:T(8,128)S(1)}, u32[]{:S(2)}, u32[]{:S(2)}) %collective-permute-start.20) | collective-permute-done | bytes 262176 | tf_op jit(solution)/shard_map/ppermute | solution.py:129
  360.0 5.7 %fusion.5 = f32[64,8,32,128]{3,1,2,0:T(8,128)S(1)} fusion(f32[256,4224]{1,0:T(8,128)} %reshape.146, s32[256]{0:T(256)S(1)} %select_reduce_fusion), kind=kOutput, calls=%fused_computation.9 | convolution fusion | flops 6442582016 | bytes 12583936 | tf_op jit(solution)/shard_map/dot_general | solution.py:101
  371.0 10.9 %copy.53 = f32[32,32,16,128]{3,2,1,0:T(8,128)} copy(f32[32,32,16,128]{3,1,2,0:T(8,128)S(1)} %bitcast_bitcast_fusion) | data formatting | bytes 16777216 | tf_op jit(solution)/shard_map/transpose | solution.py:108
  384.8 7.5 %collective-permute-start.17 = (f32[128,512]{1,0:T(8,128)S(1)}, f32[128,512]{1,0:T(8,128)S(1)}, u32[]{:S(2)}, u32[]{:S(2)}) collective-permute-start(f32[128,512]{1,0:T(8,128)S(1)} %get-tuple-element.19), channel_id=1, source_target_pairs={{0,3},{1,4},{2,5},{3,6},{4,7},{5,0},{6,1},{7,2},{8,11},{9,12},{10,... | collective-permute-start | bytes 786440 | tf_op jit(solution)/shard_map/ppermute | solution.py:138
  393.7 2.9 collective-permute-start.16
  396.7 13.8 %collective-permute-done.15 = f32[128,512]{1,0:T(8,128)S(1)} collective-permute-done((f32[128,512]{1,0:T(8,128)S(1)}, f32[128,512]{1,0:T(8,128)S(1)}, u32[]{:S(2)}, u32[]{:S(2)}) %collective-permute-start.15) | collective-permute-done | bytes 262176 | tf_op jit(solution)/shard_map/ppermute | solution.py:138
  410.5 4.5 %collective-permute-done.16 = f32[128,512]{1,0:T(8,128)S(1)} collective-permute-done((f32[128,512]{1,0:T(8,128)S(1)}, f32[128,512]{1,0:T(8,128)S(1)}, u32[]{:S(2)}, u32[]{:S(2)}) %collective-permute-start.16) | collective-permute-done | bytes 262176 | tf_op jit(solution)/shard_map/ppermute | solution.py:138
  417.4 17.3 %fusion = f32[1024,2048]{1,0:T(8,128)} fusion(f32[1024,2048]{1,0:T(8,128)} %param.4, f32[128,8,16,128]{3,2,1,0:T(8,128)} %bitcast.111, pred[2048]{0:T(1024)(128)(4,1)S(1)} %add_compare_fusion, pred[1024]{0:T(1024)(128)(4,1)S(1)} %add_compare_fusion.1, f32[1024,512]{1,0:T(8,128)S(1)} %bitcast.113, f32[2048,512]{1,0:T(8,128)} %all-gather.2.cloned.1.call-done), kind=kOutput, calls=%fused_computation.3 | convolution fusion | flops 6450839552 | bytes 31460352 | tf_op jit(solution)/shard_map/dot_general | solution.py:142
  (162 shorter events, 82.7 us)
Async XLA Ops:
  23.9 65.8 %all-to-all-start = ((f32[128,1,8448]{2,1,0:T(1,128)}), f32[128,1,8448]{2,1,0:T(1,128)}, u32[]{:S(2)}, u32[]{:S(2)}) async-start(f32[128,1,8448]{2,1,0:T(1,128)} %all_to_all.8), calls=%async_computation | async-start | bytes 8650752 | tf_op jit(solution)/shard_map/all_to_all | solution.py:39
  35.7 1.6 slice-start
  35.8 381.6 %all-gather.2.cloned.1.call-start = ((), (), s32[]{:S(2)}) async-start(), calls=%async_computation.1 | async-start | bytes 4456448 | tf_op jit(solution)/shard_map/all_gather | solution.py:130
  214.6 1.0 copy-start.1
  216.5 3.8 collective-permute-start.2
  217.2 3.1 collective-permute-start.1
  218.8 2.4 collective-permute-start
  221.4 3.8 collective-permute-start.5
  222.1 3.1 collective-permute-start.4
  223.7 1.5 collective-permute-start.3
  290.3 5.1 %copy-start.2 = (f32[512,512]{1,0:T(8,128)S(1)}, f32[512,512]{1,0:T(8,128)}, u32[]{:S(2)}) copy-start(f32[512,512]{1,0:T(8,128)} %copy-done.1) | copy-start | bytes 3145732
  291.6 3.7 copy-start.6
  291.7 3.8 copy-start.4
  291.7 3.8 copy-start.5
  297.1 29.4 %collective-permute-start.12 = (f32[128,512]{1,0:T(8,128)S(1)}, f32[128,512]{1,0:T(8,128)S(1)}, u32[]{:S(2)}, u32[]{:S(2)}) collective-permute-start(f32[128,512]{1,0:T(8,128)S(1)} %get-tuple-element.22), channel_id=1, source_target_pairs={{0,1},{8,9},{16,17},{24,25},{32,33},{40,41},{48,49},{56,57},{64,65... | collective-permute-start | bytes 786440 | tf_op jit(solution)/shard_map/ppermute | solution.py:120
  298.4 29.5 %collective-permute-start.11 = (f32[128,512]{1,0:T(8,128)S(1)}, f32[128,512]{1,0:T(8,128)S(1)}, u32[]{:S(2)}, u32[]{:S(2)}) collective-permute-start(f32[128,512]{1,0:T(8,128)S(1)} %get-tuple-element.23), channel_id=1, source_target_pairs={{0,2},{8,10},{16,18},{24,26},{32,34},{40,42},{48,50},{56,58},{64,6... | collective-permute-start | bytes 786440 | tf_op jit(solution)/shard_map/ppermute | solution.py:120
  299.1 31.0 %collective-permute-start.10 = (f32[128,512]{1,0:T(8,128)S(1)}, f32[128,512]{1,0:T(8,128)}, u32[]{:S(2)}, u32[]{:S(2)}) collective-permute-start(f32[128,512]{1,0:T(8,128)S(1)} %get-tuple-element.24), channel_id=1, source_target_pairs={{0,3},{8,11},{16,19},{24,27},{32,35},{40,43},{48,51},{56,59},{64,6... | collective-permute-start | bytes 786440 | tf_op jit(solution)/shard_map/ppermute | solution.py:120
  300.4 29.7 %collective-permute-start.9 = (f32[128,512]{1,0:T(8,128)S(1)}, f32[128,512]{1,0:T(8,128)}, u32[]{:S(2)}, u32[]{:S(2)}) collective-permute-start(f32[128,512]{1,0:T(8,128)S(1)} %get-tuple-element.25), channel_id=1, source_target_pairs={{0,4},{8,12},{16,20},{24,28},{32,36},{40,44},{48,52},{56,60},{64,6... | collective-permute-start | bytes 786440 | tf_op jit(solution)/shard_map/ppermute | solution.py:120
  301.8 28.3 %collective-permute-start.8 = (f32[128,512]{1,0:T(8,128)S(1)}, f32[128,512]{1,0:T(8,128)}, u32[]{:S(2)}, u32[]{:S(2)}) collective-permute-start(f32[128,512]{1,0:T(8,128)S(1)} %get-tuple-element.26), channel_id=1, source_target_pairs={{0,5},{8,13},{16,21},{24,29},{32,37},{40,45},{48,53},{56,61},{64,6... | collective-permute-start | bytes 786440 | tf_op jit(solution)/shard_map/ppermute | solution.py:120
  326.5 1.4 copy-start.11
  326.5 3.6 collective-permute-start.7
  328.5 1.6 collective-permute-start.6
  332.1 27.1 %collective-permute-start.20 = (f32[128,512]{1,0:T(8,128)S(1)}, f32[128,512]{1,0:T(8,128)S(1)}, u32[]{:S(2)}, u32[]{:S(2)}) collective-permute-start(f32[128,512]{1,0:T(8,128)S(1)} %get-tuple-element.19), channel_id=1, source_target_pairs={{0,0},{1,8},{2,16},{3,24},{4,32},{5,40},{6,48},{7,56},{8,64},{9,72... | collective-permute-start | bytes 786440 | tf_op jit(solution)/shard_map/ppermute | solution.py:129
  367.5 26.2 %collective-permute-start.14 = (f32[128,512]{1,0:T(8,128)S(1)}, f32[128,512]{1,0:T(8,128)S(1)}, u32[]{:S(2)}, u32[]{:S(2)}) collective-permute-start(f32[128,512]{1,0:T(8,128)S(1)} %get-tuple-element.19), channel_id=1, source_target_pairs={{0,6},{1,7},{2,0},{3,1},{4,2},{5,3},{6,4},{7,5},{8,14},{9,15},{10,... | collective-permute-start | bytes 786440 | tf_op jit(solution)/shard_map/ppermute | solution.py:138
  369.4 22.9 %collective-permute-start.13 = (f32[128,512]{1,0:T(8,128)S(1)}, f32[128,512]{1,0:T(8,128)S(1)}, u32[]{:S(2)}, u32[]{:S(2)}) collective-permute-start(f32[128,512]{1,0:T(8,128)S(1)} %get-tuple-element.19), channel_id=1, source_target_pairs={{0,7},{1,0},{2,1},{3,2},{4,3},{5,4},{6,5},{7,6},{8,15},{9,8},{10,9... | collective-permute-start | bytes 786440 | tf_op jit(solution)/shard_map/ppermute | solution.py:138
  371.0 22.7 %copy-start.9 = (f32[16,128,512]{2,1,0:T(8,128)S(1)}, f32[16,128,512]{2,1,0:T(8,128)}, u32[]{:S(2)}) copy-start(f32[16,128,512]{2,1,0:T(8,128)} %get-tuple-element.18) | copy-start | bytes 12582916
  381.9 35.0 %collective-permute-start.19 = (f32[128,512]{1,0:T(8,128)S(1)}, f32[128,512]{1,0:T(8,128)S(1)}, u32[]{:S(2)}, u32[]{:S(2)}) collective-permute-start(f32[128,512]{1,0:T(8,128)S(1)} %get-tuple-element.19), channel_id=1, source_target_pairs={{0,1},{1,2},{2,3},{3,4},{4,5},{5,6},{6,7},{7,0},{8,9},{9,10},{10,1... | collective-permute-start | bytes 786440 | tf_op jit(solution)/shard_map/ppermute | solution.py:138
  383.6 33.2 %collective-permute-start.18 = (f32[128,512]{1,0:T(8,128)S(1)}, f32[128,512]{1,0:T(8,128)S(1)}, u32[]{:S(2)}, u32[]{:S(2)}) collective-permute-start(f32[128,512]{1,0:T(8,128)S(1)} %get-tuple-element.19), channel_id=1, source_target_pairs={{0,2},{1,3},{2,4},{3,5},{4,6},{5,7},{6,0},{7,1},{8,10},{9,11},{10,... | collective-permute-start | bytes 786440 | tf_op jit(solution)/shard_map/ppermute | solution.py:138
  384.8 32.0 %collective-permute-start.17 = (f32[128,512]{1,0:T(8,128)S(1)}, f32[128,512]{1,0:T(8,128)S(1)}, u32[]{:S(2)}, u32[]{:S(2)}) collective-permute-start(f32[128,512]{1,0:T(8,128)S(1)} %get-tuple-element.19), channel_id=1, source_target_pairs={{0,3},{1,4},{2,5},{3,6},{4,7},{5,0},{6,1},{7,2},{8,11},{9,12},{10,... | collective-permute-start | bytes 786440 | tf_op jit(solution)/shard_map/ppermute | solution.py:138
  392.3 18.2 %collective-permute-start.15 = (f32[128,512]{1,0:T(8,128)S(1)}, f32[128,512]{1,0:T(8,128)S(1)}, u32[]{:S(2)}, u32[]{:S(2)}) collective-permute-start(f32[128,512]{1,0:T(8,128)S(1)} %get-tuple-element.19), channel_id=1, source_target_pairs={{0,5},{1,6},{2,7},{3,0},{4,1},{5,2},{6,3},{7,4},{8,13},{9,14},{10,... | collective-permute-start | bytes 786440 | tf_op jit(solution)/shard_map/ppermute | solution.py:138
  393.7 21.3 %collective-permute-start.16 = (f32[128,512]{1,0:T(8,128)S(1)}, f32[128,512]{1,0:T(8,128)S(1)}, u32[]{:S(2)}, u32[]{:S(2)}) collective-permute-start(f32[128,512]{1,0:T(8,128)S(1)} %get-tuple-element.19), channel_id=1, source_target_pairs={{0,4},{1,5},{2,6},{3,7},{4,0},{5,1},{6,2},{7,3},{8,12},{9,13},{10,... | collective-permute-start | bytes 786440 | tf_op jit(solution)/shard_map/ppermute | solution.py:138
  417.3 17.4 %copy-start = (f32[8,128,512]{2,1,0:T(8,128)}, f32[8,128,512]{2,1,0:T(8,128)S(1)}, u32[]{:S(2)}) copy-start(f32[8,128,512]{2,1,0:T(8,128)S(1)} %constant_dynamic-slice_fusion.1) | copy-start | bytes 6291460
  (6 other events, 5.0 us)
Sparse Core Ops, SparseCore 0:
  360.1 55.1 all-gather.1
